TPU v7x, 32 devices: a whole 2x2x4 slice. The times are simulated.
32 devices in a mesh: lat: 4 (over z), lon: 4 (over y, x), ens: 2 (over core).
Axes of the slice: x: 2, y: 2, z: 4, core: 2. Of those that a mesh axis runs over, the one named last changes fastest.
Arguments:
- field: bfloat16 [2048, 1920, 128], P(('ens', 'lat', 'lon')), parts along dimension 0, may hold values from -6 to 6
- w_first: bfloat16 [2, 128, 128], replicated, may hold values from -0.375 to 0.375
- b_first: float32 [2, 128], replicated, may hold values from -1.8 to 1.8
- w_second: bfloat16 [2, 128, 128], replicated, may hold values from -0.375 to 0.375
- b_second: float32 [2, 128], replicated, may hold values from -1.8 to 1.8
- conv_kernel: float32 [3, 3, 128], replicated, may hold values from -2 to 2
- mode_plan: int32 [16, 4], replicated, may hold values from -1 to 127, as said below
Outputs:
- block_output: bfloat16 [2048, 1920, 128], P(('ens', 'lat', 'lon')), parts along dimension 0
There are 2 independent parts, one for each index of `ens`. A program takes and returns all parts, laid end to end along the dimension named above; an argument that names none is the same for every part. Nothing has to cross between parts.
Inputs may be any that keep to these rules, and one draw needn't show every extreme that they name: `mode_plan`: entry [o, s] is, for a listing device o = i * 4 + r, the local index of one tile of device i * 4 + s, or -1 for none; the indices that name one device's tiles are distinct; tiles that no entry names are dropped.
All inputs are finite; a program needn't handle non-finite values.
Results may differ from a plain program's by a relative error of at most 0.002.
Values may be sent and summed in bfloat16 or wider, within the bound.
No kernel may reach another device: no remote copies, remote signals or barrier semaphores. Data moves between devices by JAX's collectives and lax.ppermute only.
A program may use at most 960 MiB of HBM per device.

v0:
```python
import math

import jax
import jax.numpy as jnp
from jax import lax
from jax.sharding import PartitionSpec as P

H = 1024
W = 1920
KH = 512
KW = 512
MB = 128


shrink_level = 0.01


def padded(block, sides, width):
    for axis, dim in sides:
        count = lax.axis_size(axis)
        forward = [(i, i + 1) for i in range(count - 1)]
        backward = [(target, source) for source, target in forward]
        low = lax.ppermute(
            lax.slice_in_dim(block, block.shape[dim] - width, None, axis=dim), axis, forward
        )
        high = lax.ppermute(lax.slice_in_dim(block, 0, width, axis=dim), axis, backward)
        block = jnp.concatenate([low, block, high], axis=dim)
    return block


def lon_forward_matrix():
    columns = jnp.arange(W, dtype=jnp.int32)[:, None]
    orders = jnp.arange(KW, dtype=jnp.int32)[None, :]
    phases = columns * orders % W
    angles = phases.astype(jnp.float32) * (2.0 * math.pi / W)
    factor = 1.0 / math.sqrt(W)
    return (jnp.concatenate([jnp.cos(angles), -jnp.sin(angles)], axis=1) * factor).astype(
        jnp.bfloat16
    )


def lat_angles():
    freqs = jnp.arange(KH, dtype=jnp.int32) - KH // 2
    rowids = jnp.arange(H, dtype=jnp.int32)
    phases = jnp.mod(freqs[:, None] * rowids[None, :], H)
    return phases.astype(jnp.float32) * (2.0 * math.pi / H)


def lat_forward_matrix():
    angles = lat_angles()
    factor = 1.0 / math.sqrt(H)
    cosine = jnp.cos(angles) * factor
    sine = jnp.sin(angles) * factor
    upper = jnp.stack([cosine, sine], axis=1)
    lower = jnp.stack([-sine, cosine], axis=1)
    return jnp.concatenate([upper, lower], axis=0).astype(jnp.bfloat16)


def lat_inverse_matrix():
    angles = lat_angles()
    factor = 1.0 / math.sqrt(H)
    cosine = jnp.transpose(jnp.cos(angles)) * factor
    sine = jnp.transpose(jnp.sin(angles)) * factor
    real_rows = jnp.stack([cosine, -sine], axis=1)
    imag_rows = jnp.stack([sine, cosine], axis=1)
    return jnp.stack([real_rows, imag_rows], axis=0).astype(jnp.bfloat16)


def lon_inverse_matrix():
    orders = jnp.arange(KW, dtype=jnp.int32)[:, None]
    columns = jnp.arange(W, dtype=jnp.int32)[None, :]
    phases = orders * columns % W
    angles = phases.astype(jnp.float32) * (2.0 * math.pi / W)
    weights = jnp.where(orders == 0, 1.0, 2.0).astype(jnp.float32) / math.sqrt(W)
    return jnp.stack([weights * jnp.cos(angles), -weights * jnp.sin(angles)], axis=0).astype(
        jnp.bfloat16
    )


def complexify(weights):
    real_part = weights[0]
    imag_part = weights[1]
    top_rows = jnp.concatenate([real_part, imag_part], axis=1)
    low_rows = jnp.concatenate([-imag_part, real_part], axis=1)
    return jnp.concatenate([top_rows, low_rows], axis=0)


def spectral_mlp(modes, first_mat, first_bias, second_mat, second_bias):
    hidden = jnp.einsum("tmc,cd->tmd", modes, first_mat, preferred_element_type=jnp.float32)
    hidden = jax.nn.relu(hidden + first_bias.reshape(-1)).astype(jnp.bfloat16)
    second_out = jnp.einsum("tmc,cd->tmd", hidden, second_mat, preferred_element_type=jnp.float32)
    second_out = second_out + second_bias.reshape(-1)
    return second_out - jnp.clip(second_out, -shrink_level, shrink_level)


def on_device(field, w_first, b_first, w_second, b_second, conv_kernel, mode_plan):
    row_count, width, channels = field.shape
    lat_count = lax.axis_size("lat")
    lon_count = lax.axis_size("lon")
    per_device = KW // (lat_count * lon_count)
    tile_count = KH // MB * per_device
    extended = padded(field, ((("lat", "lon"), 0),), 1)
    values = field.astype(jnp.float32)
    average = jnp.mean(values, axis=-1, keepdims=True)
    centred = values - average
    spread = jnp.mean(centred * centred, axis=-1, keepdims=True)
    normed = (centred * lax.rsqrt(spread + 1e-05)).astype(jnp.bfloat16)
    forward = jnp.einsum(
        "hwc,wk->khc", normed, lon_forward_matrix(), preferred_element_type=jnp.float32
    )
    forward = forward.astype(jnp.bfloat16).reshape(2, KW, row_count, channels)
    pencil = lax.all_to_all(forward, ("lat", "lon"), split_axis=1, concat_axis=2, tiled=True)
    spectrum = jnp.einsum(
        "pah,ajhc->jpc", lat_forward_matrix(), pencil, preferred_element_type=jnp.float32
    )
    spectrum = spectrum.astype(jnp.bfloat16).reshape(per_device, 2, KH // MB, MB, channels)
    tiles = jnp.transpose(spectrum, (0, 2, 3, 1, 4)).reshape(tile_count, MB, 2 * channels)
    first_mat = complexify(w_first)
    second_mat = complexify(w_second)
    lat_index = lax.axis_index("lat")
    lon_index = lax.axis_index("lon")
    owner_rows = lax.dynamic_slice_in_dim(mode_plan, lat_index * lon_count, lon_count, 0)
    chosen = lax.dynamic_slice_in_dim(owner_rows, lon_index, 1, 1)[:, 0]
    matched = chosen[:, None] == jnp.arange(tile_count, dtype=jnp.int32)[None, :]
    retained = jnp.any(matched, axis=0)
    shrunk = spectral_mlp(tiles, first_mat, b_first, second_mat, b_second)
    filtered = jnp.where(retained[:, None, None], shrunk, 0.0).astype(jnp.bfloat16)
    zspec = filtered.reshape(per_device, KH // MB, MB, 2, channels)
    zspec = jnp.transpose(zspec, (0, 3, 1, 2, 4)).reshape(per_device, 2, KH, channels)
    inverse = jnp.einsum(
        "ahbq,jbqc->ajhc", lat_inverse_matrix(), zspec, preferred_element_type=jnp.float32
    )
    inverse = inverse.astype(jnp.bfloat16)
    rowwise = lax.all_to_all(inverse, ("lat", "lon"), split_axis=2, concat_axis=1, tiled=True)
    filtered_grid = jnp.einsum(
        "akhc,akw->hwc", rowwise, lon_inverse_matrix(), preferred_element_type=jnp.float32
    )
    filtered_grid = filtered_grid.astype(jnp.bfloat16)
    widened = extended.astype(jnp.float32)
    stencil = jnp.zeros((row_count, width, channels), jnp.float32)
    for row_off in range(3):
        for col_off in range(3):
            shifted = jnp.roll(widened[row_off : row_off + row_count], 1 - col_off, axis=1)
            stencil = stencil + conv_kernel[row_off, col_off] * shifted
    return (values + filtered_grid.astype(jnp.float32) + stencil).astype(jnp.bfloat16)


def solution(mesh):
    placed = (P(("ens", "lat", "lon"), None, None), P(), P(), P(), P(), P(), P())
    return jax.shard_map(
        on_device,
        mesh=mesh,
        in_specs=placed,
        out_specs=P(("ens", "lat", "lon"), None, None),
        check_vma=False,
    )
```

profile of v0, /device:TPU:16, one launch (start us, length us, event | category | flops | bytes accessed | tf_op | source)
XLA Modules:
  0.0 1583.4 jit_solution(12525163808302461563)
XLA Ops:
  0.0 17.1 %sine_negate_fusion = (f32[1920,512]{0,1:T(8,128)}, f32[1920,512]{0,1:T(8,128)}) fusion(), kind=kLoop, calls=%fused_computation.64 | loop fusion | flops 9830400 | bytes 7864320 | tf_op jit(solution)/shard_map/neg | solution.py:37
  17.1 11.3 convert_reduce_fusion
  28.5 0.0 copy-start.2
  28.5 0.0 copy-start.3
  28.5 38.8 %fusion.2 = f32[64,1920]{1,0:T(8,128)S(1)} fusion(bf16[64,1920,128]{2,1,0:T(8,128)(2,1)} %param.7, f32[64,1920]{1,0:T(8,128)S(1)} %broadcast_multiply_fusion), kind=kLoop, calls=%fused_computation.5 | loop fusion | flops 62791680 | bytes 32440320 | tf_op jit(solution)/shard_map/reduce_sum | solution.py:106
  67.3 0.1 add_rsqrt_fusion
  67.4 0.8 fusion.107
  68.2 53.3 %fusion.21 = bf16[1024,64,128]{2,0,1:T(8,128)(2,1)} fusion(bf16[64,1920,128]{2,1,0:T(8,128)(2,1)} %param.7, f32[64,1920]{1,0:T(8,128)S(1)} %add_rsqrt_fusion, f32[64,1920]{1,0:T(8,128)S(1)} %broadcast_multiply_fusion, bf16[1920,1024,1]{0,1,2:T(8,128)(2,1)S(1)} %fusion.107), kind=kOutput, calls=%fused_computation.38 | convolution fusion | flops 32283557888 | bytes 53149696 | tf_op jit(solution)/shard_map/hwc,wk->khc/dot_general | solution.py:108
  121.5 18.7 %copy.34 = bf16[2,512,64,128]{3,2,0,1:T(8,128)(2,1)} copy(bf16[2,512,64,128]{3,1,0,2:T(8,128)(2,1)} %bitcast.114) | data formatting | bytes 33554432 | tf_op jit(solution)/shard_map/reshape | solution.py:111
  140.1 7.4 all-to-all-start
  147.5 0.0 copy-start.7
  147.6 0.0 copy-start.8
  147.6 0.1 dynamic-slice_bitcast_fusion
  147.7 0.1 fusion.83
  147.8 8.8 negate_convert_fusion
  156.6 2.4 maximum_bitcast_fusion.6
  159.0 0.6 fusion.93
  159.6 0.7 slice_bitcast_fusion
  160.3 10.8 fusion.63
  171.0 337.8 %all-to-all-done = bf16[2,512,64,128]{3,2,0,1:T(8,128)(2,1)} async-done(((bf16[2,512,64,128]{3,2,0,1:T(8,128)(2,1)}), bf16[2,512,64,128]{3,2,0,1:T(8,128)(2,1)}, u32[]{:S(2)}, u32[]{:S(2)}) %all-to-all-start) | async-done | bytes 16777248 | tf_op jit(solution)/shard_map/all_to_all | solution.py:112
  508.8 8.4 copy.36
  517.2 22.3 %fusion.26 = bf16[32,1024,128]{1,2,0:T(8,128)(2,1)} fusion(bf16[2,32,1024,128]{3,2,1,0:T(8,128)(2,1)S(1)} %bitcast.113, bf16[512,1,1024]{2,0,1:T(8,128)(2,1)} %get-tuple-element.39, bf16[512,1,1024]{2,0,1:T(8,128)(2,1)} %get-tuple-element.38, bf16[512,1,1024]{2,0,1:T(8,128)(2,1)S(1)} %get-tuple-element.37), kind=kOutput, calls=%fused_computation.44 | convolution fusion | flops 17200840704 | bytes 28311552 | tf_op jit(solution)/shard_map/pah,ajhc->jpc/dot_general | solution.py:113
  539.6 14.3 reshape.393
  553.9 0.0 copy-start.31
  553.9 0.0 copy-start.32
  553.9 9.4 copy.38
  563.3 0.0 copy-done.10
  563.4 9.8 fusion.19
  573.2 12.9 reshape.395
  586.1 25.1 %fusion.20 = bf16[2,32,1024,128]{2,3,0,1:T(8,128)(2,1)} fusion(bf16[32,2,512,128,1]{3,1,2,0,4:T(2,128)(2,1)} %bitcast.116, bf16[1,1024,2,512]{3,1,2,0:T(8,128)(2,1)} %get-tuple-element.20, bf16[1,1024,2,512]{3,1,2,0:T(8,128)(2,1)S(1)} %copy-done.4), kind=kOutput, calls=%fused_computation.35 | convolution fusion | flops 17196646400 | bytes 29360128 | tf_op jit(solution)/shard_map/ahbq,jbqc->ajhc/dot_general | solution.py:130
  611.2 41.4 %copy.41 = bf16[2,32,1024,128]{3,0,1,2:T(2,128)(2,1)} copy(bf16[2,32,1024,128]{2,3,0,1:T(8,128)(2,1)} %fusion.20) | data formatting | bytes 33554432 | tf_op jit(solution)/shard_map/convert_element_type | solution.py:133
  652.5 27.1 %all-to-all-start.1 = ((bf16[2,32,1024,128]{3,0,1,2:T(2,128)(2,1)}), bf16[2,32,1024,128]{3,0,1,2:T(2,128)(2,1)}, u32[]{:S(2)}, u32[]{:S(2)}) async-start(bf16[2,32,1024,128]{3,0,1,2:T(2,128)(2,1)} %copy.41), calls=%async_computation.1 | async-start | bytes 33554432 | tf_op jit(solution)/shard_map/all_to_all | solution.py:134
  679.7 1.2 fusion.96
  680.9 3.4 collective-permute-start
  684.3 4.3 collective-permute-start.1
  688.6 0.6 slice_bitcast_fusion.12
  689.2 18.0 %multiply_convert_fusion = (bf16[1,512,1920]{1,2,0:T(8,128)(2,1)}, bf16[1,512,1920]{1,2,0:T(8,128)(2,1)}) fusion(f32[512]{0:T(512)S(1)} %fusion.84, f32[512]{0:T(512)S(1)} %select_multiply_fusion), kind=kLoop, calls=%fused_computation.69 | loop fusion | flops 12779520 | bytes 3936256 | tf_op jit(solution)/shard_map/convert.16
  707.3 353.5 %collective-permute-done = bf16[1,1920,128]{2,1,0:T(8,128)(2,1)S(1)} collective-permute-done((bf16[1,1920,128]{2,1,0:T(8,128)(2,1)S(1)}, bf16[1,1920,128]{2,1,0:T(8,128)(2,1)S(1)}, u32[]{:S(2)}, u32[]{:S(2)}) %collective-permute-start) | collective-permute-done | bytes 491552 | tf_op jit(solution)/shard_map/ppermute | solution.py:23
  1060.8 0.0 collective-permute-done.1
  1060.8 2.0 maximum_convert_fusion.2
  1062.8 30.7 %maximum_convert_fusion = f32[66,1920,128]{2,1,0:T(8,128)} fusion(bf16[1,1920,128]{2,1,0:T(8,128)(2,1)S(1)} %collective-permute-done.1, bf16[64,1920,128]{2,1,0:T(8,128)(2,1)} %param.7, bf16[1,1920,128]{2,1,0:T(8,128)(2,1)S(1)} %collective-permute-done), kind=kLoop, calls=%fused_computation.28 | loop fusion | flops 48660480 | bytes 97320960 | tf_op jit(solution)/shard_map/convert_element_type | solution.py:139
  1093.5 242.4 %fusion.95 = (f32[64,1919,128]{2,1,0:T(8,128)}, f32[64,1919,128]{2,1,0:T(8,128)}, f32[64,1919,128]{2,1,0:T(8,128)}, f32[64,1919,128]{2,1,0:T(8,128)}, f32[64,1919,128]{2,1,0:T(8,128)}, /*index=5*/f32[64,1919,128]{2,1,0:T(8,128)}) fusion(f32[66,1920,128]{2,1,0:T(8,128)} %maximum_convert_fusion), kind=kLoop, calls=%fused_computation.155 | loop fusion | bytes 754581504 | tf_op jit(solution)/shard_map/jit(_roll_static)/slice | solution.py:143
  1335.9 0.0 all-to-all-done.1
  1335.9 9.8 copy.42
  1345.8 0.0 copy-start.5
  1345.9 36.0 %copy.43 = bf16[2,16,32,64,128]{4,2,1,0,3:T(8,128)(2,1)} copy(bf16[2,16,32,64,128]{4,3,1,2,0:T(8,128)(2,1)S(1)} %bitcast.111) | data formatting | bytes 33554432 | tf_op jit(solution)/shard_map/all_to_all | solution.py:134
  1382.1 0.0 copy-start.1
  1382.1 200.8 %fusion.5 = bf16[64,1920,128]{2,1,0:T(8,128)(2,1)} fusion(bf16[64,1920,128]{2,1,0:T(8,128)(2,1)} %param.7, f32[66,1920,128]{2,1,0:T(8,128)} %maximum_convert_fusion, f32[64,1919,128]{2,1,0:T(8,128)} %get-tuple-element.9, f32[64,1,128]{2,1,0:T(1,128)S(1)} %copy-done.20, f32[64,1,128]{2,1,0:T(1,128)S(1)} %copy-done.19, f32[64,1919,128]{2,1,0:T(8,128)} %get-tuple-element.7, ...), kind=kOutput, calls=%fused_computation.8 | convolution fusion | flops 32676249600 | bytes 649859584 | tf_op jit(solution)/shard_map/akhc,akw->hwc/dot_general | solution.py:135
  (61 shorter events, 0.2 us)
Async XLA Ops:
  0.0 147.6 %copy-start = (s32[16,4]{0,1:T(4,128)S(1)}, s32[16,4]{0,1:T(4,128)}, u32[]{:S(2)}) copy-start(s32[16,4]{0,1:T(4,128)} %param.13) | copy-start | bytes 772
  28.5 38.9 %copy-start.2 = (f32[1920,512]{0,1:T(8,128)S(1)}, f32[1920,512]{0,1:T(8,128)}, u32[]{:S(2)}) copy-start(f32[1920,512]{0,1:T(8,128)} %get-tuple-element.40) | copy-start | bytes 11796484
  28.5 38.9 %copy-start.3 = (f32[1920,512]{0,1:T(8,128)S(1)}, f32[1920,512]{0,1:T(8,128)}, u32[]{:S(2)}) copy-start(f32[1920,512]{0,1:T(8,128)} %get-tuple-element.41) | copy-start | bytes 11796484
  140.1 368.7 %all-to-all-start = ((bf16[2,512,64,128]{3,2,0,1:T(8,128)(2,1)}), bf16[2,512,64,128]{3,2,0,1:T(8,128)(2,1)}, u32[]{:S(2)}, u32[]{:S(2)}) async-start(bf16[2,512,64,128]{3,2,0,1:T(8,128)(2,1)} %copy.34), calls=%async_computation | async-start | bytes 33554432 | tf_op jit(solution)/shard_map/all_to_all | solution.py:112
  147.5 11.4 copy-start.7
  147.6 11.4 copy-start.8
  553.9 9.5 copy-start.9
  553.9 9.5 copy-start.10
  553.9 9.5 copy-start.11
  553.9 9.5 copy-start.12
  553.9 9.5 copy-start.13
  553.9 9.5 copy-start.14
  553.9 9.5 copy-start.31
  553.9 9.5 copy-start.32
  573.2 12.9 copy-start.4
  652.5 36.1 %copy-start.21 = (f32[3,3,128]{2,1,0:T(4,128)S(1)}, f32[3,3,128]{2,1,0:T(4,128)}, u32[]{:S(2)}) copy-start(f32[3,3,128]{2,1,0:T(4,128)} %param.12) | copy-start | bytes 13828
  652.5 683.4 %all-to-all-start.1 = ((bf16[2,32,1024,128]{3,0,1,2:T(2,128)(2,1)}), bf16[2,32,1024,128]{3,0,1,2:T(2,128)(2,1)}, u32[]{:S(2)}, u32[]{:S(2)}) async-start(bf16[2,32,1024,128]{3,0,1,2:T(2,128)(2,1)} %copy.41), calls=%async_computation.1 | async-start | bytes 33554432 | tf_op jit(solution)/shard_map/all_to_all | solution.py:134
  680.9 379.9 %collective-permute-start = (bf16[1,1920,128]{2,1,0:T(8,128)(2,1)S(1)}, bf16[1,1920,128]{2,1,0:T(8,128)(2,1)S(1)}, u32[]{:S(2)}, u32[]{:S(2)}) collective-permute-start(bf16[1,1920,128]{2,1,0:T(8,128)(2,1)S(1)} %get-tuple-element.17), channel_id=1, source_target_pairs={{0,2},{2,4},{4,6},{6,8},{8,10},{10,12},{12,14},{14,16},{16,18},{18... | collective-permute-start | bytes 1474568 | tf_op jit(solution)/shard_map/ppermute | solution.py:23
  684.3 376.5 %collective-permute-start.1 = (bf16[1,1920,128]{2,1,0:T(8,128)(2,1)S(1)}, bf16[1,1920,128]{2,1,0:T(8,128)(2,1)S(1)}, u32[]{:S(2)}, u32[]{:S(2)}) collective-permute-start(bf16[1,1920,128]{2,1,0:T(8,128)(2,1)S(1)} %get-tuple-element.18), channel_id=1, source_target_pairs={{2,0},{4,2},{6,4},{8,6},{10,8},{12,10},{14,12},{16,14},{18,16},{20... | collective-permute-start | bytes 1474568 | tf_op jit(solution)/shard_map/ppermute | solution.py:26
  1345.8 36.2 %copy-start.5 = (bf16[1,512,1920]{1,2,0:T(8,128)(2,1)S(1)}, bf16[1,512,1920]{1,2,0:T(8,128)(2,1)}, u32[]{:S(2)}) copy-start(bf16[1,512,1920]{1,2,0:T(8,128)(2,1)} %get-tuple-element.46) | copy-start | bytes 5898244
  1345.8 36.2 %copy-start.6 = (bf16[1,512,1920]{1,2,0:T(8,128)(2,1)S(1)}, bf16[1,512,1920]{1,2,0:T(8,128)(2,1)}, u32[]{:S(2)}) copy-start(bf16[1,512,1920]{1,2,0:T(8,128)(2,1)} %get-tuple-element.47) | copy-start | bytes 5898244
  1345.8 36.2 %copy-start.15 = (f32[64,1,128]{2,1,0:T(1,128)S(1)}, f32[64,1,128]{2,1,0:T(1,128)}, u32[]{:S(2)}) copy-start(f32[64,1,128]{2,1,0:T(1,128)} %get-tuple-element.11) | copy-start | bytes 98308
  1345.8 36.2 %copy-start.16 = (f32[64,1,128]{2,1,0:T(1,128)S(1)}, f32[64,1,128]{2,1,0:T(1,128)}, u32[]{:S(2)}) copy-start(f32[64,1,128]{2,1,0:T(1,128)} %get-tuple-element.12) | copy-start | bytes 98308
  1345.8 36.2 %copy-start.17 = (f32[64,1,128]{2,1,0:T(1,128)S(1)}, f32[64,1,128]{2,1,0:T(1,128)}, u32[]{:S(2)}) copy-start(f32[64,1,128]{2,1,0:T(1,128)} %get-tuple-element.13) | copy-start | bytes 98308
  1345.8 36.2 %copy-start.18 = (f32[64,1,128]{2,1,0:T(1,128)S(1)}, f32[64,1,128]{2,1,0:T(1,128)}, u32[]{:S(2)}) copy-start(f32[64,1,128]{2,1,0:T(1,128)} %get-tuple-element.14) | copy-start | bytes 98308
  1345.8 36.2 %copy-start.19 = (f32[64,1,128]{2,1,0:T(1,128)S(1)}, f32[64,1,128]{2,1,0:T(1,128)}, u32[]{:S(2)}) copy-start(f32[64,1,128]{2,1,0:T(1,128)} %get-tuple-element.15) | copy-start | bytes 98308
  1345.8 36.2 %copy-start.20 = (f32[64,1,128]{2,1,0:T(1,128)S(1)}, f32[64,1,128]{2,1,0:T(1,128)}, u32[]{:S(2)}) copy-start(f32[64,1,128]{2,1,0:T(1,128)} %get-tuple-element.16) | copy-start | bytes 98308
  1345.8 36.2 %copy-start.22 = (f32[128]{0:T(128)S(1)}, f32[128]{0:T(128)}, u32[]{:S(2)}) copy-start(f32[128]{0:T(128)} %get-tuple-element.25) | copy-start | bytes 1540
  1345.9 36.2 %copy-start.23 = (f32[128]{0:T(128)S(1)}, f32[128]{0:T(128)}, u32[]{:S(2)}) copy-start(f32[128]{0:T(128)} %get-tuple-element.26) | copy-start | bytes 1540
  1345.9 36.2 %copy-start.24 = (f32[128]{0:T(128)S(1)}, f32[128]{0:T(128)}, u32[]{:S(2)}) copy-start(f32[128]{0:T(128)} %get-tuple-element.27) | copy-start | bytes 1540
  1345.9 36.2 %copy-start.25 = (f32[128]{0:T(128)S(1)}, f32[128]{0:T(128)}, u32[]{:S(2)}) copy-start(f32[128]{0:T(128)} %get-tuple-element.28) | copy-start | bytes 1540
  1345.9 36.2 %copy-start.26 = (f32[128]{0:T(128)S(1)}, f32[128]{0:T(128)}, u32[]{:S(2)}) copy-start(f32[128]{0:T(128)} %get-tuple-element.29) | copy-start | bytes 1540
  1345.9 36.2 %copy-start.27 = (f32[128]{0:T(128)S(1)}, f32[128]{0:T(128)}, u32[]{:S(2)}) copy-start(f32[128]{0:T(128)} %get-tuple-element.30) | copy-start | bytes 1540
  1345.9 36.2 %copy-start.28 = (f32[128]{0:T(128)S(1)}, f32[128]{0:T(128)}, u32[]{:S(2)}) copy-start(f32[128]{0:T(128)} %get-tuple-element.31) | copy-start | bytes 1540
  1345.9 36.2 %copy-start.29 = (f32[128]{0:T(128)S(1)}, f32[128]{0:T(128)}, u32[]{:S(2)}) copy-start(f32[128]{0:T(128)} %get-tuple-element.32) | copy-start | bytes 1540
  1345.9 36.2 %copy-start.30 = (f32[128]{0:T(128)S(1)}, f32[128]{0:T(128)}, u32[]{:S(2)}) copy-start(f32[128]{0:T(128)} %get-tuple-element.33) | copy-start | bytes 1540
  1382.1 200.8 %copy-start.1 = (s32[16,4]{0,1:T(4,128)S(1)}, s32[16,4]{0,1:T(4,128)}, u32[]{:S(2)}) copy-start(s32[16,4]{0,1:T(4,128)} %param.13) | copy-start | bytes 772
where the time goes:
time: 1590 us; the launch traced here: 1580 us
  waiting for transfers between devices  691 us (43%)
  local copies, waits for them, and re-layouts  396 us (25%)
  matrix products  311 us (20%)
  other arithmetic  142 us (9%)
  starting transfers between devices  42.2 us (3%)
    ppermute x1, waiting for transfers between devices, padded(): lax.ppermute(lax.slice_in_dim(block, block.shape[dim] - width, None, axis...  354 us
    all_to_all x1, waiting for transfers between devices, on_device(): lax.all_to_all(forward, ('lat', 'lon'), split_axis=1, concat_axis=2, tile...  338 us
    slice x1, local copies, waits for them, and re-layouts, on_device(): jnp.roll(widened[row_off:row_off + row_count], 1 - col_off, axis=1)  242 us
    dot_general x1, matrix products, on_device(): jnp.einsum('akhc,akw->hwc', rowwise, lon_inverse_matrix(), preferred_elem...  201 us
    dot_general x1, matrix products, on_device(): jnp.einsum('hwc,wk->khc', normed, lon_forward_matrix(), preferred_element...  53.3 us
    all_to_all x2, local copies, waits for them, and re-layouts, on_device(): lax.all_to_all(inverse, ('lat', 'lon'), split_axis=2, concat_axis=1, tile...  45.8 us
    convert_element_type x1, local copies, waits for them, and re-layouts, on_device(): inverse = inverse.astype(jnp.bfloat16)  41.4 us
    reduce_sum x1, other arithmetic, on_device(): spread = jnp.mean(centred * centred, axis=-1, keepdims=True)  38.8 us
  transfers between devices with their start and end apart: 4, of which 2 were waited for; matrix products, arithmetic and copies ran while one was open for 20% of the time, Pallas kernels for 0%

commit v1 on v0

v1 whole, which is shorter than its diff:
```python
import math

import jax
import jax.numpy as jnp
from jax import lax
from jax.experimental import pallas as pl
from jax.experimental.pallas import tpu as pltpu
from jax.sharding import PartitionSpec as P

H = 1024
W = 1920
KH = 512
KW = 512
MB = 128


shrink_level = 0.01


def padded(block, sides, width):
    for axis, dim in sides:
        count = lax.axis_size(axis)
        forward = [(i, i + 1) for i in range(count - 1)]
        backward = [(target, source) for source, target in forward]
        low = lax.ppermute(
            lax.slice_in_dim(block, block.shape[dim] - width, None, axis=dim), axis, forward
        )
        high = lax.ppermute(lax.slice_in_dim(block, 0, width, axis=dim), axis, backward)
        block = jnp.concatenate([low, block, high], axis=dim)
    return block


def complexify(weights):
    real_part = weights[0]
    imag_part = weights[1]
    top_rows = jnp.concatenate([real_part, imag_part], axis=1)
    low_rows = jnp.concatenate([-imag_part, real_part], axis=1)
    return jnp.concatenate([top_rows, low_rows], axis=0)


def spectral_mlp(modes, first_mat, first_bias, second_mat, second_bias):
    hidden = jnp.einsum("tmc,cd->tmd", modes, first_mat, preferred_element_type=jnp.float32)
    hidden = jax.nn.relu(hidden + first_bias.reshape(-1)).astype(jnp.bfloat16)
    second_out = jnp.einsum("tmc,cd->tmd", hidden, second_mat, preferred_element_type=jnp.float32)
    second_out = second_out + second_bias.reshape(-1)
    return second_out - jnp.clip(second_out, -shrink_level, shrink_level)


def lon_angles(modes, width):
    columns = jnp.arange(width, dtype=jnp.int32)[:, None]
    phases = columns * modes[None, :] % width
    return phases.astype(jnp.float32) * (2.0 * math.pi / width)


def lat_trig(lat_modes, height):
    freqs = lat_modes - KH // 2
    rowids = jnp.arange(height, dtype=jnp.int32)
    phases = jnp.mod(freqs[..., None] * rowids, height)
    angles = phases.astype(jnp.float32) * (2.0 * math.pi / height)
    factor = 1.0 / math.sqrt(height)
    return jnp.cos(angles) * factor, jnp.sin(angles) * factor


def epilogue_kernel(taps_ref, above_ref, main_ref, below_ref, *refs):
    out_ref = refs[-1]
    block_rows, width, _ = main_ref.shape
    taps = [taps_ref[pl.ds(i, 1), :] for i in range(9)]

    def row(i):
        if i < 0:
            return above_ref[0].astype(jnp.float32)
        if i >= block_rows:
            return below_ref[0].astype(jnp.float32)
        return main_ref[i].astype(jnp.float32)

    for h in range(block_rows):
        acc = None
        for r in range(3):
            x = row(h + r - 1)
            left = pltpu.roll(x, 1, 0)
            right = pltpu.roll(x, width - 1, 0)
            term = taps[3 * r] * left + taps[3 * r + 1] * x + taps[3 * r + 2] * right
            acc = term if acc is None else acc + term
        if len(refs) == 3:
            grid_ref, lon_ref = refs[0], refs[1]
            wave = jnp.dot(lon_ref[...], grid_ref[h], preferred_element_type=jnp.float32)
            wave = wave.astype(jnp.bfloat16)
        else:
            wave = refs[0][h]
        out_ref[h] = ((row(h) + wave.astype(jnp.float32)) + acc).astype(jnp.bfloat16)


def epilogue(field, low, high, conv_kernel, wave_args):
    rows, width, channels = field.shape
    block_rows = math.gcd(rows, 4)
    count = rows // block_rows
    above = jnp.concatenate([low, field[block_rows - 1 : rows - 1 : block_rows]], axis=0)
    below = jnp.concatenate([field[block_rows::block_rows], high], axis=0)
    taps = conv_kernel.reshape(9, channels)
    row_spec = pl.BlockSpec((1, width, channels), lambda i: (i, 0, 0))
    main_spec = pl.BlockSpec((block_rows, width, channels), lambda i: (i, 0, 0))
    if len(wave_args) == 2:
        grid_rows, lon_inv = wave_args
        n = grid_rows.shape[1]
        wave_specs = [
            pl.BlockSpec((block_rows, n, channels), lambda i: (i, 0, 0)),
            pl.BlockSpec((width, n), lambda i: (0, 0)),
        ]
    else:
        wave_specs = [main_spec]
    return pl.pallas_call(
        epilogue_kernel,
        grid=(count,),
        in_specs=[pl.BlockSpec((9, channels), lambda i: (0, 0)), row_spec, main_spec, row_spec]
        + wave_specs,
        out_specs=main_spec,
        out_shape=jax.ShapeDtypeStruct((rows, width, channels), jnp.bfloat16),
        compiler_params=pltpu.CompilerParams(dimension_semantics=("arbitrary",)),
    )(taps, above, field, below, *wave_args)


def on_device(field, w_first, b_first, w_second, b_second, conv_kernel, mode_plan):
    rows, width, channels = field.shape
    lat_count = lax.axis_size("lat")
    lon_count = lax.axis_size("lon")
    devs = lat_count * lon_count
    per_device = KW // devs
    blocks = KH // MB
    slots = mode_plan.shape[0] // lat_count
    height = rows * devs
    me = lax.axis_index("lat") * lon_count + lax.axis_index("lon")

    plan = mode_plan.reshape(lat_count, slots, lon_count).transpose(0, 2, 1).reshape(devs, slots)
    valid = plan >= 0
    tile = jnp.maximum(plan, 0)
    local_mode = tile // blocks
    lat_block = tile % blocks
    modes = jnp.arange(devs, dtype=jnp.int32)[:, None] * per_device + local_mode

    values = field.astype(jnp.float32)
    average = jnp.mean(values, axis=-1, keepdims=True)
    centred = values - average
    spread = jnp.mean(centred * centred, axis=-1, keepdims=True)
    normed = (centred * lax.rsqrt(spread + 1e-05)).astype(jnp.bfloat16)
    angles = lon_angles(modes.reshape(-1), width)
    factor = 1.0 / math.sqrt(width)
    lon_sub = (jnp.stack([jnp.cos(angles), -jnp.sin(angles)], axis=-1) * factor).astype(jnp.bfloat16)
    forward = jnp.einsum("hwc,wna->nahc", normed, lon_sub, preferred_element_type=jnp.float32)
    forward = forward.astype(jnp.bfloat16).reshape(devs, slots, 2, rows, channels)
    pencil = lax.all_to_all(forward, ("lat", "lon"), split_axis=0, concat_axis=0, tiled=True)

    my_block = lax.dynamic_index_in_dim(lat_block, me, 0, keepdims=False)
    my_valid = lax.dynamic_index_in_dim(valid, me, 0, keepdims=False)
    my_mode = lax.dynamic_index_in_dim(local_mode, me, 0, keepdims=False)
    lat_modes = my_block[:, None] * MB + jnp.arange(MB, dtype=jnp.int32)[None, :]
    cosine, sine = lat_trig(lat_modes, height)
    lat_fwd = jnp.stack(
        [jnp.stack([cosine, sine], axis=2), jnp.stack([-sine, cosine], axis=2)], axis=1
    ).astype(jnp.bfloat16)
    lat_fwd = lat_fwd.reshape(slots, 2, MB, 2, devs, rows)
    spectrum = jnp.einsum(
        "joqasr,sjarc->jqoc", lat_fwd, pencil, preferred_element_type=jnp.float32
    )
    tiles = spectrum.astype(jnp.bfloat16).reshape(slots, MB, 2 * channels)

    first_mat = complexify(w_first)
    second_mat = complexify(w_second)
    shrunk = spectral_mlp(tiles, first_mat, b_first, second_mat, b_second)
    filtered = jnp.where(my_valid[:, None, None], shrunk, 0.0).astype(jnp.bfloat16)
    filtered = filtered.reshape(slots, MB, 2, channels)

    lat_inv = jnp.stack(
        [jnp.stack([cosine, -sine], axis=1), jnp.stack([sine, cosine], axis=1)], axis=1
    ).astype(jnp.bfloat16)
    lat_inv = lat_inv.reshape(slots, 2, 2, MB, devs, rows)
    partial = jnp.einsum(
        "jabqsr,jqbc->sjarc", lat_inv, filtered, preferred_element_type=jnp.float32
    )
    same = (my_mode[:, None] == my_mode[None, :]) & my_valid[None, :]
    earlier = jnp.tril(jnp.ones((slots, slots), jnp.bool_), -1)
    first = my_valid & ~jnp.any(same & earlier, axis=1)
    merge = (same & first[:, None]).astype(jnp.float32)
    combined = jnp.einsum(
        "jk,skarc->sjarc", merge, partial, precision=lax.Precision.HIGHEST,
        preferred_element_type=jnp.float32,
    )
    inverse = combined.astype(jnp.bfloat16)
    rowwise = lax.all_to_all(inverse, ("lat", "lon"), split_axis=0, concat_axis=0, tiled=True)

    inv_angles = lon_angles(modes.reshape(-1), width)
    weights = jnp.where(modes.reshape(-1) == 0, 1.0, 2.0).astype(jnp.float32) / math.sqrt(width)
    lon_inv = jnp.stack(
        [weights * jnp.cos(inv_angles), -weights * jnp.sin(inv_angles)], axis=-1
    ).astype(jnp.bfloat16)
    lon_inv = lon_inv.reshape(width, devs * slots * 2)
    grid_rows = jnp.transpose(rowwise, (3, 0, 1, 2, 4)).reshape(rows, devs * slots * 2, channels)
    if devs * slots * 2 <= 512:
        wave_args = (grid_rows, lon_inv)
    else:
        wave = jnp.einsum("rnc,wn->rwc", grid_rows, lon_inv, preferred_element_type=jnp.float32)
        wave_args = (wave.astype(jnp.bfloat16),)

    count = devs
    forward_pairs = [(i, i + 1) for i in range(count - 1)]
    backward_pairs = [(t, s) for s, t in forward_pairs]
    low = lax.ppermute(field[rows - 1 :], ("lat", "lon"), forward_pairs)
    high = lax.ppermute(field[:1], ("lat", "lon"), backward_pairs)
    return epilogue(field, low, high, conv_kernel, wave_args)


def solution(mesh):
    placed = (P(("ens", "lat", "lon"), None, None), P(), P(), P(), P(), P(), P())
    return jax.shard_map(
        on_device,
        mesh=mesh,
        in_specs=placed,
        out_specs=P(("ens", "lat", "lon"), None, None),
        check_vma=False,
    )
```

time: 1590 us -> 320 us (0.20)
  waiting for transfers between devices: 691 us -> 56.9 us
  local copies, waits for them, and re-layouts: 396 us -> 26.9 us
  matrix products: 311 us -> 55.4 us
  Pallas kernels: 0 us -> 72.1 us
  other arithmetic: 142 us -> 87.4 us
  starting transfers between devices: 42.2 us -> 18.7 us
    ppermute x2, waiting for transfers between devices: 354 us -> 32.8 us  [the longest x1 32.8 us: on_device(): high = lax.ppermute(field[:1], ('lat', 'lon'), backward_pairs)]
    all_to_all x2, waiting for transfers between devices: 338 us -> 24.1 us  [the longest x1 24.1 us: on_device(): lax.all_to_all(forward, ('lat', 'lon'), split_axis=0, concat_axis=0, tile...]
    dot_general x4, matrix products: 302 us -> 54.2 us  [the longest x1 41.9 us: on_device(): jnp.einsum('hwc,wna->nahc', normed, lon_sub, preferred_element_type=jnp.f...]
    slice x2, local copies, waits for them, and re-layouts: 244 us -> 13.3 us  [the longest x1 11.3 us: epilogue(): below = jnp.concatenate([field[block_rows::block_rows], high], axis=0)]
    pallas_call x0 -> x1, Pallas kernels: none -> 72.1 us  [epilogue(): pl.pallas_call(epilogue_kernel, grid=(count,), in_specs=[pl.BlockSpec((9,...]
    all_to_all x3 -> x0, local copies, waits for them, and re-layouts: 54.2 us -> none  [the longest x2 45.8 us: on_device(): lax.all_to_all(inverse, ('lat', 'lon'), split_axis=2, concat_axis=1, tile...]
    reshape x4 -> x3, local copies, waits for them, and re-layouts: 55.2 us -> 3.34 us  [the longest x1 2.67 us: on_device(): forward.astype(jnp.bfloat16).reshape(devs, slots, 2, rows, channels)]
    convert_element_type x1 -> x2, local copies, waits for them, and re-layouts: 41.4 us -> 1.21 us  [on_device(): lon_inv = jnp.stack([weights * jnp.cos(inv_angles), -weights * jnp.sin(in...]
  transfers between devices with their start and end apart: 4 -> 4, of which waited for: 2 -> 2; matrix products, arithmetic and copies ran while one was open for 20% -> 16% of each run, Pallas kernels for 0% -> 0%
where the time goes in v1:
time: 320 us; the launch traced here: 318 us
  other arithmetic  87.4 us (27%)
  Pallas kernels  72.1 us (23%)
  waiting for transfers between devices  56.9 us (18%)
  matrix products  55.4 us (17%)
  local copies, waits for them, and re-layouts  26.9 us (8%)
  starting transfers between devices  18.7 us (6%)
    pallas_call x1, Pallas kernels, epilogue(): pl.pallas_call(epilogue_kernel, grid=(count,), in_specs=[pl.BlockSpec((9,...  72.1 us
    dot_general x1, matrix products, on_device(): jnp.einsum('hwc,wna->nahc', normed, lon_sub, preferred_element_type=jnp.f...  41.9 us
    reduce_sum x1, other arithmetic, on_device(): spread = jnp.mean(centred * centred, axis=-1, keepdims=True)  38.4 us
    ppermute x1, waiting for transfers between devices, on_device(): high = lax.ppermute(field[:1], ('lat', 'lon'), backward_pairs)  32.8 us
    all_to_all x1, waiting for transfers between devices, on_device(): lax.all_to_all(forward, ('lat', 'lon'), split_axis=0, concat_axis=0, tile...  24.1 us
    another operation x3, other arithmetic  24.1 us
    reduce_sum x1, other arithmetic, on_device(): average = jnp.mean(values, axis=-1, keepdims=True)  11.3 us
    slice x1, local copies, waits for them, and re-layouts, epilogue(): below = jnp.concatenate([field[block_rows::block_rows], high], axis=0)  11.3 us
  transfers between devices with their start and end apart: 4, of which 2 were waited for; matrix products, arithmetic and copies ran while one was open for 16% of the time, Pallas kernels for 0%

profile of v1, /device:TPU:16, one launch (start us, length us, event | category | flops | bytes accessed | tf_op | source)
XLA Modules:
  0.0 317.6 jit_solution(1247725713795183307)
XLA Ops:
  0.0 0.7 broadcast_compare_fusion.1
  0.7 0.7 maximum_shift-right-logical_fusion
  1.4 0.1 reshape.483
  1.6 0.1 add.191
  1.7 0.1 rem.93
  1.8 0.1 and.174
  1.9 0.1 div.32
  2.0 11.3 %convert_reduce_fusion = f32[64,1920]{1,0:T(8,128)S(1)} fusion(bf16[64,1920,128]{2,1,0:T(8,128)(2,1)} %main_ref.1), kind=kLoop, calls=%fused_computation.1 | loop fusion | flops 31334400 | bytes 31948800 | tf_op jit(solution)/shard_map/reduce_sum | solution.py:141
  13.4 38.4 %fusion.2 = f32[64,1920]{1,0:T(8,128)S(1)} fusion(bf16[64,1920,128]{2,1,0:T(8,128)(2,1)} %main_ref.1, f32[64,1920]{1,0:T(8,128)S(1)} %broadcast_multiply_fusion), kind=kLoop, calls=%fused_computation.4 | loop fusion | flops 62791680 | bytes 32440320 | tf_op jit(solution)/shard_map/reduce_sum | solution.py:143
  51.8 3.1 multiply_convert_fusion.3
  55.0 41.9 %fusion.29 = bf16[64,2,64,128]{3,0,2,1:T(8,128)(2,1)S(1)} fusion(bf16[64,1920,128]{2,1,0:T(8,128)(2,1)} %main_ref.1, f32[64,1920]{1,0:T(8,128)S(1)} %add_rsqrt_fusion, f32[64,1920]{1,0:T(8,128)S(1)} %broadcast_multiply_fusion, bf16[1920,64,2,1]{0,1,3,2:T(8,128)(2,1)S(1)} %fusion.102), kind=kOutput, calls=%fused_computation.48 | convolution fusion | flops 4090494976 | bytes 35028992 | tf_op jit(solution)/shard_map/hwc,wna->nahc/dot_general | solution.py:148
  96.9 2.7 copy.30
  99.6 7.1 %all-to-all-start = ((bf16[16,4,2,64,128]{4,3,2,1,0:T(8,128)(2,1)}), bf16[16,4,2,64,128]{4,3,2,1,0:T(8,128)(2,1)S(1)}, u32[]{:S(2)}, u32[]{:S(2)}) async-start(bf16[16,4,2,64,128]{4,3,2,1,0:T(8,128)(2,1)} %copy.30), calls=%async_computation | async-start | bytes 4194304 | tf_op jit(solution)/shard_map/all_to_all | solution.py:150
  106.7 0.1 copy.36
  106.8 0.1 ge.17
  106.9 0.1 copy.27
  107.0 0.1 ge.19
  107.1 0.1 copy.35
  107.3 0.1 ne.200
  107.3 0.1 copy.31
  107.5 0.1 rem.97
  107.5 0.1 div.35
  107.6 0.2 dynamic-slice_reduce_fusion.1
  107.8 0.2 dynamic-slice_reduce_fusion
  108.1 0.2 fusion.74
  108.3 0.6 not_and_fusion
  109.0 0.6 slice_bitcast_fusion
  109.6 10.0 %negate_convert_fusion = (bf16[4,1,1,128,16,64]{3,5,2,4,1,0:T(8,128)(2,1)S(1)}, bf16[4,1,1,128,16,64]{3,5,2,4,1,0:T(8,128)(2,1)}, bf16[4,1,1,128,16,64]{3,5,2,4,1,0:T(8,128)(2,1)}) fusion(s32[16,64]{1,0:T(8,128)S(1)} %multiply_add_fusion, s32[4,128]{1,0:T(4,128)S(1)} %add_add_fusion), kind=kLoop, calls=%fused_computation.42 | loop fusion | flops 10485760 | bytes 3151872 | tf_op jit(solution)/shard_map/convert.7
  119.6 11.0 %fusion.34 = (bf16[4,1,128,1,16,64]{2,5,4,3,1,0:T(8,128)(2,1)}, bf16[4,1,128,1,16,64]{2,5,4,3,1,0:T(8,128)(2,1)}, bf16[4,1,128,1,16,64]{2,5,4,3,1,0:T(8,128)(2,1)}) fusion(s32[16,64]{1,0:T(8,128)S(1)} %multiply_add_fusion, s32[4,128]{1,0:T(4,128)S(1)} %add_add_fusion), kind=kLoop, calls=%fused_computation.49 | loop fusion | flops 10485760 | bytes 3151872 | tf_op jit(solution)/shard_map/convert.13
  130.6 24.1 %all-to-all-done = bf16[16,4,2,64,128]{4,3,2,1,0:T(8,128)(2,1)S(1)} async-done(((bf16[16,4,2,64,128]{4,3,2,1,0:T(8,128)(2,1)}), bf16[16,4,2,64,128]{4,3,2,1,0:T(8,128)(2,1)S(1)}, u32[]{:S(2)}, u32[]{:S(2)}) %all-to-all-start) | async-done | bytes 2097184 | tf_op jit(solution)/shard_map/all_to_all | solution.py:150
  154.7 2.8 fusion.15
  157.6 1.2 fusion.40
  158.9 3.1 fusion.19
  162.0 6.4 %convert_bitcast_fusion = bf16[16,4,2,64,128]{4,1,3,2,0:T(4,128)(2,1)} fusion(f32[16,4,2,64,128]{4,3,0,2,1:T(8,128)S(1)} %fusion.19, s32[4]{0:T(128)S(1)} %copy-done.4, pred[4]{0:T(512)(128)(4,1)S(1)} %copy-done.8, pred[4]{0:T(512)(128)(4,1)S(1)} %copy-done.7), kind=kOutput, calls=%fused_computation.41 | convolution fusion | flops 51380272 | bytes 6291480 | tf_op jit(solution)/shard_map/jk,skarc->sjarc/dot_general | solution.py:183
  168.4 5.0 %all-to-all-start.1 = ((bf16[16,4,2,64,128]{4,1,3,2,0:T(4,128)(2,1)}), bf16[16,4,2,64,128]{4,1,3,2,0:T(4,128)(2,1)}, u32[]{:S(2)}, u32[]{:S(2)}) async-start(bf16[16,4,2,64,128]{4,1,3,2,0:T(4,128)(2,1)} %convert_bitcast_fusion), calls=%async_computation.1 | async-start | bytes 4194304 | tf_op jit(solution)/shard_map/all_to_all | solution.py:188
  173.4 2.0 fusion.94
  175.5 4.3 %collective-permute-start.1 = (bf16[1,1920,128]{2,1,0:T(8,128)(2,1)S(1)}, bf16[1,1920,128]{2,1,0:T(8,128)(2,1)}, u32[]{:S(2)}, u32[]{:S(2)}) collective-permute-start(bf16[1,1920,128]{2,1,0:T(8,128)(2,1)S(1)} %get-tuple-element.9), channel_id=1, source_target_pairs={{2,0},{4,2},{6,4},{8,6},{10,8},{12,10},{14,12},{16,14},{18,16},{20... | collective-permute-start | bytes 1474568 | tf_op jit(solution)/shard_map/ppermute | solution.py:207
  179.8 2.3 collective-permute-start
  182.0 11.3 %fusion.93 = (bf16[15,1920,128]{2,1,0:T(8,128)(2,1)}, bf16[15,1920,128]{2,1,0:T(8,128)(2,1)}) fusion(bf16[64,1920,128]{2,1,0:T(8,128)(2,1)} %main_ref.1), kind=kLoop, calls=%fused_computation.137 | loop fusion | bytes 29491200 | tf_op jit(solution)/shard_map/slice | solution.py:98
  193.4 0.6 reshape.477.taps_ref
  194.0 0.5 copy.39
  194.5 0.2 convert_element_type.119
  194.7 1.0 copy.40.refs_1_
  195.7 32.8 %collective-permute-done.1 = bf16[1,1920,128]{2,1,0:T(8,128)(2,1)} collective-permute-done((bf16[1,1920,128]{2,1,0:T(8,128)(2,1)S(1)}, bf16[1,1920,128]{2,1,0:T(8,128)(2,1)}, u32[]{:S(2)}, u32[]{:S(2)}) %collective-permute-start.1) | collective-permute-done | bytes 491552 | tf_op jit(solution)/shard_map/ppermute | solution.py:207
  228.5 7.1 %pad_maximum_fusion.1.below_ref = bf16[16,1920,128]{2,1,0:T(8,128)(2,1)} fusion(bf16[1,1920,128]{2,1,0:T(8,128)(2,1)} %collective-permute-done.1, bf16[15,1920,128]{2,1,0:T(8,128)(2,1)} %get-tuple-element.7), kind=kLoop, calls=%fused_computation.9 | loop fusion | flops 3932160 | bytes 15728640 | tf_op jit(solution)/shard_map/concatenate | solution.py:98
  235.6 3.8 %pad_maximum_fusion.above_ref = bf16[16,1920,128]{2,1,0:T(8,128)(2,1)} fusion(bf16[15,1920,128]{2,1,0:T(8,128)(2,1)S(1)} %bitcast.93, bf16[1,1920,128]{2,1,0:T(8,128)(2,1)S(1)} %collective-permute-done), kind=kLoop, calls=%fused_computation.8 | loop fusion | flops 3932160 | bytes 15728640 | tf_op jit(solution)/shard_map/concatenate | solution.py:97
  239.4 6.1 %copy.38 = bf16[64,16,4,2,128]{4,3,2,1,0:T(2,128)(2,1)} copy(bf16[64,16,4,2,128]{4,2,0,3,1:T(4,128)(2,1)} %bitcast.28) | data formatting | bytes 4194304 | tf_op jit(solution)/shard_map/transpose | solution.py:196
  245.6 72.1 %shard_map.73 = bf16[64,1920,128]{2,1,0:T(8,128)(2,1)} custom-call(f32[9,128]{1,0:T(8,128)} %reshape.477.taps_ref, bf16[16,1920,128]{2,1,0:T(8,128)(2,1)} %pad_maximum_fusion.above_ref, bf16[64,1920,128]{2,1,0:T(8,128)(2,1)} %main_ref.1, bf16[16,1920,128]{2,1,0:T(8,128)(2,1)} %pad_maximum_fusion.1.below_ref, bf16[64,128,128]{2,1,0:T(8,128)(2,1)} %bitcast.94, ...), custom_call_target="tpu_custom_call" | custom-call | tf_op jit(solution)/shard_map/pallas_call | solution.py:111
  (44 shorter events, 0.7 us)
Async XLA Ops:
  96.9 12.0 %copy-start.1 = (bf16[2,128,128]{2,1,0:T(8,128)(2,1)S(1)}, bf16[2,128,128]{2,1,0:T(8,128)(2,1)}, u32[]{:S(2)}) copy-start(bf16[2,128,128]{2,1,0:T(8,128)(2,1)} %param.10) | copy-start | bytes 196612
  96.9 12.0 %copy-start.2 = (bf16[2,128,128]{2,1,0:T(8,128)(2,1)S(1)}, bf16[2,128,128]{2,1,0:T(8,128)(2,1)}, u32[]{:S(2)}) copy-start(bf16[2,128,128]{2,1,0:T(8,128)(2,1)} %param.8) | copy-start | bytes 196612
  99.6 55.1 %all-to-all-start = ((bf16[16,4,2,64,128]{4,3,2,1,0:T(8,128)(2,1)}), bf16[16,4,2,64,128]{4,3,2,1,0:T(8,128)(2,1)S(1)}, u32[]{:S(2)}, u32[]{:S(2)}) async-start(bf16[16,4,2,64,128]{4,3,2,1,0:T(8,128)(2,1)} %copy.30), calls=%async_computation | async-start | bytes 4194304 | tf_op jit(solution)/shard_map/all_to_all | solution.py:150
  107.8 1.1 copy-start.6
  108.1 0.9 copy-start.3
  158.9 3.1 copy-start.4
  158.9 3.1 copy-start.7
  158.9 3.1 copy-start.8
  168.4 71.0 %all-to-all-start.1 = ((bf16[16,4,2,64,128]{4,1,3,2,0:T(4,128)(2,1)}), bf16[16,4,2,64,128]{4,1,3,2,0:T(4,128)(2,1)}, u32[]{:S(2)}, u32[]{:S(2)}) async-start(bf16[16,4,2,64,128]{4,1,3,2,0:T(4,128)(2,1)} %convert_bitcast_fusion), calls=%async_computation.1 | async-start | bytes 4194304 | tf_op jit(solution)/shard_map/all_to_all | solution.py:188
  175.5 53.0 %collective-permute-start.1 = (bf16[1,1920,128]{2,1,0:T(8,128)(2,1)S(1)}, bf16[1,1920,128]{2,1,0:T(8,128)(2,1)}, u32[]{:S(2)}, u32[]{:S(2)}) collective-permute-start(bf16[1,1920,128]{2,1,0:T(8,128)(2,1)S(1)} %get-tuple-element.9), channel_id=1, source_target_pairs={{2,0},{4,2},{6,4},{8,6},{10,8},{12,10},{14,12},{16,14},{18,16},{20... | collective-permute-start | bytes 1474568 | tf_op jit(solution)/shard_map/ppermute | solution.py:207
  179.7 13.6 %copy-start = (bf16[1920,64,1]{0,1,2:T(8,128)(2,1)S(1)}, bf16[1920,64,1]{0,1,2:T(8,128)(2,1)}, u32[]{:S(2)}) copy-start(bf16[1920,64,1]{0,1,2:T(8,128)(2,1)} %get-tuple-element.28) | copy-start | bytes 737284
  179.7 13.6 %copy-start.5 = (f32[3,3,128]{2,1,0:T(4,128)S(1)}, f32[3,3,128]{2,1,0:T(4,128)}, u32[]{:S(2)}) copy-start(f32[3,3,128]{2,1,0:T(4,128)} %param.12) | copy-start | bytes 13828
  179.8 55.8 %collective-permute-start = (bf16[1,1920,128]{2,1,0:T(8,128)(2,1)}, bf16[1,1920,128]{2,1,0:T(8,128)(2,1)S(1)}, u32[]{:S(2)}, u32[]{:S(2)}) collective-permute-start(bf16[1,1920,128]{2,1,0:T(8,128)(2,1)} %get-tuple-element.10), channel_id=1, source_target_pairs={{0,2},{2,4},{4,6},{6,8},{8,10},{10,12},{12,14},{14,16},{16,18},{18... | collective-permute-start | bytes 1474568 | tf_op jit(solution)/shard_map/ppermute | solution.py:206
  228.5 7.1 %slice-start = ((s8[7372800]{0:T(1024)(128)(4,1)}), s8[4194304]{0:T(1024)(128)(4,1)S(1)}, s32[]{:S(2)}) async-start(s8[7372800]{0:T(1024)(128)(4,1)} %bitcast.92), calls=%async_computation.2 | async-start | bytes 8388608
  228.5 7.1 %slice-start.1 = ((s8[7372800]{0:T(1024)(128)(4,1)}), s8[3178496]{0:T(1024)(128)(4,1)S(1)}, s32[]{:S(2)}) async-start(s8[7372800]{0:T(1024)(128)(4,1)} %bitcast.92), calls=%async_computation.3 | async-start | bytes 6356992

commit v2 on v1

--- a/solution.py
+++ b/solution.py
@@ -15,19 +15,6 @@
 
 
 shrink_level = 0.01
-
-
-def padded(block, sides, width):
-    for axis, dim in sides:
-        count = lax.axis_size(axis)
-        forward = [(i, i + 1) for i in range(count - 1)]
-        backward = [(target, source) for source, target in forward]
-        low = lax.ppermute(
-            lax.slice_in_dim(block, block.shape[dim] - width, None, axis=dim), axis, forward
-        )
-        high = lax.ppermute(lax.slice_in_dim(block, 0, width, axis=dim), axis, backward)
-        block = jnp.concatenate([low, block, high], axis=dim)
-    return block
 
 
 def complexify(weights):
@@ -59,6 +46,35 @@
     angles = phases.astype(jnp.float32) * (2.0 * math.pi / height)
     factor = 1.0 / math.sqrt(height)
     return jnp.cos(angles) * factor, jnp.sin(angles) * factor
+
+
+def forward_kernel(field_ref, lon_ref, out_ref):
+    block_rows, _, channels = field_ref.shape
+    lon = lon_ref[...]
+    for h in range(block_rows):
+        x = field_ref[h].astype(jnp.float32)
+        average = jnp.sum(x, axis=1, keepdims=True) * (1.0 / channels)
+        centred = x - average
+        spread = jnp.sum(centred * centred, axis=1, keepdims=True) * (1.0 / channels)
+        normed = (centred * lax.rsqrt(spread + 1e-05)).astype(jnp.bfloat16)
+        out_ref[h] = jnp.dot(lon, normed, preferred_element_type=jnp.float32).astype(jnp.bfloat16)
+
+
+def forward_rows(field, lon_t):
+    rows, width, channels = field.shape
+    n = lon_t.shape[0]
+    block_rows = math.gcd(rows, 4)
+    return pl.pallas_call(
+        forward_kernel,
+        grid=(rows // block_rows,),
+        in_specs=[
+            pl.BlockSpec((block_rows, width, channels), lambda i: (i, 0, 0)),
+            pl.BlockSpec((n, width), lambda i: (0, 0)),
+        ],
+        out_specs=pl.BlockSpec((block_rows, n, channels), lambda i: (i, 0, 0)),
+        out_shape=jax.ShapeDtypeStruct((rows, n, channels), jnp.bfloat16),
+        compiler_params=pltpu.CompilerParams(dimension_semantics=("arbitrary",)),
+    )(field, lon_t)
 
 
 def epilogue_kernel(taps_ref, above_ref, main_ref, below_ref, *refs):
@@ -137,16 +153,21 @@
     lat_block = tile % blocks
     modes = jnp.arange(devs, dtype=jnp.int32)[:, None] * per_device + local_mode
 
-    values = field.astype(jnp.float32)
-    average = jnp.mean(values, axis=-1, keepdims=True)
-    centred = values - average
-    spread = jnp.mean(centred * centred, axis=-1, keepdims=True)
-    normed = (centred * lax.rsqrt(spread + 1e-05)).astype(jnp.bfloat16)
     angles = lon_angles(modes.reshape(-1), width)
     factor = 1.0 / math.sqrt(width)
     lon_sub = (jnp.stack([jnp.cos(angles), -jnp.sin(angles)], axis=-1) * factor).astype(jnp.bfloat16)
-    forward = jnp.einsum("hwc,wna->nahc", normed, lon_sub, preferred_element_type=jnp.float32)
-    forward = forward.astype(jnp.bfloat16).reshape(devs, slots, 2, rows, channels)
+    if devs * slots * 2 <= 512:
+        lon_t = jnp.transpose(lon_sub, (1, 2, 0)).reshape(devs * slots * 2, width)
+        forward = forward_rows(field, lon_t).reshape(rows, devs, slots, 2, channels)
+        forward = jnp.transpose(forward, (1, 2, 3, 0, 4))
+    else:
+        values = field.astype(jnp.float32)
+        average = jnp.mean(values, axis=-1, keepdims=True)
+        centred = values - average
+        spread = jnp.mean(centred * centred, axis=-1, keepdims=True)
+        normed = (centred * lax.rsqrt(spread + 1e-05)).astype(jnp.bfloat16)
+        forward = jnp.einsum("hwc,wna->nahc", normed, lon_sub, preferred_element_type=jnp.float32)
+        forward = forward.astype(jnp.bfloat16).reshape(devs, slots, 2, rows, channels)
     pencil = lax.all_to_all(forward, ("lat", "lon"), split_axis=0, concat_axis=0, tiled=True)
 
     my_block = lax.dynamic_index_in_dim(lat_block, me, 0, keepdims=False)

time: 320 us -> 276 us (0.86)
  other arithmetic: 87.4 us -> 37.5 us
  matrix products: 55.4 us -> 13.7 us
  Pallas kernels: 72.1 us -> 113 us
  local copies, waits for them, and re-layouts: 26.9 us -> 33.2 us
    reduce_sum x2 -> x0, other arithmetic: 49.7 us -> none  [the longest x1 38.4 us: on_device(): spread = jnp.mean(centred * centred, axis=-1, keepdims=True)]
    dot_general x1 -> x0, matrix products: 41.9 us -> none  [on_device(): jnp.einsum('hwc,wna->nahc', normed, lon_sub, preferred_element_type=jnp.f...]
    pallas_call x0 -> x1, Pallas kernels: none -> 40.9 us  [forward_rows(): pl.pallas_call(forward_kernel, grid=(rows // block_rows,), in_specs=[pl.B...]
    reshape x1 -> x2, local copies, waits for them, and re-layouts: 2.67 us -> 6.33 us  [the longest x1 5.35 us: on_device(): forward = forward_rows(field, lon_t).reshape(rows, devs, slots, 2, channels)]
  transfers between devices with their start and end apart: 4 -> 4, of which waited for: 2 -> 2; matrix products, arithmetic and copies ran while one was open for 16% -> 18% of each run, Pallas kernels for 0% -> 0%
where the time goes in v2:
time: 276 us; the launch traced here: 274 us
  Pallas kernels  113 us (41%)
  waiting for transfers between devices  57.1 us (21%)
  other arithmetic  37.5 us (14%)
  local copies, waits for them, and re-layouts  33.2 us (12%)
  starting transfers between devices  18.8 us (7%)
  matrix products  13.7 us (5%)
    pallas_call x1, Pallas kernels, epilogue(): pl.pallas_call(epilogue_kernel, grid=(count,), in_specs=[pl.BlockSpec((9,...  72.1 us
    pallas_call x1, Pallas kernels, forward_rows(): pl.pallas_call(forward_kernel, grid=(rows // block_rows,), in_specs=[pl.B...  40.9 us
    ppermute x1, waiting for transfers between devices, on_device(): high = lax.ppermute(field[:1], ('lat', 'lon'), backward_pairs)  32.9 us
    all_to_all x1, waiting for transfers between devices, on_device(): lax.all_to_all(forward, ('lat', 'lon'), split_axis=0, concat_axis=0, tile...  24.3 us
    another operation x3, other arithmetic  24 us
    slice x1, local copies, waits for them, and re-layouts, epilogue(): below = jnp.concatenate([field[block_rows::block_rows], high], axis=0)  11.2 us
    all_to_all x1, starting transfers between devices, on_device(): lax.all_to_all(forward, ('lat', 'lon'), split_axis=0, concat_axis=0, tile...  7.24 us
    concatenate x1, other arithmetic, epilogue(): below = jnp.concatenate([field[block_rows::block_rows], high], axis=0)  7.11 us
  transfers between devices with their start and end apart: 4, of which 2 were waited for; matrix products, arithmetic and copies ran while one was open for 18% of the time, Pallas kernels for 0%

profile of v2, /device:TPU:16, one launch (start us, length us, event | category | flops | bytes accessed | tf_op | source)
XLA Modules:
  0.0 273.7 jit_solution(28560661850212656)
XLA Ops:
  0.0 0.7 broadcast_compare_fusion.1
  0.7 0.7 maximum_shift-right-logical_fusion
  1.4 0.1 reshape.475
  1.6 0.1 add.180
  1.8 0.1 and.174
  1.9 0.1 div.26
  2.0 3.1 %multiply_convert_fusion.3 = (bf16[1920,64,1]{0,1,2:T(8,128)(2,1)S(1)}, bf16[1920,64,1]{0,1,2:T(8,128)(2,1)}, f32[1920,64,1]{0,1,2:T(8,128)S(1)}, f32[1920,64,1]{0,1,2:T(8,128)S(1)}) fusion(f32[64]{0:T(128)S(1)} %get-tuple-element.5, s32[64]{0:T(128)S(1)} %get-tuple-element.6, f32[64]{0:T(128)S(1)} %fusion.75), kind=kLoop, calls=%fused_computation.59 | loop fusion | flops 1720320 | bytes 1475328 | tf_op jit(solution)/shard_map/convert
  5.2 0.5 copy.55
  5.7 1.0 reshape.469.lon_ref
  6.7 40.9 %shard_map.73 = bf16[64,128,128]{2,1,0:T(8,128)(2,1)} custom-call(bf16[64,1920,128]{2,1,0:T(8,128)(2,1)} %main_ref.1, bf16[128,1920]{1,0:T(8,128)(2,1)} %reshape.469.lon_ref), custom_call_target="tpu_custom_call" | custom-call | tf_op jit(solution)/shard_map/pallas_call | solution.py:67
  47.6 5.4 %copy.85 = bf16[64,16,4,2,128]{4,0,3,2,1:T(8,128)(2,1)} copy(bf16[64,16,4,2,128]{4,3,2,1,0:T(2,128)(2,1)} %bitcast.82) | data formatting | bytes 4194304 | tf_op jit(solution)/shard_map/reshape | solution.py:161
  53.0 7.2 %all-to-all-start = ((bf16[16,4,2,64,128]{4,3,2,1,0:T(8,128)(2,1)}), bf16[16,4,2,64,128]{4,3,2,1,0:T(8,128)(2,1)S(1)}, u32[]{:S(2)}, u32[]{:S(2)}) async-start(bf16[16,4,2,64,128]{4,3,2,1,0:T(8,128)(2,1)} %bitcast.77), calls=%async_computation | async-start | bytes 4194304 | tf_op jit(solution)/shard_map/all_to_all | solution.py:171
  60.2 0.1 copy.61
  60.3 0.1 ge.17
  60.4 0.1 copy.52
  60.5 0.1 ge.19
  60.6 0.1 copy.60
  60.8 0.1 ne.200
  60.8 0.1 copy.57
  61.0 0.1 rem.97
  61.1 0.2 dynamic-slice_reduce_fusion.1
  61.3 0.2 dynamic-slice_reduce_fusion
  61.6 0.2 fusion.62
  61.8 0.5 not_and_fusion
  62.4 0.6 slice_bitcast_fusion
  63.0 10.0 %negate_convert_fusion = (bf16[4,1,1,128,16,64]{3,5,2,4,1,0:T(8,128)(2,1)S(1)}, bf16[4,1,1,128,16,64]{3,5,2,4,1,0:T(8,128)(2,1)}, bf16[4,1,1,128,16,64]{3,5,2,4,1,0:T(8,128)(2,1)}) fusion(s32[16,64]{1,0:T(8,128)S(1)} %multiply_add_fusion, s32[4,128]{1,0:T(4,128)S(1)} %add_add_fusion), kind=kLoop, calls=%fused_computation.35 | loop fusion | flops 10485760 | bytes 3151872 | tf_op jit(solution)/shard_map/convert.7
  73.0 11.0 %fusion.24 = (bf16[4,1,128,1,16,64]{2,5,3,1,0,4:T(8,128)(2,1)}, bf16[4,1,128,1,16,64]{2,5,3,1,0,4:T(8,128)(2,1)}, bf16[4,1,128,1,16,64]{2,5,3,1,0,4:T(8,128)(2,1)}) fusion(s32[16,64]{1,0:T(8,128)S(1)} %multiply_add_fusion, s32[4,128]{1,0:T(4,128)S(1)} %add_add_fusion), kind=kLoop, calls=%fused_computation.41 | loop fusion | flops 10485760 | bytes 3151872 | tf_op jit(solution)/shard_map/convert.13
  84.0 24.3 %all-to-all-done = bf16[16,4,2,64,128]{4,3,2,1,0:T(8,128)(2,1)S(1)} async-done(((bf16[16,4,2,64,128]{4,3,2,1,0:T(8,128)(2,1)}), bf16[16,4,2,64,128]{4,3,2,1,0:T(8,128)(2,1)S(1)}, u32[]{:S(2)}, u32[]{:S(2)}) %all-to-all-start) | async-done | bytes 2097184 | tf_op jit(solution)/shard_map/all_to_all | solution.py:171
  108.3 2.8 %fusion.8 = bf16[4,128,2,128,1,1]{3,1,4,0,2,5:T(8,128)(2,1)S(1)} fusion(bf16[16,4,2,64,128]{4,3,2,1,0:T(8,128)(2,1)S(1)} %all-to-all-done, bf16[4,1,128,1,16,64]{2,5,3,1,0,4:T(8,128)(2,1)} %get-tuple-element.17, bf16[4,1,128,1,16,64]{2,5,3,1,0,4:T(8,128)(2,1)} %get-tuple-element.16, bf16[4,1,128,1,16,64]{2,5,3,1,0,4:T(8,128)(2,1)} %get-tuple-element.15), kind=kOutput, calls=%fused_computation.11 | convolution fusion | flops 543162368 | bytes 5505024 | tf_op jit(solution)/shard_map/joqasr,sjarc->jqoc/dot_general | solution.py:182
  111.1 0.7 copy.86
  111.8 2.1 fusion.30
  113.9 1.7 reshape.472
  115.6 2.4 fusion.12
  118.1 6.4 %convert_bitcast_fusion = bf16[16,4,2,64,128]{4,1,3,2,0:T(4,128)(2,1)} fusion(f32[16,4,2,64,128]{4,3,0,2,1:T(8,128)S(1)} %fusion.12, s32[4]{0:T(128)S(1)} %copy-done.6, pred[4]{0:T(512)(128)(4,1)S(1)} %copy-done.10, pred[4]{0:T(512)(128)(4,1)S(1)} %copy-done.9), kind=kOutput, calls=%fused_computation.34 | convolution fusion | flops 51380272 | bytes 6291480 | tf_op jit(solution)/shard_map/jk,skarc->sjarc/dot_general | solution.py:204
  124.5 5.0 %all-to-all-start.1 = ((bf16[16,4,2,64,128]{4,1,3,2,0:T(4,128)(2,1)}), bf16[16,4,2,64,128]{4,1,3,2,0:T(4,128)(2,1)}, u32[]{:S(2)}, u32[]{:S(2)}) async-start(bf16[16,4,2,64,128]{4,1,3,2,0:T(4,128)(2,1)} %convert_bitcast_fusion), calls=%async_computation.1 | async-start | bytes 4194304 | tf_op jit(solution)/shard_map/all_to_all | solution.py:209
  129.5 2.0 fusion.80
  131.5 4.3 %collective-permute-start.1 = (bf16[1,1920,128]{2,1,0:T(8,128)(2,1)S(1)}, bf16[1,1920,128]{2,1,0:T(8,128)(2,1)}, u32[]{:S(2)}, u32[]{:S(2)}) collective-permute-start(bf16[1,1920,128]{2,1,0:T(8,128)(2,1)S(1)} %get-tuple-element.9), channel_id=1, source_target_pairs={{2,0},{4,2},{6,4},{8,6},{10,8},{12,10},{14,12},{16,14},{18,16},{20... | collective-permute-start | bytes 1474568 | tf_op jit(solution)/shard_map/ppermute | solution.py:228
  135.8 2.3 collective-permute-start
  138.1 11.2 %fusion.79 = (bf16[15,1920,128]{2,1,0:T(8,128)(2,1)}, bf16[15,1920,128]{2,1,0:T(8,128)(2,1)}) fusion(bf16[64,1920,128]{2,1,0:T(8,128)(2,1)} %main_ref.1), kind=kLoop, calls=%fused_computation.124 | loop fusion | bytes 29491200 | tf_op jit(solution)/shard_map/slice | solution.py:114
  149.4 0.6 reshape.468.taps_ref
  150.0 0.5 copy.64
  150.5 0.2 convert_element_type.107
  150.7 1.0 copy.65.refs_1_
  151.7 32.9 %collective-permute-done.1 = bf16[1,1920,128]{2,1,0:T(8,128)(2,1)} collective-permute-done((bf16[1,1920,128]{2,1,0:T(8,128)(2,1)S(1)}, bf16[1,1920,128]{2,1,0:T(8,128)(2,1)}, u32[]{:S(2)}, u32[]{:S(2)}) %collective-permute-start.1) | collective-permute-done | bytes 491552 | tf_op jit(solution)/shard_map/ppermute | solution.py:228
  184.5 7.1 %pad_maximum_fusion.1.below_ref = bf16[16,1920,128]{2,1,0:T(8,128)(2,1)} fusion(bf16[1,1920,128]{2,1,0:T(8,128)(2,1)} %collective-permute-done.1, bf16[15,1920,128]{2,1,0:T(8,128)(2,1)} %get-tuple-element.7), kind=kLoop, calls=%fused_computation.1 | loop fusion | flops 3932160 | bytes 15728640 | tf_op jit(solution)/shard_map/concatenate | solution.py:114
  191.7 3.8 %pad_maximum_fusion.above_ref = bf16[16,1920,128]{2,1,0:T(8,128)(2,1)} fusion(bf16[15,1920,128]{2,1,0:T(8,128)(2,1)S(1)} %bitcast.80, bf16[1,1920,128]{2,1,0:T(8,128)(2,1)S(1)} %collective-permute-done), kind=kLoop, calls=%fused_computation | loop fusion | flops 3932160 | bytes 15728640 | tf_op jit(solution)/shard_map/concatenate | solution.py:113
  195.5 6.1 %copy.63 = bf16[64,16,4,2,128]{4,3,2,1,0:T(2,128)(2,1)} copy(bf16[64,16,4,2,128]{4,2,0,3,1:T(4,128)(2,1)} %bitcast.28) | data formatting | bytes 4194304 | tf_op jit(solution)/shard_map/transpose | solution.py:217
  201.6 72.1 %shard_map.74 = bf16[64,1920,128]{2,1,0:T(8,128)(2,1)} custom-call(f32[9,128]{1,0:T(8,128)} %reshape.468.taps_ref, bf16[16,1920,128]{2,1,0:T(8,128)(2,1)} %pad_maximum_fusion.above_ref, bf16[64,1920,128]{2,1,0:T(8,128)(2,1)} %main_ref.1, bf16[16,1920,128]{2,1,0:T(8,128)(2,1)} %pad_maximum_fusion.1.below_ref, bf16[64,128,128]{2,1,0:T(8,128)(2,1)} %bitcast.81, ...), custom_call_target="tpu_custom_call" | custom-call | tf_op jit(solution)/shard_map/pallas_call | solution.py:127
  (46 shorter events, 0.6 us)
Async XLA Ops:
  53.0 9.4 %copy-start.3 = (bf16[2,128,128]{2,1,0:T(8,128)(2,1)S(1)}, bf16[2,128,128]{2,1,0:T(8,128)(2,1)}, u32[]{:S(2)}) copy-start(bf16[2,128,128]{2,1,0:T(8,128)(2,1)} %param.10) | copy-start | bytes 196612
  53.0 9.4 %copy-start.4 = (bf16[2,128,128]{2,1,0:T(8,128)(2,1)S(1)}, bf16[2,128,128]{2,1,0:T(8,128)(2,1)}, u32[]{:S(2)}) copy-start(bf16[2,128,128]{2,1,0:T(8,128)(2,1)} %param.8) | copy-start | bytes 196612
  53.0 55.3 %all-to-all-start = ((bf16[16,4,2,64,128]{4,3,2,1,0:T(8,128)(2,1)}), bf16[16,4,2,64,128]{4,3,2,1,0:T(8,128)(2,1)S(1)}, u32[]{:S(2)}, u32[]{:S(2)}) async-start(bf16[16,4,2,64,128]{4,3,2,1,0:T(8,128)(2,1)} %bitcast.77), calls=%async_computation | async-start | bytes 4194304 | tf_op jit(solution)/shard_map/all_to_all | solution.py:171
  61.3 1.1 copy-start.8
  61.6 0.9 copy-start.5
  111.1 4.6 %copy-start = (bf16[4,1,1,128,16,64]{3,5,2,4,1,0:T(8,128)(2,1)S(1)}, bf16[4,1,1,128,16,64]{3,5,2,4,1,0:T(8,128)(2,1)}, u32[]{:S(2)}) copy-start(bf16[4,1,1,128,16,64]{3,5,2,4,1,0:T(8,128)(2,1)} %get-tuple-element.19) | copy-start | bytes 3145732
  111.1 4.5 %copy-start.1 = (bf16[4,1,1,128,16,64]{3,5,2,4,1,0:T(8,128)(2,1)S(1)}, bf16[4,1,1,128,16,64]{3,5,2,4,1,0:T(8,128)(2,1)}, u32[]{:S(2)}) copy-start(bf16[4,1,1,128,16,64]{3,5,2,4,1,0:T(8,128)(2,1)} %get-tuple-element.20) | copy-start | bytes 3145732
  115.6 2.4 copy-start.6
  115.6 2.4 copy-start.9
  115.6 2.4 copy-start.10
  124.5 71.0 %all-to-all-start.1 = ((bf16[16,4,2,64,128]{4,1,3,2,0:T(4,128)(2,1)}), bf16[16,4,2,64,128]{4,1,3,2,0:T(4,128)(2,1)}, u32[]{:S(2)}, u32[]{:S(2)}) async-start(bf16[16,4,2,64,128]{4,1,3,2,0:T(4,128)(2,1)} %convert_bitcast_fusion), calls=%async_computation.1 | async-start | bytes 4194304 | tf_op jit(solution)/shard_map/all_to_all | solution.py:209
  131.5 53.0 %collective-permute-start.1 = (bf16[1,1920,128]{2,1,0:T(8,128)(2,1)S(1)}, bf16[1,1920,128]{2,1,0:T(8,128)(2,1)}, u32[]{:S(2)}, u32[]{:S(2)}) collective-permute-start(bf16[1,1920,128]{2,1,0:T(8,128)(2,1)S(1)} %get-tuple-element.9), channel_id=1, source_target_pairs={{2,0},{4,2},{6,4},{8,6},{10,8},{12,10},{14,12},{16,14},{18,16},{20... | collective-permute-start | bytes 1474568 | tf_op jit(solution)/shard_map/ppermute | solution.py:228
  135.8 13.5 %copy-start.2 = (bf16[1920,64,1]{0,1,2:T(8,128)(2,1)S(1)}, bf16[1920,64,1]{0,1,2:T(8,128)(2,1)}, u32[]{:S(2)}) copy-start(bf16[1920,64,1]{0,1,2:T(8,128)(2,1)} %get-tuple-element.28) | copy-start | bytes 737284
  135.8 13.6 %copy-start.7 = (f32[3,3,128]{2,1,0:T(4,128)S(1)}, f32[3,3,128]{2,1,0:T(4,128)}, u32[]{:S(2)}) copy-start(f32[3,3,128]{2,1,0:T(4,128)} %param.12) | copy-start | bytes 13828
  135.8 55.8 %collective-permute-start = (bf16[1,1920,128]{2,1,0:T(8,128)(2,1)}, bf16[1,1920,128]{2,1,0:T(8,128)(2,1)S(1)}, u32[]{:S(2)}, u32[]{:S(2)}) collective-permute-start(bf16[1,1920,128]{2,1,0:T(8,128)(2,1)} %get-tuple-element.10), channel_id=1, source_target_pairs={{0,2},{2,4},{4,6},{6,8},{8,10},{10,12},{12,14},{14,16},{16,18},{18... | collective-permute-start | bytes 1474568 | tf_op jit(solution)/shard_map/ppermute | solution.py:227
  184.5 7.1 %slice-start = ((s8[7372800]{0:T(1024)(128)(4,1)}), s8[4194304]{0:T(1024)(128)(4,1)S(1)}, s32[]{:S(2)}) async-start(s8[7372800]{0:T(1024)(128)(4,1)} %bitcast.79), calls=%async_computation.2 | async-start | bytes 8388608
  184.5 7.1 %slice-start.1 = ((s8[7372800]{0:T(1024)(128)(4,1)}), s8[3178496]{0:T(1024)(128)(4,1)S(1)}, s32[]{:S(2)}) async-start(s8[7372800]{0:T(1024)(128)(4,1)} %bitcast.79), calls=%async_computation.3 | async-start | bytes 6356992

commit v3 on v2

--- a/solution.py
+++ b/solution.py
@@ -77,43 +77,47 @@
     )(field, lon_t)
 
 
-def epilogue_kernel(taps_ref, above_ref, main_ref, below_ref, *refs):
+def epilogue_kernel(taps_ref, low_ref, high_ref, above_ref, main_ref, below_ref, *refs):
     out_ref = refs[-1]
     block_rows, width, _ = main_ref.shape
+    step = pl.program_id(0)
     taps = [taps_ref[pl.ds(i, 1), :] for i in range(9)]
+    first_row = jnp.where(step == 0, low_ref[0], above_ref[0]).astype(jnp.float32)
+    last_row = jnp.where(step == pl.num_programs(0) - 1, high_ref[0], below_ref[0])
+    last_row = last_row.astype(jnp.float32)
 
     def row(i):
         if i < 0:
-            return above_ref[0].astype(jnp.float32)
+            return first_row
         if i >= block_rows:
-            return below_ref[0].astype(jnp.float32)
+            return last_row
         return main_ref[i].astype(jnp.float32)
 
     for h in range(block_rows):
-        acc = None
-        for r in range(3):
-            x = row(h + r - 1)
-            left = pltpu.roll(x, 1, 0)
-            right = pltpu.roll(x, width - 1, 0)
-            term = taps[3 * r] * left + taps[3 * r + 1] * x + taps[3 * r + 2] * right
-            acc = term if acc is None else acc + term
+        xs = [row(h - 1), row(h), row(h + 1)]
+        cols = [taps[s] * xs[0] + taps[3 + s] * xs[1] + taps[6 + s] * xs[2] for s in range(3)]
+        stencil = pltpu.roll(cols[0], 1, 0) + cols[1] + pltpu.roll(cols[2], width - 1, 0)
         if len(refs) == 3:
             grid_ref, lon_ref = refs[0], refs[1]
             wave = jnp.dot(lon_ref[...], grid_ref[h], preferred_element_type=jnp.float32)
             wave = wave.astype(jnp.bfloat16)
         else:
             wave = refs[0][h]
-        out_ref[h] = ((row(h) + wave.astype(jnp.float32)) + acc).astype(jnp.bfloat16)
+        out_ref[h] = ((xs[1] + wave.astype(jnp.float32)) + stencil).astype(jnp.bfloat16)
 
 
 def epilogue(field, low, high, conv_kernel, wave_args):
     rows, width, channels = field.shape
     block_rows = math.gcd(rows, 4)
     count = rows // block_rows
-    above = jnp.concatenate([low, field[block_rows - 1 : rows - 1 : block_rows]], axis=0)
-    below = jnp.concatenate([field[block_rows::block_rows], high], axis=0)
     taps = conv_kernel.reshape(9, channels)
-    row_spec = pl.BlockSpec((1, width, channels), lambda i: (i, 0, 0))
+    halo_spec = pl.BlockSpec((1, width, channels), lambda i: (0, 0, 0))
+    above_spec = pl.BlockSpec(
+        (1, width, channels), lambda i: (jnp.maximum(i * block_rows - 1, 0), 0, 0)
+    )
+    below_spec = pl.BlockSpec(
+        (1, width, channels), lambda i: (jnp.minimum((i + 1) * block_rows, rows - 1), 0, 0)
+    )
     main_spec = pl.BlockSpec((block_rows, width, channels), lambda i: (i, 0, 0))
     if len(wave_args) == 2:
         grid_rows, lon_inv = wave_args
@@ -127,12 +131,13 @@
     return pl.pallas_call(
         epilogue_kernel,
         grid=(count,),
-        in_specs=[pl.BlockSpec((9, channels), lambda i: (0, 0)), row_spec, main_spec, row_spec]
+        in_specs=[pl.BlockSpec((9, channels), lambda i: (0, 0)), halo_spec, halo_spec]
+        + [above_spec, main_spec, below_spec]
         + wave_specs,
         out_specs=main_spec,
         out_shape=jax.ShapeDtypeStruct((rows, width, channels), jnp.bfloat16),
         compiler_params=pltpu.CompilerParams(dimension_semantics=("arbitrary",)),
-    )(taps, above, field, below, *wave_args)
+    )(taps, low, high, field, field, field, *wave_args)
 
 
 def on_device(field, w_first, b_first, w_second, b_second, conv_kernel, mode_plan):

time: 276 us -> 252 us (0.913)
  local copies, waits for them, and re-layouts: 33.2 us -> 20.7 us
  other arithmetic: 37.5 us -> 26.6 us
  waiting for transfers between devices: 57.1 us -> 67.1 us
  Pallas kernels: 113 us -> 105 us
    all_to_all x1, waiting for transfers between devices: 0.01 us -> 36.3 us  [on_device(): lax.all_to_all(inverse, ('lat', 'lon'), split_axis=0, concat_axis=0, tile...]
    ppermute x1, waiting for transfers between devices: 32.9 us -> 3.26 us  [on_device(): high = lax.ppermute(field[:1], ('lat', 'lon'), backward_pairs)]
    slice x1 -> x0, local copies, waits for them, and re-layouts: 11.2 us -> none  [epilogue(): below = jnp.concatenate([field[block_rows::block_rows], high], axis=0)]
    concatenate x2 -> x0, other arithmetic: 10.9 us -> none  [the longest x1 7.11 us: epilogue(): below = jnp.concatenate([field[block_rows::block_rows], high], axis=0)]
    pallas_call x1, Pallas kernels: 72.1 us -> 63.9 us  [epilogue(): pl.pallas_call(epilogue_kernel, grid=(count,), in_specs=[pl.BlockSpec((9,...]
    ppermute x1, waiting for transfers between devices: 0.01 us -> 3.28 us  [on_device(): low = lax.ppermute(field[rows - 1:], ('lat', 'lon'), forward_pairs)]
  transfers between devices with their start and end apart: 4 -> 4, of which waited for: 2 -> 4; matrix products, arithmetic and copies ran while one was open for 18% -> 13% of each run, Pallas kernels for 0% -> 0%
where the time goes in v3:
time: 252 us
  Pallas kernels  105 us (42%)
  waiting for transfers between devices  67.1 us (27%)
  other arithmetic  26.6 us (11%)
  local copies, waits for them, and re-layouts  20.7 us (8%)
  starting transfers between devices  18.8 us (7%)
  matrix products  13.7 us (5%)
    pallas_call x1, Pallas kernels, epilogue(): pl.pallas_call(epilogue_kernel, grid=(count,), in_specs=[pl.BlockSpec((9,...  63.9 us
    pallas_call x1, Pallas kernels, forward_rows(): pl.pallas_call(forward_kernel, grid=(rows // block_rows,), in_specs=[pl.B...  40.9 us
    all_to_all x1, waiting for transfers between devices, on_device(): lax.all_to_all(inverse, ('lat', 'lon'), split_axis=0, concat_axis=0, tile...  36.3 us
    all_to_all x1, waiting for transfers between devices, on_device(): lax.all_to_all(forward, ('lat', 'lon'), split_axis=0, concat_axis=0, tile...  24.2 us
    another operation x3, other arithmetic  24.1 us
    all_to_all x1, starting transfers between devices, on_device(): lax.all_to_all(forward, ('lat', 'lon'), split_axis=0, concat_axis=0, tile...  7.24 us
    dot_general x1, matrix products, on_device(): jnp.einsum('jk,skarc->sjarc', merge, partial, precision=lax.Precision.HIG...  6.41 us
    reshape x1, local copies, waits for them, and re-layouts, on_device(): forward = forward_rows(field, lon_t).reshape(rows, devs, slots, 2, channels)  5.35 us
  transfers between devices with their start and end apart: 4, of which 4 were waited for; matrix products, arithmetic and copies ran while one was open for 13% of the time, Pallas kernels for 0%

profile of v3, /device:TPU:16, one launch (start us, length us, event | category | flops | bytes accessed | tf_op | source)
XLA Modules:
  0.0 252.0 jit_solution(3067564667029630444)
XLA Ops:
  0.0 0.7 broadcast_compare_fusion.1
  0.7 0.7 maximum_shift-right-logical_fusion
  1.4 0.1 reshape.475
  1.6 0.1 add.180
  1.8 0.1 and.174
  1.9 0.1 div.26
  2.0 3.1 %multiply_convert_fusion.3 = (bf16[1920,64,1]{0,1,2:T(8,128)(2,1)S(1)}, bf16[1920,64,1]{0,1,2:T(8,128)(2,1)}, f32[1920,64,1]{0,1,2:T(8,128)S(1)}, f32[1920,64,1]{0,1,2:T(8,128)S(1)}) fusion(f32[64]{0:T(128)S(1)} %get-tuple-element.5, s32[64]{0:T(128)S(1)} %get-tuple-element.6, f32[64]{0:T(128)S(1)} %fusion.75), kind=kLoop, calls=%fused_computation.57 | loop fusion | flops 1720320 | bytes 1475328 | tf_op jit(solution)/shard_map/convert
  5.2 0.5 copy.55
  5.7 1.0 reshape.469.lon_ref
  6.7 40.9 %shard_map.73 = bf16[64,128,128]{2,1,0:T(8,128)(2,1)} custom-call(bf16[64,1920,128]{2,1,0:T(8,128)(2,1)} %below_ref.1, bf16[128,1920]{1,0:T(8,128)(2,1)} %reshape.469.lon_ref), custom_call_target="tpu_custom_call" | custom-call | tf_op jit(solution)/shard_map/pallas_call | solution.py:67
  47.6 5.4 %copy.85 = bf16[64,16,4,2,128]{4,0,3,2,1:T(8,128)(2,1)} copy(bf16[64,16,4,2,128]{4,3,2,1,0:T(2,128)(2,1)} %bitcast.80) | data formatting | bytes 4194304 | tf_op jit(solution)/shard_map/reshape | solution.py:166
  53.0 7.2 %all-to-all-start = ((bf16[16,4,2,64,128]{4,3,2,1,0:T(8,128)(2,1)}), bf16[16,4,2,64,128]{4,3,2,1,0:T(8,128)(2,1)S(1)}, u32[]{:S(2)}, u32[]{:S(2)}) async-start(bf16[16,4,2,64,128]{4,3,2,1,0:T(8,128)(2,1)} %bitcast.77), calls=%async_computation | async-start | bytes 4194304 | tf_op jit(solution)/shard_map/all_to_all | solution.py:176
  60.2 0.1 copy.61
  60.3 0.1 ge.17
  60.4 0.1 copy.52
  60.5 0.1 ge.19
  60.6 0.1 copy.60
  60.8 0.1 ne.200
  60.8 0.1 copy.57
  61.0 0.1 rem.97
  61.0 0.1 div.27
  61.1 0.2 dynamic-slice_reduce_fusion.1
  61.3 0.2 dynamic-slice_reduce_fusion
  61.6 0.2 fusion.62
  61.8 0.5 not_and_fusion
  62.4 0.6 slice_bitcast_fusion
  63.0 10.0 %negate_convert_fusion = (bf16[4,1,1,128,16,64]{3,5,2,4,1,0:T(8,128)(2,1)S(1)}, bf16[4,1,1,128,16,64]{3,5,2,4,1,0:T(8,128)(2,1)}, bf16[4,1,1,128,16,64]{3,5,2,4,1,0:T(8,128)(2,1)}) fusion(s32[16,64]{1,0:T(8,128)S(1)} %multiply_add_fusion, s32[4,128]{1,0:T(4,128)S(1)} %add_add_fusion), kind=kLoop, calls=%fused_computation.33 | loop fusion | flops 10485760 | bytes 3151872 | tf_op jit(solution)/shard_map/convert.7
  73.0 11.0 %fusion.24 = (bf16[4,1,128,1,16,64]{2,5,3,1,0,4:T(8,128)(2,1)}, bf16[4,1,128,1,16,64]{2,5,3,1,0,4:T(8,128)(2,1)}, bf16[4,1,128,1,16,64]{2,5,3,1,0,4:T(8,128)(2,1)}) fusion(s32[16,64]{1,0:T(8,128)S(1)} %multiply_add_fusion, s32[4,128]{1,0:T(4,128)S(1)} %add_add_fusion), kind=kLoop, calls=%fused_computation.39 | loop fusion | flops 10485760 | bytes 3151872 | tf_op jit(solution)/shard_map/convert.13
  84.0 24.2 %all-to-all-done = bf16[16,4,2,64,128]{4,3,2,1,0:T(8,128)(2,1)S(1)} async-done(((bf16[16,4,2,64,128]{4,3,2,1,0:T(8,128)(2,1)}), bf16[16,4,2,64,128]{4,3,2,1,0:T(8,128)(2,1)S(1)}, u32[]{:S(2)}, u32[]{:S(2)}) %all-to-all-start) | async-done | bytes 2097184 | tf_op jit(solution)/shard_map/all_to_all | solution.py:176
  108.2 2.8 %fusion.8 = bf16[4,128,2,128,1,1]{3,1,4,0,2,5:T(8,128)(2,1)S(1)} fusion(bf16[16,4,2,64,128]{4,3,2,1,0:T(8,128)(2,1)S(1)} %all-to-all-done, bf16[4,1,128,1,16,64]{2,5,3,1,0,4:T(8,128)(2,1)} %get-tuple-element.15, bf16[4,1,128,1,16,64]{2,5,3,1,0,4:T(8,128)(2,1)} %get-tuple-element.14, bf16[4,1,128,1,16,64]{2,5,3,1,0,4:T(8,128)(2,1)} %get-tuple-element.13), kind=kOutput, calls=%fused_computation.9 | convolution fusion | flops 543162368 | bytes 5505024 | tf_op jit(solution)/shard_map/joqasr,sjarc->jqoc/dot_general | solution.py:187
  111.1 0.7 copy.86
  111.8 2.1 fusion.30
  113.9 1.7 reshape.472
  115.6 2.4 fusion.12
  118.1 6.4 %convert_bitcast_fusion = bf16[16,4,2,64,128]{4,1,3,2,0:T(4,128)(2,1)} fusion(f32[16,4,2,64,128]{4,3,0,2,1:T(8,128)S(1)} %fusion.12, s32[4]{0:T(128)S(1)} %copy-done.6, pred[4]{0:T(512)(128)(4,1)S(1)} %copy-done.10, pred[4]{0:T(512)(128)(4,1)S(1)} %copy-done.9), kind=kOutput, calls=%fused_computation.32 | convolution fusion | flops 51380272 | bytes 6291480 | tf_op jit(solution)/shard_map/jk,skarc->sjarc/dot_general | solution.py:209
  124.5 5.1 %all-to-all-start.1 = ((bf16[16,4,2,64,128]{4,1,3,2,0:T(4,128)(2,1)}), bf16[16,4,2,64,128]{4,1,3,2,0:T(4,128)(2,1)S(1)}, u32[]{:S(2)}, u32[]{:S(2)}) async-start(bf16[16,4,2,64,128]{4,1,3,2,0:T(4,128)(2,1)} %convert_bitcast_fusion), calls=%async_computation.1 | async-start | bytes 4194304 | tf_op jit(solution)/shard_map/all_to_all | solution.py:214
  129.6 2.2 fusion.79
  131.8 4.3 %collective-permute-start.1 = (bf16[1,1920,128]{2,1,0:T(8,128)(2,1)}, bf16[1,1920,128]{2,1,0:T(8,128)(2,1)}, u32[]{:S(2)}, u32[]{:S(2)}) collective-permute-start(bf16[1,1920,128]{2,1,0:T(8,128)(2,1)} %get-tuple-element.7), channel_id=1, source_target_pairs={{2,0},{4,2},{6,4},{8,6},{10,8},{12,10},{14,12},{16,14},{18,16},{20... | collective-permute-start | bytes 1474568 | tf_op jit(solution)/shard_map/ppermute | solution.py:233
  136.1 2.1 collective-permute-start
  138.2 0.6 reshape.468.taps_ref
  138.9 0.5 copy.64
  139.4 0.2 convert_element_type.107
  139.6 1.0 copy.65.refs_1_
  140.6 36.3 %all-to-all-done.1 = bf16[16,4,2,64,128]{4,1,3,2,0:T(4,128)(2,1)S(1)} async-done(((bf16[16,4,2,64,128]{4,1,3,2,0:T(4,128)(2,1)}), bf16[16,4,2,64,128]{4,1,3,2,0:T(4,128)(2,1)S(1)}, u32[]{:S(2)}, u32[]{:S(2)}) %all-to-all-start.1) | async-done | bytes 2097184 | tf_op jit(solution)/shard_map/all_to_all | solution.py:214
  177.0 4.6 %copy.63 = bf16[64,16,4,2,128]{4,3,2,1,0:T(2,128)(2,1)} copy(bf16[64,16,4,2,128]{4,2,0,3,1:T(4,128)(2,1)S(1)} %bitcast.81) | data formatting | bytes 4194304 | tf_op jit(solution)/shard_map/transpose | solution.py:222
  181.5 3.3 %collective-permute-done.1.high_ref = bf16[1,1920,128]{2,1,0:T(8,128)(2,1)} collective-permute-done((bf16[1,1920,128]{2,1,0:T(8,128)(2,1)}, bf16[1,1920,128]{2,1,0:T(8,128)(2,1)}, u32[]{:S(2)}, u32[]{:S(2)}) %collective-permute-start.1) | collective-permute-done | bytes 491552 | tf_op jit(solution)/shard_map/ppermute | solution.py:233
  184.8 3.3 %collective-permute-done.low_ref = bf16[1,1920,128]{2,1,0:T(8,128)(2,1)} collective-permute-done((bf16[1,1920,128]{2,1,0:T(8,128)(2,1)}, bf16[1,1920,128]{2,1,0:T(8,128)(2,1)}, u32[]{:S(2)}, u32[]{:S(2)}) %collective-permute-start) | collective-permute-done | bytes 491552 | tf_op jit(solution)/shard_map/ppermute | solution.py:232
  188.1 63.9 %shard_map.74 = bf16[64,1920,128]{2,1,0:T(8,128)(2,1)} custom-call(f32[9,128]{1,0:T(8,128)} %reshape.468.taps_ref, bf16[1,1920,128]{2,1,0:T(8,128)(2,1)} %collective-permute-done.low_ref, bf16[1,1920,128]{2,1,0:T(8,128)(2,1)} %collective-permute-done.1.high_ref, bf16[64,1920,128]{2,1,0:T(8,128)(2,1)} %below_ref.1, bf16[64,1920,128]{2,1,0:T(8,128)(2,1)} %below_ref.1, ...), custom_call_target="tpu_custom_call" | custom-call | tf_op jit(solution)/shard_map/pallas_call | solution.py:131
  (38 shorter events, 0.6 us)
Async XLA Ops:
  53.0 9.4 %copy-start.3 = (bf16[2,128,128]{2,1,0:T(8,128)(2,1)S(1)}, bf16[2,128,128]{2,1,0:T(8,128)(2,1)}, u32[]{:S(2)}) copy-start(bf16[2,128,128]{2,1,0:T(8,128)(2,1)} %param.10) | copy-start | bytes 196612
  53.0 9.4 %copy-start.4 = (bf16[2,128,128]{2,1,0:T(8,128)(2,1)S(1)}, bf16[2,128,128]{2,1,0:T(8,128)(2,1)}, u32[]{:S(2)}) copy-start(bf16[2,128,128]{2,1,0:T(8,128)(2,1)} %param.8) | copy-start | bytes 196612
  53.0 55.3 %all-to-all-start = ((bf16[16,4,2,64,128]{4,3,2,1,0:T(8,128)(2,1)}), bf16[16,4,2,64,128]{4,3,2,1,0:T(8,128)(2,1)S(1)}, u32[]{:S(2)}, u32[]{:S(2)}) async-start(bf16[16,4,2,64,128]{4,3,2,1,0:T(8,128)(2,1)} %bitcast.77), calls=%async_computation | async-start | bytes 4194304 | tf_op jit(solution)/shard_map/all_to_all | solution.py:176
  61.3 1.1 copy-start.8
  61.6 0.9 copy-start.5
  111.1 4.6 %copy-start = (bf16[4,1,1,128,16,64]{3,5,2,4,1,0:T(8,128)(2,1)S(1)}, bf16[4,1,1,128,16,64]{3,5,2,4,1,0:T(8,128)(2,1)}, u32[]{:S(2)}) copy-start(bf16[4,1,1,128,16,64]{3,5,2,4,1,0:T(8,128)(2,1)} %get-tuple-element.17) | copy-start | bytes 3145732
  111.1 4.6 %copy-start.1 = (bf16[4,1,1,128,16,64]{3,5,2,4,1,0:T(8,128)(2,1)S(1)}, bf16[4,1,1,128,16,64]{3,5,2,4,1,0:T(8,128)(2,1)}, u32[]{:S(2)}) copy-start(bf16[4,1,1,128,16,64]{3,5,2,4,1,0:T(8,128)(2,1)} %get-tuple-element.18) | copy-start | bytes 3145732
  115.6 2.4 copy-start.6
  115.6 2.4 copy-start.9
  115.6 2.4 copy-start.10
  124.5 13.8 %copy-start.7 = (f32[3,3,128]{2,1,0:T(4,128)S(1)}, f32[3,3,128]{2,1,0:T(4,128)}, u32[]{:S(2)}) copy-start(f32[3,3,128]{2,1,0:T(4,128)} %param.12) | copy-start | bytes 13828
  124.5 14.4 %copy-start.2 = (bf16[1920,64,1]{0,1,2:T(8,128)(2,1)S(1)}, bf16[1920,64,1]{0,1,2:T(8,128)(2,1)}, u32[]{:S(2)}) copy-start(bf16[1920,64,1]{0,1,2:T(8,128)(2,1)} %get-tuple-element.26) | copy-start | bytes 737284
  124.5 52.5 %all-to-all-start.1 = ((bf16[16,4,2,64,128]{4,1,3,2,0:T(4,128)(2,1)}), bf16[16,4,2,64,128]{4,1,3,2,0:T(4,128)(2,1)S(1)}, u32[]{:S(2)}, u32[]{:S(2)}) async-start(bf16[16,4,2,64,128]{4,1,3,2,0:T(4,128)(2,1)} %convert_bitcast_fusion), calls=%async_computation.1 | async-start | bytes 4194304 | tf_op jit(solution)/shard_map/all_to_all | solution.py:214
  131.8 53.0 %collective-permute-start.1 = (bf16[1,1920,128]{2,1,0:T(8,128)(2,1)}, bf16[1,1920,128]{2,1,0:T(8,128)(2,1)}, u32[]{:S(2)}, u32[]{:S(2)}) collective-permute-start(bf16[1,1920,128]{2,1,0:T(8,128)(2,1)} %get-tuple-element.7), channel_id=1, source_target_pairs={{2,0},{4,2},{6,4},{8,6},{10,8},{12,10},{14,12},{16,14},{18,16},{20... | collective-permute-start | bytes 1474568 | tf_op jit(solution)/shard_map/ppermute | solution.py:233
  136.1 52.0 %collective-permute-start = (bf16[1,1920,128]{2,1,0:T(8,128)(2,1)}, bf16[1,1920,128]{2,1,0:T(8,128)(2,1)}, u32[]{:S(2)}, u32[]{:S(2)}) collective-permute-start(bf16[1,1920,128]{2,1,0:T(8,128)(2,1)} %get-tuple-element.8), channel_id=1, source_target_pairs={{0,2},{2,4},{4,6},{6,8},{8,10},{10,12},{12,14},{14,16},{16,18},{18... | collective-permute-start | bytes 1474568 | tf_op jit(solution)/shard_map/ppermute | solution.py:232

commit v4 on v3

v4 whole, which is shorter than its diff:
```python
import math

import jax
import jax.numpy as jnp
from jax import lax
from jax.experimental import pallas as pl
from jax.experimental.pallas import tpu as pltpu
from jax.sharding import PartitionSpec as P

H = 1024
W = 1920
KH = 512
KW = 512
MB = 128


shrink_level = 0.01


def complexify(weights):
    real_part = weights[0]
    imag_part = weights[1]
    top_rows = jnp.concatenate([real_part, imag_part], axis=1)
    low_rows = jnp.concatenate([-imag_part, real_part], axis=1)
    return jnp.concatenate([top_rows, low_rows], axis=0)


def spectral_mlp(modes, first_mat, first_bias, second_mat, second_bias):
    hidden = jnp.einsum("tmc,cd->tmd", modes, first_mat, preferred_element_type=jnp.float32)
    hidden = jax.nn.relu(hidden + first_bias.reshape(-1)).astype(jnp.bfloat16)
    second_out = jnp.einsum("tmc,cd->tmd", hidden, second_mat, preferred_element_type=jnp.float32)
    second_out = second_out + second_bias.reshape(-1)
    return second_out - jnp.clip(second_out, -shrink_level, shrink_level)


def lon_angles(modes, width):
    columns = jnp.arange(width, dtype=jnp.int32)[:, None]
    phases = columns * modes[None, :] % width
    return phases.astype(jnp.float32) * (2.0 * math.pi / width)


def lat_trig(lat_modes, height):
    freqs = lat_modes - KH // 2
    rowids = jnp.arange(height, dtype=jnp.int32)
    phases = jnp.mod(freqs[..., None] * rowids, height)
    angles = phases.astype(jnp.float32) * (2.0 * math.pi / height)
    factor = 1.0 / math.sqrt(height)
    return jnp.cos(angles) * factor, jnp.sin(angles) * factor


def forward_kernel(field_ref, lon_ref, out_ref):
    block_rows, _, channels = field_ref.shape
    lon = lon_ref[...]
    for h in range(block_rows):
        x = field_ref[h].astype(jnp.float32)
        average = jnp.sum(x, axis=1, keepdims=True) * (1.0 / channels)
        centred = x - average
        spread = jnp.sum(centred * centred, axis=1, keepdims=True) * (1.0 / channels)
        normed = (centred * lax.rsqrt(spread + 1e-05)).astype(jnp.bfloat16)
        out_ref[h] = jnp.dot(lon, normed, preferred_element_type=jnp.float32).astype(jnp.bfloat16)


def forward_rows(field, lon_t, start, count):
    _, width, channels = field.shape
    n = lon_t.shape[0]
    block_rows = math.gcd(count, 4)
    offset = start // block_rows
    return pl.pallas_call(
        forward_kernel,
        grid=(count // block_rows,),
        in_specs=[
            pl.BlockSpec((block_rows, width, channels), lambda i: (i + offset, 0, 0)),
            pl.BlockSpec((n, width), lambda i: (0, 0)),
        ],
        out_specs=pl.BlockSpec((block_rows, n, channels), lambda i: (i, 0, 0)),
        out_shape=jax.ShapeDtypeStruct((count, n, channels), jnp.bfloat16),
        compiler_params=pltpu.CompilerParams(dimension_semantics=("arbitrary",)),
    )(field, lon_t)


def make_epilogue_kernel(in_wave, first_block, last_block):
    def kernel(taps_ref, low_ref, high_ref, above_ref, main_ref, below_ref, *refs):
        out_ref = refs[-1]
        block_rows, width, _ = main_ref.shape
        step = pl.program_id(0) + first_block
        taps = [taps_ref[pl.ds(i, 1), :] for i in range(9)]
        first_row = jnp.where(step == 0, low_ref[0], above_ref[0]).astype(jnp.float32)
        last_row = jnp.where(step == last_block, high_ref[0], below_ref[0])
        last_row = last_row.astype(jnp.float32)

        def row(i):
            if i < 0:
                return first_row
            if i >= block_rows:
                return last_row
            return main_ref[i].astype(jnp.float32)

        for h in range(block_rows):
            xs = [row(h - 1), row(h), row(h + 1)]
            cols = [taps[s] * xs[0] + taps[3 + s] * xs[1] + taps[6 + s] * xs[2] for s in range(3)]
            stencil = pltpu.roll(cols[0], 1, 0) + cols[1] + pltpu.roll(cols[2], width - 1, 0)
            if in_wave:
                grid_ref, lon_ref = refs[0], refs[1]
                wave = jnp.dot(lon_ref[...], grid_ref[h], preferred_element_type=jnp.float32)
                wave = wave.astype(jnp.bfloat16)
            else:
                wave = refs[0][h]
            out_ref[h] = ((xs[1] + wave.astype(jnp.float32)) + stencil).astype(jnp.bfloat16)

    return kernel


def epilogue(field, low, high, conv_kernel, wave_args, start, count, prior):
    rows, width, channels = field.shape
    block_rows = math.gcd(count, 4)
    offset = start // block_rows
    taps = conv_kernel.reshape(9, channels)
    halo_spec = pl.BlockSpec((1, width, channels), lambda i: (0, 0, 0))
    above_spec = pl.BlockSpec(
        (1, width, channels), lambda i: (jnp.maximum((i + offset) * block_rows - 1, 0), 0, 0)
    )
    below_spec = pl.BlockSpec(
        (1, width, channels),
        lambda i: (jnp.minimum((i + offset + 1) * block_rows, rows - 1), 0, 0),
    )
    main_spec = pl.BlockSpec((block_rows, width, channels), lambda i: (i + offset, 0, 0))
    in_wave = len(wave_args) == 2
    if in_wave:
        grid_rows, lon_inv = wave_args
        n = grid_rows.shape[1]
        wave_specs = [
            pl.BlockSpec((block_rows, n, channels), lambda i: (i, 0, 0)),
            pl.BlockSpec((width, n), lambda i: (0, 0)),
        ]
    else:
        wave_specs = [pl.BlockSpec((block_rows, width, channels), lambda i: (i, 0, 0))]
    operands = [taps, low, high, field, field, field, *wave_args]
    specs = [pl.BlockSpec((9, channels), lambda i: (0, 0)), halo_spec, halo_spec]
    specs += [above_spec, main_spec, below_spec] + wave_specs
    aliases = {}
    if prior is not None:
        aliases = {len(operands): 0}
        operands.append(prior)
        specs.append(pl.BlockSpec(memory_space=pl.ANY))
    kernel = make_epilogue_kernel(in_wave, offset, rows // block_rows - 1)
    return pl.pallas_call(
        kernel,
        grid=(count // block_rows,),
        in_specs=specs,
        out_specs=main_spec,
        out_shape=jax.ShapeDtypeStruct((rows, width, channels), jnp.bfloat16),
        input_output_aliases=aliases,
        compiler_params=pltpu.CompilerParams(dimension_semantics=("arbitrary",)),
    )(*operands)


def on_device(field, w_first, b_first, w_second, b_second, conv_kernel, mode_plan):
    rows, width, channels = field.shape
    lat_count = lax.axis_size("lat")
    lon_count = lax.axis_size("lon")
    devs = lat_count * lon_count
    per_device = KW // devs
    blocks = KH // MB
    slots = mode_plan.shape[0] // lat_count
    height = rows * devs
    me = lax.axis_index("lat") * lon_count + lax.axis_index("lon")
    n = devs * slots * 2
    chunks = 2 if rows % 8 == 0 else 1
    part = rows // chunks

    plan = mode_plan.reshape(lat_count, slots, lon_count).transpose(0, 2, 1).reshape(devs, slots)
    valid = plan >= 0
    tile = jnp.maximum(plan, 0)
    local_mode = tile // blocks
    lat_block = tile % blocks
    modes = jnp.arange(devs, dtype=jnp.int32)[:, None] * per_device + local_mode

    angles = lon_angles(modes.reshape(-1), width)
    factor = 1.0 / math.sqrt(width)
    lon_sub = (jnp.stack([jnp.cos(angles), -jnp.sin(angles)], axis=-1) * factor).astype(jnp.bfloat16)
    pencils = []
    if n <= 512:
        lon_t = jnp.transpose(lon_sub, (1, 2, 0)).reshape(n, width)
        for c in range(chunks):
            forward = forward_rows(field, lon_t, c * part, part)
            forward = forward.reshape(part, devs, slots, 2, channels)
            forward = jnp.transpose(forward, (1, 2, 3, 0, 4))
            pencils.append(
                lax.all_to_all(forward, ("lat", "lon"), split_axis=0, concat_axis=0, tiled=True)
            )
    else:
        values = field.astype(jnp.float32)
        average = jnp.mean(values, axis=-1, keepdims=True)
        centred = values - average
        spread = jnp.mean(centred * centred, axis=-1, keepdims=True)
        normed = (centred * lax.rsqrt(spread + 1e-05)).astype(jnp.bfloat16)
        forward = jnp.einsum("hwc,wna->nahc", normed, lon_sub, preferred_element_type=jnp.float32)
        forward = forward.astype(jnp.bfloat16).reshape(devs, slots, 2, rows, channels)
        chunks, part = 1, rows
        pencils.append(
            lax.all_to_all(forward, ("lat", "lon"), split_axis=0, concat_axis=0, tiled=True)
        )

    my_block = lax.dynamic_index_in_dim(lat_block, me, 0, keepdims=False)
    my_valid = lax.dynamic_index_in_dim(valid, me, 0, keepdims=False)
    my_mode = lax.dynamic_index_in_dim(local_mode, me, 0, keepdims=False)
    lat_modes = my_block[:, None] * MB + jnp.arange(MB, dtype=jnp.int32)[None, :]
    cosine, sine = lat_trig(lat_modes, height)
    lat_fwd = jnp.stack(
        [jnp.stack([cosine, sine], axis=2), jnp.stack([-sine, cosine], axis=2)], axis=1
    ).astype(jnp.bfloat16)
    lat_fwd = lat_fwd.reshape(slots, 2, MB, 2, devs, rows)
    spectrum = None
    for c in range(chunks):
        term = jnp.einsum(
            "joqasr,sjarc->jqoc",
            lat_fwd[..., c * part : (c + 1) * part],
            pencils[c],
            preferred_element_type=jnp.float32,
        )
        spectrum = term if spectrum is None else spectrum + term
    tiles = spectrum.astype(jnp.bfloat16).reshape(slots, MB, 2 * channels)

    first_mat = complexify(w_first)
    second_mat = complexify(w_second)
    shrunk = spectral_mlp(tiles, first_mat, b_first, second_mat, b_second)
    filtered = jnp.where(my_valid[:, None, None], shrunk, 0.0).astype(jnp.bfloat16)
    filtered = filtered.reshape(slots, MB, 2, channels)

    lat_inv = jnp.stack(
        [jnp.stack([cosine, -sine], axis=1), jnp.stack([sine, cosine], axis=1)], axis=1
    ).astype(jnp.bfloat16)
    lat_inv = lat_inv.reshape(slots, 2, 2, MB, devs, rows)
    same = (my_mode[:, None] == my_mode[None, :]) & my_valid[None, :]
    earlier = jnp.tril(jnp.ones((slots, slots), jnp.bool_), -1)
    first = my_valid & ~jnp.any(same & earlier, axis=1)
    merge = (same & first[:, None]).astype(jnp.float32)

    inv_angles = lon_angles(modes.reshape(-1), width)
    weights = jnp.where(modes.reshape(-1) == 0, 1.0, 2.0).astype(jnp.float32) / math.sqrt(width)
    lon_inv = jnp.stack(
        [weights * jnp.cos(inv_angles), -weights * jnp.sin(inv_angles)], axis=-1
    ).astype(jnp.bfloat16)
    lon_inv = lon_inv.reshape(width, n)

    forward_pairs = [(i, i + 1) for i in range(devs - 1)]
    backward_pairs = [(t, s) for s, t in forward_pairs]
    low = lax.ppermute(field[rows - 1 :], ("lat", "lon"), forward_pairs)
    high = lax.ppermute(field[:1], ("lat", "lon"), backward_pairs)

    partial = jnp.einsum(
        "jabqsr,jqbc->sjarc", lat_inv, filtered, preferred_element_type=jnp.float32
    )
    combined = jnp.einsum(
        "jk,skarc->sjarc", merge, partial, precision=lax.Precision.HIGHEST,
        preferred_element_type=jnp.float32,
    )
    inverse = combined.astype(jnp.bfloat16)
    rowwise = lax.all_to_all(inverse, ("lat", "lon"), split_axis=0, concat_axis=0, tiled=True)
    grid_rows = jnp.transpose(rowwise, (3, 0, 1, 2, 4)).reshape(rows, n, channels)
    if n <= 512:
        wave_args = (grid_rows, lon_inv)
    else:
        wave = jnp.einsum("rnc,wn->rwc", grid_rows, lon_inv, preferred_element_type=jnp.float32)
        wave_args = (wave.astype(jnp.bfloat16),)
    return epilogue(field, low, high, conv_kernel, wave_args, 0, rows, None)


def solution(mesh):
    placed = (P(("ens", "lat", "lon"), None, None), P(), P(), P(), P(), P(), P())
    return jax.shard_map(
        on_device,
        mesh=mesh,
        in_specs=placed,
        out_specs=P(("ens", "lat", "lon"), None, None),
        check_vma=False,
    )
```

time: 252 us -> 242 us (0.960)
  waiting for transfers between devices: 67.1 us -> 43.7 us
  starting transfers between devices: 18.8 us -> 26.4 us
    all_to_all x1 -> x2, waiting for transfers between devices: 24.2 us -> 1.07 us  [on_device(): lax.all_to_all(forward, ('lat', 'lon'), split_axis=0, concat_axis=0, tile...]
    all_to_all x1 -> x2, starting transfers between devices: 7.24 us -> 14 us  [on_device(): lax.all_to_all(forward, ('lat', 'lon'), split_axis=0, concat_axis=0, tile...]
    pallas_call x2 -> x3, Pallas kernels: 105 us -> 107 us  [the longest x1 63.9 us: epilogue(): pl.pallas_call(kernel, grid=(count // block_rows,), in_specs=specs, out_s...]
    reshape x2 -> x3, local copies, waits for them, and re-layouts: 6.32 us -> 7.84 us  [the longest x2 6.87 us: on_device(): forward = forward.reshape(part, devs, slots, 2, channels)]
    another operation x3 -> x4, other arithmetic: 24.1 us -> 23.7 us
  transfers between devices with their start and end apart: 4 -> 5, of which waited for: 4 -> 4; matrix products, arithmetic and copies ran while one was open for 13% -> 16% of each run, Pallas kernels for 0% -> 9%
where the time goes in v4:
time: 242 us; the launch traced here: 241 us
  Pallas kernels  107 us (44%)
  waiting for transfers between devices  43.7 us (18%)
  other arithmetic  27 us (11%)
  starting transfers between devices  26.4 us (11%)
  local copies, waits for them, and re-layouts  22.3 us (9%)
  matrix products  14.4 us (6%)
    pallas_call x1, Pallas kernels, epilogue(): pl.pallas_call(kernel, grid=(count // block_rows,), in_specs=specs, out_s...  63.9 us
    pallas_call x2, Pallas kernels, forward_rows(): pl.pallas_call(forward_kernel, grid=(count // block_rows,), in_specs=[pl....  43.2 us
    all_to_all x1, waiting for transfers between devices, on_device(): lax.all_to_all(inverse, ('lat', 'lon'), split_axis=0, concat_axis=0, tile...  35.8 us
    another operation x3, other arithmetic  23.4 us
    all_to_all x2, starting transfers between devices, on_device(): lax.all_to_all(forward, ('lat', 'lon'), split_axis=0, concat_axis=0, tile...  14 us
    reshape x2, local copies, waits for them, and re-layouts, on_device(): forward = forward.reshape(part, devs, slots, 2, channels)  6.87 us
    dot_general x1, matrix products, on_device(): jnp.einsum('jk,skarc->sjarc', merge, partial, precision=lax.Precision.HIG...  6.41 us
    all_to_all x1, starting transfers between devices, on_device(): lax.all_to_all(inverse, ('lat', 'lon'), split_axis=0, concat_axis=0, tile...  5.98 us
  transfers between devices with their start and end apart: 5, of which 4 were waited for; matrix products, arithmetic and copies ran while one was open for 16% of the time, Pallas kernels for 9%

profile of v4, /device:TPU:16, one launch (start us, length us, event | category | flops | bytes accessed | tf_op | source)
XLA Modules:
  0.0 241.3 jit_solution(7774733092709175075)
XLA Ops:
  0.0 0.7 broadcast_compare_fusion.1
  0.7 0.7 maximum_shift-right-logical_fusion
  1.6 0.1 add.184
  1.8 0.1 and.174
  1.9 0.1 div.26
  2.0 3.1 %multiply_convert_fusion.3 = (bf16[1920,64,1]{0,1,2:T(8,128)(2,1)S(1)}, bf16[1920,64,1]{0,1,2:T(8,128)(2,1)}, f32[1920,64,1]{0,1,2:T(8,128)S(1)}, f32[1920,64,1]{0,1,2:T(8,128)S(1)}) fusion(f32[64]{0:T(128)S(1)} %get-tuple-element.5, s32[64]{0:T(128)S(1)} %get-tuple-element.6, f32[64]{0:T(128)S(1)} %fusion.79), kind=kLoop, calls=%fused_computation.62 | loop fusion | flops 1720320 | bytes 1475328 | tf_op jit(solution)/shard_map/convert
  5.2 0.5 copy.60
  5.7 1.0 reshape.472.lon_ref
  6.7 21.6 %shard_map.74 = bf16[32,128,128]{2,1,0:T(8,128)(2,1)} custom-call(bf16[64,1920,128]{2,1,0:T(8,128)(2,1)} %below_ref.1, bf16[128,1920]{1,0:T(8,128)(2,1)} %reshape.472.lon_ref), custom_call_target="tpu_custom_call" | custom-call | tf_op jit(solution)/shard_map/pallas_call | solution.py:68
  28.3 3.4 %copy.98 = bf16[32,16,4,2,128]{4,0,3,2,1:T(8,128)(2,1)} copy(bf16[32,16,4,2,128]{4,3,2,1,0:T(2,128)(2,1)} %bitcast.94) | data formatting | bytes 2097152 | tf_op jit(solution)/shard_map/reshape | solution.py:186
  31.7 7.1 %all-to-all-start.1 = ((bf16[16,4,2,32,128]{4,3,2,1,0:T(8,128)(2,1)}), bf16[16,4,2,32,128]{4,3,2,1,0:T(8,128)(2,1)S(1)}, u32[]{:S(2)}, u32[]{:S(2)}) async-start(bf16[16,4,2,32,128]{4,3,2,1,0:T(8,128)(2,1)} %bitcast.89), calls=%async_computation.1 | async-start | bytes 2097152 | tf_op jit(solution)/shard_map/all_to_all | solution.py:189
  38.9 0.1 copy.67
  39.0 21.6 %shard_map.73 = bf16[32,128,128]{2,1,0:T(8,128)(2,1)} custom-call(bf16[64,1920,128]{2,1,0:T(8,128)(2,1)} %below_ref.1, bf16[128,1920]{1,0:T(8,128)(2,1)} %reshape.472.lon_ref), custom_call_target="tpu_custom_call" | custom-call | tf_op jit(solution)/shard_map/pallas_call | solution.py:68
  60.6 0.1 copy.57
  60.9 0.1 copy.66
  61.1 0.1 copy.62
  61.4 3.4 %copy.99 = bf16[32,16,4,2,128]{4,0,3,2,1:T(8,128)(2,1)} copy(bf16[32,16,4,2,128]{4,3,2,1,0:T(2,128)(2,1)} %bitcast.93) | data formatting | bytes 2097152 | tf_op jit(solution)/shard_map/reshape | solution.py:186
  64.8 0.2 dynamic-slice_reduce_fusion.1
  65.0 0.2 dynamic-slice_reduce_fusion
  65.2 0.2 fusion.66
  65.4 0.5 not_and_fusion
  66.1 0.6 slice_bitcast_fusion
  66.7 6.9 %all-to-all-start = ((bf16[16,4,2,32,128]{4,3,2,1,0:T(8,128)(2,1)}), bf16[16,4,2,32,128]{4,3,2,1,0:T(8,128)(2,1)}, u32[]{:S(2)}, u32[]{:S(2)}) async-start(bf16[16,4,2,32,128]{4,3,2,1,0:T(8,128)(2,1)} %bitcast.90), calls=%async_computation | async-start | bytes 2097152 | tf_op jit(solution)/shard_map/all_to_all | solution.py:189
  73.6 9.3 %fusion.25 = (bf16[4,1,128,1,16,64]{2,5,3,1,0,4:T(8,128)(2,1)S(1)}, bf16[4,1,128,1,16,64]{2,5,3,1,0,4:T(8,128)(2,1)S(1)}, bf16[4,1,128,1,16,64]{2,5,3,1,0,4:T(8,128)(2,1)S(1)}) fusion(s32[16,64]{1,0:T(8,128)S(1)} %multiply_add_fusion, s32[4,128]{1,0:T(4,128)S(1)} %add_add_fusion), kind=kLoop, calls=%fused_computation.39 | loop fusion | flops 10485760 | bytes 3151872 | tf_op jit(solution)/shard_map/convert.13
  82.9 0.4 maximum_maximum_fusion
  83.3 0.9 fusion.84
  84.2 11.0 %negate_convert_fusion = (bf16[4,1,1,128,16,64]{3,5,2,4,1,0:T(8,128)(2,1)}, bf16[4,1,1,128,16,64]{3,5,2,4,1,0:T(8,128)(2,1)}, bf16[4,1,1,128,16,64]{3,5,2,4,1,0:T(8,128)(2,1)}) fusion(s32[16,64]{1,0:T(8,128)S(1)} %multiply_add_fusion, s32[4,128]{1,0:T(4,128)S(1)} %copy-done.8), kind=kLoop, calls=%fused_computation.33 | loop fusion | flops 10485760 | bytes 3151872 | tf_op jit(solution)/shard_map/convert.7
  95.2 1.4 fusion.19
  96.6 1.1 all-to-all-done
  97.6 1.8 fusion.21
  99.5 0.8 fusion.34
  100.3 2.4 fusion.33
  102.7 1.7 reshape.476
  104.4 2.4 fusion.10
  106.8 6.4 %convert_bitcast_fusion = bf16[16,4,2,64,128]{4,1,3,2,0:T(4,128)(2,1)} fusion(f32[16,4,2,64,128]{4,3,0,2,1:T(8,128)S(1)} %fusion.10, s32[4]{0:T(128)S(1)} %copy-done.10, pred[4]{0:T(512)(128)(4,1)S(1)} %copy-done.14, pred[4]{0:T(512)(128)(4,1)S(1)} %copy-done.13), kind=kOutput, calls=%fused_computation.32 | convolution fusion | flops 51380272 | bytes 6291480 | tf_op jit(solution)/shard_map/jk,skarc->sjarc/dot_general | solution.py:254
  113.3 6.0 %all-to-all-start.2 = ((bf16[16,4,2,64,128]{4,1,3,2,0:T(4,128)(2,1)}), bf16[16,4,2,64,128]{4,1,3,2,0:T(4,128)(2,1)S(1)}, u32[]{:S(2)}, u32[]{:S(2)}) async-start(bf16[16,4,2,64,128]{4,1,3,2,0:T(4,128)(2,1)} %convert_bitcast_fusion), calls=%async_computation.2 | async-start | bytes 4194304 | tf_op jit(solution)/shard_map/all_to_all | solution.py:259
  119.2 2.2 fusion.83
  121.4 4.3 %collective-permute-start.1 = (bf16[1,1920,128]{2,1,0:T(8,128)(2,1)}, bf16[1,1920,128]{2,1,0:T(8,128)(2,1)}, u32[]{:S(2)}, u32[]{:S(2)}) collective-permute-start(bf16[1,1920,128]{2,1,0:T(8,128)(2,1)} %get-tuple-element.7), channel_id=1, source_target_pairs={{2,0},{4,2},{6,4},{8,6},{10,8},{12,10},{14,12},{16,14},{18,16},{20... | collective-permute-start | bytes 1474568 | tf_op jit(solution)/shard_map/ppermute | solution.py:249
  125.7 2.1 collective-permute-start
  127.9 0.6 reshape.471.taps_ref
  128.5 0.5 copy.70
  129.0 0.2 convert_element_type.107
  129.2 1.0 copy.71.refs_1_
  130.2 35.8 %all-to-all-done.2 = bf16[16,4,2,64,128]{4,1,3,2,0:T(4,128)(2,1)S(1)} async-done(((bf16[16,4,2,64,128]{4,1,3,2,0:T(4,128)(2,1)}), bf16[16,4,2,64,128]{4,1,3,2,0:T(4,128)(2,1)S(1)}, u32[]{:S(2)}, u32[]{:S(2)}) %all-to-all-start.2) | async-done | bytes 2097184 | tf_op jit(solution)/shard_map/all_to_all | solution.py:259
  166.0 4.6 %copy.69 = bf16[64,16,4,2,128]{4,3,2,1,0:T(2,128)(2,1)} copy(bf16[64,16,4,2,128]{4,2,0,3,1:T(4,128)(2,1)S(1)} %bitcast.92) | data formatting | bytes 4194304 | tf_op jit(solution)/shard_map/transpose | solution.py:260
  170.5 3.4 %collective-permute-done.1.high_ref = bf16[1,1920,128]{2,1,0:T(8,128)(2,1)} collective-permute-done((bf16[1,1920,128]{2,1,0:T(8,128)(2,1)}, bf16[1,1920,128]{2,1,0:T(8,128)(2,1)}, u32[]{:S(2)}, u32[]{:S(2)}) %collective-permute-start.1) | collective-permute-done | bytes 491552 | tf_op jit(solution)/shard_map/ppermute | solution.py:249
  174.0 3.5 %collective-permute-done.low_ref = bf16[1,1920,128]{2,1,0:T(8,128)(2,1)} collective-permute-done((bf16[1,1920,128]{2,1,0:T(8,128)(2,1)}, bf16[1,1920,128]{2,1,0:T(8,128)(2,1)}, u32[]{:S(2)}, u32[]{:S(2)}) %collective-permute-start) | collective-permute-done | bytes 491552 | tf_op jit(solution)/shard_map/ppermute | solution.py:248
  177.4 63.9 %shard_map.75 = bf16[64,1920,128]{2,1,0:T(8,128)(2,1)} custom-call(f32[9,128]{1,0:T(8,128)} %reshape.471.taps_ref, bf16[1,1920,128]{2,1,0:T(8,128)(2,1)} %collective-permute-done.low_ref, bf16[1,1920,128]{2,1,0:T(8,128)(2,1)} %collective-permute-done.1.high_ref, bf16[64,1920,128]{2,1,0:T(8,128)(2,1)} %below_ref.1, bf16[64,1920,128]{2,1,0:T(8,128)(2,1)} %below_ref.1, ...), custom_call_target="tpu_custom_call" | custom-call | tf_op jit(solution)/shard_map/pallas_call | solution.py:146
  (53 shorter events, 1.1 us)
Async XLA Ops:
  31.7 34.9 %all-to-all-start.1 = ((bf16[16,4,2,32,128]{4,3,2,1,0:T(8,128)(2,1)}), bf16[16,4,2,32,128]{4,3,2,1,0:T(8,128)(2,1)S(1)}, u32[]{:S(2)}, u32[]{:S(2)}) async-start(bf16[16,4,2,32,128]{4,3,2,1,0:T(8,128)(2,1)} %bitcast.89), calls=%async_computation.1 | async-start | bytes 2097152 | tf_op jit(solution)/shard_map/all_to_all | solution.py:189
  60.6 5.5 %copy-start.5 = (bf16[2,128,128]{2,1,0:T(8,128)(2,1)S(1)}, bf16[2,128,128]{2,1,0:T(8,128)(2,1)}, u32[]{:S(2)}) copy-start(bf16[2,128,128]{2,1,0:T(8,128)(2,1)} %param.10) | copy-start | bytes 196612
  60.6 5.5 %copy-start.6 = (bf16[2,128,128]{2,1,0:T(8,128)(2,1)S(1)}, bf16[2,128,128]{2,1,0:T(8,128)(2,1)}, u32[]{:S(2)}) copy-start(bf16[2,128,128]{2,1,0:T(8,128)(2,1)} %param.8) | copy-start | bytes 196612
  65.0 1.1 copy-start.12
  65.2 0.8 copy-start.9
  66.0 16.9 %copy-start.7 = (s32[4,128]{1,0:T(4,128)}, s32[4,128]{1,0:T(4,128)S(1)}, u32[]{:S(2)}) copy-start(s32[4,128]{1,0:T(4,128)S(1)} %add_add_fusion) | copy-start | bytes 6148
  66.7 30.9 %all-to-all-start = ((bf16[16,4,2,32,128]{4,3,2,1,0:T(8,128)(2,1)}), bf16[16,4,2,32,128]{4,3,2,1,0:T(8,128)(2,1)}, u32[]{:S(2)}, u32[]{:S(2)}) async-start(bf16[16,4,2,32,128]{4,3,2,1,0:T(8,128)(2,1)} %bitcast.90), calls=%async_computation | async-start | bytes 2097152 | tf_op jit(solution)/shard_map/all_to_all | solution.py:189
  83.3 0.9 copy-start.8
  97.6 1.8 copy-start.4
  99.5 4.9 %copy-start = (bf16[4,1,1,128,16,64]{3,5,2,4,1,0:T(8,128)(2,1)S(1)}, bf16[4,1,1,128,16,64]{3,5,2,4,1,0:T(8,128)(2,1)}, u32[]{:S(2)}) copy-start(bf16[4,1,1,128,16,64]{3,5,2,4,1,0:T(8,128)(2,1)} %get-tuple-element.18) | copy-start | bytes 3145732
  99.5 4.9 %copy-start.1 = (bf16[4,1,1,128,16,64]{3,5,2,4,1,0:T(8,128)(2,1)S(1)}, bf16[4,1,1,128,16,64]{3,5,2,4,1,0:T(8,128)(2,1)}, u32[]{:S(2)}) copy-start(bf16[4,1,1,128,16,64]{3,5,2,4,1,0:T(8,128)(2,1)} %get-tuple-element.19) | copy-start | bytes 3145732
  99.5 4.9 %copy-start.2 = (bf16[4,1,1,128,16,64]{3,5,2,4,1,0:T(8,128)(2,1)S(1)}, bf16[4,1,1,128,16,64]{3,5,2,4,1,0:T(8,128)(2,1)}, u32[]{:S(2)}) copy-start(bf16[4,1,1,128,16,64]{3,5,2,4,1,0:T(8,128)(2,1)} %get-tuple-element.20) | copy-start | bytes 3145732
  104.4 2.4 %copy-start.10 = (s32[4]{0:T(128)S(1)}, s32[4]{0:T(128)}, u32[]{:S(2)}) copy-start(s32[4]{0:T(128)} %copy-done.9) | copy-start | bytes 52
  104.4 2.4 %copy-start.13 = (pred[4]{0:T(512)(128)(4,1)S(1)}, pred[4]{0:T(512)(128)(4,1)}, u32[]{:S(2)}) copy-start(pred[4]{0:T(512)(128)(4,1)} %copy-done.12) | copy-start | bytes 16
  104.4 2.4 %copy-start.14 = (pred[4]{0:T(512)(128)(4,1)S(1)}, pred[4]{0:T(512)(128)(4,1)}, u32[]{:S(2)}) copy-start(pred[4]{0:T(512)(128)(4,1)} %not_and_fusion) | copy-start | bytes 16
  113.2 14.6 %copy-start.11 = (f32[3,3,128]{2,1,0:T(4,128)S(1)}, f32[3,3,128]{2,1,0:T(4,128)}, u32[]{:S(2)}) copy-start(f32[3,3,128]{2,1,0:T(4,128)} %param.12) | copy-start | bytes 13828
  113.3 15.2 %copy-start.3 = (bf16[1920,64,1]{0,1,2:T(8,128)(2,1)S(1)}, bf16[1920,64,1]{0,1,2:T(8,128)(2,1)}, u32[]{:S(2)}) copy-start(bf16[1920,64,1]{0,1,2:T(8,128)(2,1)} %get-tuple-element.28) | copy-start | bytes 737284
  113.3 52.7 %all-to-all-start.2 = ((bf16[16,4,2,64,128]{4,1,3,2,0:T(4,128)(2,1)}), bf16[16,4,2,64,128]{4,1,3,2,0:T(4,128)(2,1)S(1)}, u32[]{:S(2)}, u32[]{:S(2)}) async-start(bf16[16,4,2,64,128]{4,1,3,2,0:T(4,128)(2,1)} %convert_bitcast_fusion), calls=%async_computation.2 | async-start | bytes 4194304 | tf_op jit(solution)/shard_map/all_to_all | solution.py:259
  121.4 52.5 %collective-permute-start.1 = (bf16[1,1920,128]{2,1,0:T(8,128)(2,1)}, bf16[1,1920,128]{2,1,0:T(8,128)(2,1)}, u32[]{:S(2)}, u32[]{:S(2)}) collective-permute-start(bf16[1,1920,128]{2,1,0:T(8,128)(2,1)} %get-tuple-element.7), channel_id=1, source_target_pairs={{2,0},{4,2},{6,4},{8,6},{10,8},{12,10},{14,12},{16,14},{18,16},{20... | collective-permute-start | bytes 1474568 | tf_op jit(solution)/shard_map/ppermute | solution.py:249
  125.7 51.7 %collective-permute-start = (bf16[1,1920,128]{2,1,0:T(8,128)(2,1)}, bf16[1,1920,128]{2,1,0:T(8,128)(2,1)}, u32[]{:S(2)}, u32[]{:S(2)}) collective-permute-start(bf16[1,1920,128]{2,1,0:T(8,128)(2,1)} %get-tuple-element.8), channel_id=1, source_target_pairs={{0,2},{2,4},{4,6},{6,8},{8,10},{10,12},{12,14},{14,16},{16,18},{18... | collective-permute-start | bytes 1474568 | tf_op jit(solution)/shard_map/ppermute | solution.py:248

commit v5 on v4

--- a/solution.py
+++ b/solution.py
@@ -51,11 +51,17 @@
 def forward_kernel(field_ref, lon_ref, out_ref):
     block_rows, _, channels = field_ref.shape
     lon = lon_ref[...]
+    ones = jnp.ones((channels, channels), jnp.bfloat16)
     for h in range(block_rows):
-        x = field_ref[h].astype(jnp.float32)
-        average = jnp.sum(x, axis=1, keepdims=True) * (1.0 / channels)
-        centred = x - average
-        spread = jnp.sum(centred * centred, axis=1, keepdims=True) * (1.0 / channels)
+        raw = field_ref[h]
+        total = jnp.dot(raw, ones, preferred_element_type=jnp.float32)
+        average = total * (1.0 / channels)
+        centred = raw.astype(jnp.float32) - average
+        square = centred * centred
+        high = square.astype(jnp.bfloat16)
+        low = (square - high.astype(jnp.float32)).astype(jnp.bfloat16)
+        spread = jnp.dot(high, ones, preferred_element_type=jnp.float32)
+        spread = (spread + jnp.dot(low, ones, preferred_element_type=jnp.float32)) * (1.0 / channels)
         normed = (centred * lax.rsqrt(spread + 1e-05)).astype(jnp.bfloat16)
         out_ref[h] = jnp.dot(lon, normed, preferred_element_type=jnp.float32).astype(jnp.bfloat16)
 
@@ -102,10 +108,9 @@
             if in_wave:
                 grid_ref, lon_ref = refs[0], refs[1]
                 wave = jnp.dot(lon_ref[...], grid_ref[h], preferred_element_type=jnp.float32)
-                wave = wave.astype(jnp.bfloat16)
             else:
-                wave = refs[0][h]
-            out_ref[h] = ((xs[1] + wave.astype(jnp.float32)) + stencil).astype(jnp.bfloat16)
+                wave = refs[0][h].astype(jnp.float32)
+            out_ref[h] = ((xs[1] + wave) + stencil).astype(jnp.bfloat16)
 
     return kernel
 

time: 242 us -> 256 us (1.058)
  Pallas kernels: 107 us -> 121 us
    pallas_call x2, Pallas kernels: 43.2 us -> 58.2 us  [forward_rows(): pl.pallas_call(forward_kernel, grid=(count // block_rows,), in_specs=[pl....]
  transfers between devices with their start and end apart: 5 -> 5, of which waited for: 4 -> 4; matrix products, arithmetic and copies ran while one was open for 16% -> 15% of each run, Pallas kernels for 9% -> 11%
where the time goes in v5:
time: 256 us; the launch traced here: 255 us
  Pallas kernels  121 us (47%)
  waiting for transfers between devices  43.7 us (17%)
  other arithmetic  27 us (11%)
  starting transfers between devices  26.4 us (10%)
  local copies, waits for them, and re-layouts  22.3 us (9%)
  matrix products  14.4 us (6%)
    pallas_call x1, Pallas kernels, epilogue(): pl.pallas_call(kernel, grid=(count // block_rows,), in_specs=specs, out_s...  62.7 us
    pallas_call x2, Pallas kernels, forward_rows(): pl.pallas_call(forward_kernel, grid=(count // block_rows,), in_specs=[pl....  58.2 us
    all_to_all x1, waiting for transfers between devices, on_device(): lax.all_to_all(inverse, ('lat', 'lon'), split_axis=0, concat_axis=0, tile...  35.8 us
    another operation x3, other arithmetic  23.4 us
    all_to_all x2, starting transfers between devices, on_device(): lax.all_to_all(forward, ('lat', 'lon'), split_axis=0, concat_axis=0, tile...  14 us
    reshape x2, local copies, waits for them, and re-layouts, on_device(): forward = forward.reshape(part, devs, slots, 2, channels)  6.87 us
    dot_general x1, matrix products, on_device(): jnp.einsum('jk,skarc->sjarc', merge, partial, precision=lax.Precision.HIG...  6.41 us
    all_to_all x1, starting transfers between devices, on_device(): lax.all_to_all(inverse, ('lat', 'lon'), split_axis=0, concat_axis=0, tile...  5.99 us
  transfers between devices with their start and end apart: 5, of which 4 were waited for; matrix products, arithmetic and copies ran while one was open for 15% of the time, Pallas kernels for 11%

profile of v5, /device:TPU:16, one launch (start us, length us, event | category | flops | bytes accessed | tf_op | source)
XLA Modules:
  0.0 255.1 jit_solution(6103541404255635209)
XLA Ops:
  0.0 0.7 broadcast_compare_fusion.1
  0.7 0.7 maximum_shift-right-logical_fusion
  1.6 0.1 add.184
  1.8 0.1 and.174
  1.9 0.1 div.26
  2.0 3.1 %multiply_convert_fusion.3 = (bf16[1920,64,1]{0,1,2:T(8,128)(2,1)S(1)}, bf16[1920,64,1]{0,1,2:T(8,128)(2,1)}, f32[1920,64,1]{0,1,2:T(8,128)S(1)}, f32[1920,64,1]{0,1,2:T(8,128)S(1)}) fusion(f32[64]{0:T(128)S(1)} %get-tuple-element.5, s32[64]{0:T(128)S(1)} %get-tuple-element.6, f32[64]{0:T(128)S(1)} %fusion.79), kind=kLoop, calls=%fused_computation.62 | loop fusion | flops 1720320 | bytes 1475328 | tf_op jit(solution)/shard_map/convert
  5.2 0.5 copy.60
  5.7 1.0 reshape.472.lon_ref
  6.7 29.1 %shard_map.74 = bf16[32,128,128]{2,1,0:T(8,128)(2,1)} custom-call(bf16[64,1920,128]{2,1,0:T(8,128)(2,1)} %below_ref.1, bf16[128,1920]{1,0:T(8,128)(2,1)} %reshape.472.lon_ref), custom_call_target="tpu_custom_call" | custom-call | tf_op jit(solution)/shard_map/pallas_call | solution.py:74
  35.8 3.4 %copy.98 = bf16[32,16,4,2,128]{4,0,3,2,1:T(8,128)(2,1)} copy(bf16[32,16,4,2,128]{4,3,2,1,0:T(2,128)(2,1)} %bitcast.94) | data formatting | bytes 2097152 | tf_op jit(solution)/shard_map/reshape | solution.py:191
  39.2 7.1 %all-to-all-start.1 = ((bf16[16,4,2,32,128]{4,3,2,1,0:T(8,128)(2,1)}), bf16[16,4,2,32,128]{4,3,2,1,0:T(8,128)(2,1)S(1)}, u32[]{:S(2)}, u32[]{:S(2)}) async-start(bf16[16,4,2,32,128]{4,3,2,1,0:T(8,128)(2,1)} %bitcast.89), calls=%async_computation.1 | async-start | bytes 2097152 | tf_op jit(solution)/shard_map/all_to_all | solution.py:194
  46.3 0.1 copy.67
  46.4 29.1 %shard_map.73 = bf16[32,128,128]{2,1,0:T(8,128)(2,1)} custom-call(bf16[64,1920,128]{2,1,0:T(8,128)(2,1)} %below_ref.1, bf16[128,1920]{1,0:T(8,128)(2,1)} %reshape.472.lon_ref), custom_call_target="tpu_custom_call" | custom-call | tf_op jit(solution)/shard_map/pallas_call | solution.py:74
  75.6 0.1 copy.57
  75.8 0.1 copy.66
  76.0 0.1 copy.62
  76.3 3.4 %copy.99 = bf16[32,16,4,2,128]{4,0,3,2,1:T(8,128)(2,1)} copy(bf16[32,16,4,2,128]{4,3,2,1,0:T(2,128)(2,1)} %bitcast.93) | data formatting | bytes 2097152 | tf_op jit(solution)/shard_map/reshape | solution.py:191
  79.7 0.2 dynamic-slice_reduce_fusion.1
  79.9 0.2 dynamic-slice_reduce_fusion
  80.2 0.2 fusion.66
  80.4 0.5 not_and_fusion
  81.0 0.6 slice_bitcast_fusion
  81.6 6.9 %all-to-all-start = ((bf16[16,4,2,32,128]{4,3,2,1,0:T(8,128)(2,1)}), bf16[16,4,2,32,128]{4,3,2,1,0:T(8,128)(2,1)}, u32[]{:S(2)}, u32[]{:S(2)}) async-start(bf16[16,4,2,32,128]{4,3,2,1,0:T(8,128)(2,1)} %bitcast.90), calls=%async_computation | async-start | bytes 2097152 | tf_op jit(solution)/shard_map/all_to_all | solution.py:194
  88.6 9.3 %fusion.25 = (bf16[4,1,128,1,16,64]{2,5,3,1,0,4:T(8,128)(2,1)S(1)}, bf16[4,1,128,1,16,64]{2,5,3,1,0,4:T(8,128)(2,1)S(1)}, bf16[4,1,128,1,16,64]{2,5,3,1,0,4:T(8,128)(2,1)S(1)}) fusion(s32[16,64]{1,0:T(8,128)S(1)} %multiply_add_fusion, s32[4,128]{1,0:T(4,128)S(1)} %add_add_fusion), kind=kLoop, calls=%fused_computation.39 | loop fusion | flops 10485760 | bytes 3151872 | tf_op jit(solution)/shard_map/convert.13
  97.8 0.4 maximum_maximum_fusion
  98.2 0.9 fusion.84
  99.1 11.0 %negate_convert_fusion = (bf16[4,1,1,128,16,64]{3,5,2,4,1,0:T(8,128)(2,1)}, bf16[4,1,1,128,16,64]{3,5,2,4,1,0:T(8,128)(2,1)}, bf16[4,1,1,128,16,64]{3,5,2,4,1,0:T(8,128)(2,1)}) fusion(s32[16,64]{1,0:T(8,128)S(1)} %multiply_add_fusion, s32[4,128]{1,0:T(4,128)S(1)} %copy-done.8), kind=kLoop, calls=%fused_computation.33 | loop fusion | flops 10485760 | bytes 3151872 | tf_op jit(solution)/shard_map/convert.7
  110.1 1.4 fusion.19
  111.5 1.1 all-to-all-done
  112.6 1.8 fusion.21
  114.5 0.8 fusion.34
  115.2 2.4 fusion.33
  117.6 1.7 reshape.476
  119.4 2.4 fusion.10
  121.8 6.4 %convert_bitcast_fusion = bf16[16,4,2,64,128]{4,1,3,2,0:T(4,128)(2,1)} fusion(f32[16,4,2,64,128]{4,3,0,2,1:T(8,128)S(1)} %fusion.10, s32[4]{0:T(128)S(1)} %copy-done.10, pred[4]{0:T(512)(128)(4,1)S(1)} %copy-done.14, pred[4]{0:T(512)(128)(4,1)S(1)} %copy-done.13), kind=kOutput, calls=%fused_computation.32 | convolution fusion | flops 51380272 | bytes 6291480 | tf_op jit(solution)/shard_map/jk,skarc->sjarc/dot_general | solution.py:259
  128.2 6.0 %all-to-all-start.2 = ((bf16[16,4,2,64,128]{4,1,3,2,0:T(4,128)(2,1)}), bf16[16,4,2,64,128]{4,1,3,2,0:T(4,128)(2,1)S(1)}, u32[]{:S(2)}, u32[]{:S(2)}) async-start(bf16[16,4,2,64,128]{4,1,3,2,0:T(4,128)(2,1)} %convert_bitcast_fusion), calls=%async_computation.2 | async-start | bytes 4194304 | tf_op jit(solution)/shard_map/all_to_all | solution.py:264
  134.2 2.2 fusion.83
  136.4 4.3 %collective-permute-start.1 = (bf16[1,1920,128]{2,1,0:T(8,128)(2,1)}, bf16[1,1920,128]{2,1,0:T(8,128)(2,1)}, u32[]{:S(2)}, u32[]{:S(2)}) collective-permute-start(bf16[1,1920,128]{2,1,0:T(8,128)(2,1)} %get-tuple-element.7), channel_id=1, source_target_pairs={{2,0},{4,2},{6,4},{8,6},{10,8},{12,10},{14,12},{16,14},{18,16},{20... | collective-permute-start | bytes 1474568 | tf_op jit(solution)/shard_map/ppermute | solution.py:254
  140.6 2.1 collective-permute-start
  142.8 0.6 reshape.471.taps_ref
  143.5 0.5 copy.70
  144.0 0.2 convert_element_type.107
  144.2 1.0 copy.71.refs_1_
  145.2 35.8 %all-to-all-done.2 = bf16[16,4,2,64,128]{4,1,3,2,0:T(4,128)(2,1)S(1)} async-done(((bf16[16,4,2,64,128]{4,1,3,2,0:T(4,128)(2,1)}), bf16[16,4,2,64,128]{4,1,3,2,0:T(4,128)(2,1)S(1)}, u32[]{:S(2)}, u32[]{:S(2)}) %all-to-all-start.2) | async-done | bytes 2097184 | tf_op jit(solution)/shard_map/all_to_all | solution.py:264
  180.9 4.6 %copy.69 = bf16[64,16,4,2,128]{4,3,2,1,0:T(2,128)(2,1)} copy(bf16[64,16,4,2,128]{4,2,0,3,1:T(4,128)(2,1)S(1)} %bitcast.92) | data formatting | bytes 4194304 | tf_op jit(solution)/shard_map/transpose | solution.py:265
  185.5 3.4 %collective-permute-done.1.high_ref = bf16[1,1920,128]{2,1,0:T(8,128)(2,1)} collective-permute-done((bf16[1,1920,128]{2,1,0:T(8,128)(2,1)}, bf16[1,1920,128]{2,1,0:T(8,128)(2,1)}, u32[]{:S(2)}, u32[]{:S(2)}) %collective-permute-start.1) | collective-permute-done | bytes 491552 | tf_op jit(solution)/shard_map/ppermute | solution.py:254
  188.9 3.5 %collective-permute-done.low_ref = bf16[1,1920,128]{2,1,0:T(8,128)(2,1)} collective-permute-done((bf16[1,1920,128]{2,1,0:T(8,128)(2,1)}, bf16[1,1920,128]{2,1,0:T(8,128)(2,1)}, u32[]{:S(2)}, u32[]{:S(2)}) %collective-permute-start) | collective-permute-done | bytes 491552 | tf_op jit(solution)/shard_map/ppermute | solution.py:253
  192.4 62.7 %shard_map.75 = bf16[64,1920,128]{2,1,0:T(8,128)(2,1)} custom-call(f32[9,128]{1,0:T(8,128)} %reshape.471.taps_ref, bf16[1,1920,128]{2,1,0:T(8,128)(2,1)} %collective-permute-done.low_ref, bf16[1,1920,128]{2,1,0:T(8,128)(2,1)} %collective-permute-done.1.high_ref, bf16[64,1920,128]{2,1,0:T(8,128)(2,1)} %below_ref.1, bf16[64,1920,128]{2,1,0:T(8,128)(2,1)} %below_ref.1, ...), custom_call_target="tpu_custom_call" | custom-call | tf_op jit(solution)/shard_map/pallas_call | solution.py:151
  (53 shorter events, 1.1 us)
Async XLA Ops:
  39.2 42.4 %all-to-all-start.1 = ((bf16[16,4,2,32,128]{4,3,2,1,0:T(8,128)(2,1)}), bf16[16,4,2,32,128]{4,3,2,1,0:T(8,128)(2,1)S(1)}, u32[]{:S(2)}, u32[]{:S(2)}) async-start(bf16[16,4,2,32,128]{4,3,2,1,0:T(8,128)(2,1)} %bitcast.89), calls=%async_computation.1 | async-start | bytes 2097152 | tf_op jit(solution)/shard_map/all_to_all | solution.py:194
  75.5 5.5 %copy-start.5 = (bf16[2,128,128]{2,1,0:T(8,128)(2,1)S(1)}, bf16[2,128,128]{2,1,0:T(8,128)(2,1)}, u32[]{:S(2)}) copy-start(bf16[2,128,128]{2,1,0:T(8,128)(2,1)} %param.10) | copy-start | bytes 196612
  75.5 5.5 %copy-start.6 = (bf16[2,128,128]{2,1,0:T(8,128)(2,1)S(1)}, bf16[2,128,128]{2,1,0:T(8,128)(2,1)}, u32[]{:S(2)}) copy-start(bf16[2,128,128]{2,1,0:T(8,128)(2,1)} %param.8) | copy-start | bytes 196612
  79.9 1.1 copy-start.12
  80.2 0.8 copy-start.9
  81.0 16.9 %copy-start.7 = (s32[4,128]{1,0:T(4,128)}, s32[4,128]{1,0:T(4,128)S(1)}, u32[]{:S(2)}) copy-start(s32[4,128]{1,0:T(4,128)S(1)} %add_add_fusion) | copy-start | bytes 6148
  81.6 30.9 %all-to-all-start = ((bf16[16,4,2,32,128]{4,3,2,1,0:T(8,128)(2,1)}), bf16[16,4,2,32,128]{4,3,2,1,0:T(8,128)(2,1)}, u32[]{:S(2)}, u32[]{:S(2)}) async-start(bf16[16,4,2,32,128]{4,3,2,1,0:T(8,128)(2,1)} %bitcast.90), calls=%async_computation | async-start | bytes 2097152 | tf_op jit(solution)/shard_map/all_to_all | solution.py:194
  98.2 0.9 copy-start.8
  112.6 1.8 copy-start.4
  114.4 4.9 %copy-start = (bf16[4,1,1,128,16,64]{3,5,2,4,1,0:T(8,128)(2,1)S(1)}, bf16[4,1,1,128,16,64]{3,5,2,4,1,0:T(8,128)(2,1)}, u32[]{:S(2)}) copy-start(bf16[4,1,1,128,16,64]{3,5,2,4,1,0:T(8,128)(2,1)} %get-tuple-element.18) | copy-start | bytes 3145732
  114.4 4.9 %copy-start.1 = (bf16[4,1,1,128,16,64]{3,5,2,4,1,0:T(8,128)(2,1)S(1)}, bf16[4,1,1,128,16,64]{3,5,2,4,1,0:T(8,128)(2,1)}, u32[]{:S(2)}) copy-start(bf16[4,1,1,128,16,64]{3,5,2,4,1,0:T(8,128)(2,1)} %get-tuple-element.19) | copy-start | bytes 3145732
  114.5 4.9 %copy-start.2 = (bf16[4,1,1,128,16,64]{3,5,2,4,1,0:T(8,128)(2,1)S(1)}, bf16[4,1,1,128,16,64]{3,5,2,4,1,0:T(8,128)(2,1)}, u32[]{:S(2)}) copy-start(bf16[4,1,1,128,16,64]{3,5,2,4,1,0:T(8,128)(2,1)} %get-tuple-element.20) | copy-start | bytes 3145732
  119.3 2.4 copy-start.10
  119.3 2.4 copy-start.13
  119.3 2.4 copy-start.14
  128.2 14.6 %copy-start.11 = (f32[3,3,128]{2,1,0:T(4,128)S(1)}, f32[3,3,128]{2,1,0:T(4,128)}, u32[]{:S(2)}) copy-start(f32[3,3,128]{2,1,0:T(4,128)} %param.12) | copy-start | bytes 13828
  128.2 15.2 %copy-start.3 = (bf16[1920,64,1]{0,1,2:T(8,128)(2,1)S(1)}, bf16[1920,64,1]{0,1,2:T(8,128)(2,1)}, u32[]{:S(2)}) copy-start(bf16[1920,64,1]{0,1,2:T(8,128)(2,1)} %get-tuple-element.28) | copy-start | bytes 737284
  128.2 52.7 %all-to-all-start.2 = ((bf16[16,4,2,64,128]{4,1,3,2,0:T(4,128)(2,1)}), bf16[16,4,2,64,128]{4,1,3,2,0:T(4,128)(2,1)S(1)}, u32[]{:S(2)}, u32[]{:S(2)}) async-start(bf16[16,4,2,64,128]{4,1,3,2,0:T(4,128)(2,1)} %convert_bitcast_fusion), calls=%async_computation.2 | async-start | bytes 4194304 | tf_op jit(solution)/shard_map/all_to_all | solution.py:264
  136.4 52.5 %collective-permute-start.1 = (bf16[1,1920,128]{2,1,0:T(8,128)(2,1)}, bf16[1,1920,128]{2,1,0:T(8,128)(2,1)}, u32[]{:S(2)}, u32[]{:S(2)}) collective-permute-start(bf16[1,1920,128]{2,1,0:T(8,128)(2,1)} %get-tuple-element.7), channel_id=1, source_target_pairs={{2,0},{4,2},{6,4},{8,6},{10,8},{12,10},{14,12},{16,14},{18,16},{20... | collective-permute-start | bytes 1474568 | tf_op jit(solution)/shard_map/ppermute | solution.py:254
  140.6 51.7 %collective-permute-start = (bf16[1,1920,128]{2,1,0:T(8,128)(2,1)}, bf16[1,1920,128]{2,1,0:T(8,128)(2,1)}, u32[]{:S(2)}, u32[]{:S(2)}) collective-permute-start(bf16[1,1920,128]{2,1,0:T(8,128)(2,1)} %get-tuple-element.8), channel_id=1, source_target_pairs={{0,2},{2,4},{4,6},{6,8},{8,10},{10,12},{12,14},{14,16},{16,18},{18... | collective-permute-start | bytes 1474568 | tf_op jit(solution)/shard_map/ppermute | solution.py:253

commit v6 on v4

--- a/solution.py
+++ b/solution.py
@@ -102,17 +102,16 @@
             if in_wave:
                 grid_ref, lon_ref = refs[0], refs[1]
                 wave = jnp.dot(lon_ref[...], grid_ref[h], preferred_element_type=jnp.float32)
-                wave = wave.astype(jnp.bfloat16)
             else:
-                wave = refs[0][h]
-            out_ref[h] = ((xs[1] + wave.astype(jnp.float32)) + stencil).astype(jnp.bfloat16)
+                wave = refs[0][h].astype(jnp.float32)
+            out_ref[h] = ((xs[1] + wave) + stencil).astype(jnp.bfloat16)
 
     return kernel
 
 
 def epilogue(field, low, high, conv_kernel, wave_args, start, count, prior):
     rows, width, channels = field.shape
-    block_rows = math.gcd(count, 4)
+    block_rows = math.gcd(count, 8)
     offset = start // block_rows
     taps = conv_kernel.reshape(9, channels)
     halo_spec = pl.BlockSpec((1, width, channels), lambda i: (0, 0, 0))

time: 242 us -> 241 us (level)
  no operation moved by 1% of the time
where the time goes in v6:
time: 241 us; the launch traced here: 240 us
  Pallas kernels  106 us (44%)
  waiting for transfers between devices  43.7 us (18%)
  other arithmetic  27 us (11%)
  starting transfers between devices  26.4 us (11%)
  local copies, waits for them, and re-layouts  22.3 us (9%)
  matrix products  14.4 us (6%)
    pallas_call x1, Pallas kernels, epilogue(): pl.pallas_call(kernel, grid=(count // block_rows,), in_specs=specs, out_s...  62.8 us
    pallas_call x2, Pallas kernels, forward_rows(): pl.pallas_call(forward_kernel, grid=(count // block_rows,), in_specs=[pl....  43.2 us
    all_to_all x1, waiting for transfers between devices, on_device(): lax.all_to_all(inverse, ('lat', 'lon'), split_axis=0, concat_axis=0, tile...  35.8 us
    another operation x3, other arithmetic  23.4 us
    all_to_all x2, starting transfers between devices, on_device(): lax.all_to_all(forward, ('lat', 'lon'), split_axis=0, concat_axis=0, tile...  14 us
    reshape x2, local copies, waits for them, and re-layouts, on_device(): forward = forward.reshape(part, devs, slots, 2, channels)  6.87 us
    dot_general x1, matrix products, on_device(): jnp.einsum('jk,skarc->sjarc', merge, partial, precision=lax.Precision.HIG...  6.41 us
    all_to_all x1, starting transfers between devices, on_device(): lax.all_to_all(inverse, ('lat', 'lon'), split_axis=0, concat_axis=0, tile...  5.98 us
  transfers between devices with their start and end apart: 5, of which 4 were waited for; matrix products, arithmetic and copies ran while one was open for 16% of the time, Pallas kernels for 9%

profile of v6, /device:TPU:16, one launch (start us, length us, event | category | flops | bytes accessed | tf_op | source)
XLA Modules:
  0.0 240.2 jit_solution(12632766073950760322)
XLA Ops:
  0.0 0.7 broadcast_compare_fusion.1
  0.7 0.7 maximum_shift-right-logical_fusion
  1.6 0.1 add.184
  1.8 0.1 and.174
  1.9 0.1 div.26
  2.0 3.1 %multiply_convert_fusion.3 = (bf16[1920,64,1]{0,1,2:T(8,128)(2,1)S(1)}, bf16[1920,64,1]{0,1,2:T(8,128)(2,1)}, f32[1920,64,1]{0,1,2:T(8,128)S(1)}, f32[1920,64,1]{0,1,2:T(8,128)S(1)}) fusion(f32[64]{0:T(128)S(1)} %get-tuple-element.5, s32[64]{0:T(128)S(1)} %get-tuple-element.6, f32[64]{0:T(128)S(1)} %fusion.79), kind=kLoop, calls=%fused_computation.62 | loop fusion | flops 1720320 | bytes 1475328 | tf_op jit(solution)/shard_map/convert
  5.2 0.5 copy.60
  5.7 1.0 reshape.472.lon_ref
  6.7 21.6 %shard_map.74 = bf16[32,128,128]{2,1,0:T(8,128)(2,1)} custom-call(bf16[64,1920,128]{2,1,0:T(8,128)(2,1)} %below_ref.1, bf16[128,1920]{1,0:T(8,128)(2,1)} %reshape.472.lon_ref), custom_call_target="tpu_custom_call" | custom-call | tf_op jit(solution)/shard_map/pallas_call | solution.py:68
  28.3 3.4 %copy.98 = bf16[32,16,4,2,128]{4,0,3,2,1:T(8,128)(2,1)} copy(bf16[32,16,4,2,128]{4,3,2,1,0:T(2,128)(2,1)} %bitcast.94) | data formatting | bytes 2097152 | tf_op jit(solution)/shard_map/reshape | solution.py:185
  31.7 7.1 %all-to-all-start.1 = ((bf16[16,4,2,32,128]{4,3,2,1,0:T(8,128)(2,1)}), bf16[16,4,2,32,128]{4,3,2,1,0:T(8,128)(2,1)S(1)}, u32[]{:S(2)}, u32[]{:S(2)}) async-start(bf16[16,4,2,32,128]{4,3,2,1,0:T(8,128)(2,1)} %bitcast.89), calls=%async_computation.1 | async-start | bytes 2097152 | tf_op jit(solution)/shard_map/all_to_all | solution.py:188
  38.9 0.1 copy.67
  39.0 21.6 %shard_map.73 = bf16[32,128,128]{2,1,0:T(8,128)(2,1)} custom-call(bf16[64,1920,128]{2,1,0:T(8,128)(2,1)} %below_ref.1, bf16[128,1920]{1,0:T(8,128)(2,1)} %reshape.472.lon_ref), custom_call_target="tpu_custom_call" | custom-call | tf_op jit(solution)/shard_map/pallas_call | solution.py:68
  60.6 0.1 copy.57
  60.9 0.1 copy.66
  61.1 0.1 copy.62
  61.4 3.4 %copy.99 = bf16[32,16,4,2,128]{4,0,3,2,1:T(8,128)(2,1)} copy(bf16[32,16,4,2,128]{4,3,2,1,0:T(2,128)(2,1)} %bitcast.93) | data formatting | bytes 2097152 | tf_op jit(solution)/shard_map/reshape | solution.py:185
  64.8 0.2 dynamic-slice_reduce_fusion.1
  65.0 0.2 dynamic-slice_reduce_fusion
  65.2 0.2 fusion.66
  65.4 0.5 not_and_fusion
  66.1 0.6 slice_bitcast_fusion
  66.7 6.9 %all-to-all-start = ((bf16[16,4,2,32,128]{4,3,2,1,0:T(8,128)(2,1)}), bf16[16,4,2,32,128]{4,3,2,1,0:T(8,128)(2,1)}, u32[]{:S(2)}, u32[]{:S(2)}) async-start(bf16[16,4,2,32,128]{4,3,2,1,0:T(8,128)(2,1)} %bitcast.90), calls=%async_computation | async-start | bytes 2097152 | tf_op jit(solution)/shard_map/all_to_all | solution.py:188
  73.6 9.3 %fusion.25 = (bf16[4,1,128,1,16,64]{2,5,3,1,0,4:T(8,128)(2,1)S(1)}, bf16[4,1,128,1,16,64]{2,5,3,1,0,4:T(8,128)(2,1)S(1)}, bf16[4,1,128,1,16,64]{2,5,3,1,0,4:T(8,128)(2,1)S(1)}) fusion(s32[16,64]{1,0:T(8,128)S(1)} %multiply_add_fusion, s32[4,128]{1,0:T(4,128)S(1)} %add_add_fusion), kind=kLoop, calls=%fused_computation.39 | loop fusion | flops 10485760 | bytes 3151872 | tf_op jit(solution)/shard_map/convert.13
  82.9 0.4 maximum_maximum_fusion
  83.3 0.9 fusion.84
  84.2 11.0 %negate_convert_fusion = (bf16[4,1,1,128,16,64]{3,5,2,4,1,0:T(8,128)(2,1)}, bf16[4,1,1,128,16,64]{3,5,2,4,1,0:T(8,128)(2,1)}, bf16[4,1,1,128,16,64]{3,5,2,4,1,0:T(8,128)(2,1)}) fusion(s32[16,64]{1,0:T(8,128)S(1)} %multiply_add_fusion, s32[4,128]{1,0:T(4,128)S(1)} %copy-done.8), kind=kLoop, calls=%fused_computation.33 | loop fusion | flops 10485760 | bytes 3151872 | tf_op jit(solution)/shard_map/convert.7
  95.2 1.4 fusion.19
  96.6 1.1 all-to-all-done
  97.6 1.8 fusion.21
  99.5 0.8 fusion.34
  100.3 2.4 fusion.33
  102.7 1.7 reshape.476
  104.4 2.4 fusion.10
  106.8 6.4 %convert_bitcast_fusion = bf16[16,4,2,64,128]{4,1,3,2,0:T(4,128)(2,1)} fusion(f32[16,4,2,64,128]{4,3,0,2,1:T(8,128)S(1)} %fusion.10, s32[4]{0:T(128)S(1)} %copy-done.10, pred[4]{0:T(512)(128)(4,1)S(1)} %copy-done.14, pred[4]{0:T(512)(128)(4,1)S(1)} %copy-done.13), kind=kOutput, calls=%fused_computation.32 | convolution fusion | flops 51380272 | bytes 6291480 | tf_op jit(solution)/shard_map/jk,skarc->sjarc/dot_general | solution.py:253
  113.3 6.0 %all-to-all-start.2 = ((bf16[16,4,2,64,128]{4,1,3,2,0:T(4,128)(2,1)}), bf16[16,4,2,64,128]{4,1,3,2,0:T(4,128)(2,1)S(1)}, u32[]{:S(2)}, u32[]{:S(2)}) async-start(bf16[16,4,2,64,128]{4,1,3,2,0:T(4,128)(2,1)} %convert_bitcast_fusion), calls=%async_computation.2 | async-start | bytes 4194304 | tf_op jit(solution)/shard_map/all_to_all | solution.py:258
  119.2 2.2 fusion.83
  121.4 4.3 %collective-permute-start.1 = (bf16[1,1920,128]{2,1,0:T(8,128)(2,1)}, bf16[1,1920,128]{2,1,0:T(8,128)(2,1)}, u32[]{:S(2)}, u32[]{:S(2)}) collective-permute-start(bf16[1,1920,128]{2,1,0:T(8,128)(2,1)} %get-tuple-element.7), channel_id=1, source_target_pairs={{2,0},{4,2},{6,4},{8,6},{10,8},{12,10},{14,12},{16,14},{18,16},{20... | collective-permute-start | bytes 1474568 | tf_op jit(solution)/shard_map/ppermute | solution.py:248
  125.7 2.1 collective-permute-start
  127.9 0.6 reshape.471.taps_ref
  128.5 0.5 copy.70
  129.0 0.2 convert_element_type.107
  129.2 1.0 copy.71.refs_1_
  130.2 35.8 %all-to-all-done.2 = bf16[16,4,2,64,128]{4,1,3,2,0:T(4,128)(2,1)S(1)} async-done(((bf16[16,4,2,64,128]{4,1,3,2,0:T(4,128)(2,1)}), bf16[16,4,2,64,128]{4,1,3,2,0:T(4,128)(2,1)S(1)}, u32[]{:S(2)}, u32[]{:S(2)}) %all-to-all-start.2) | async-done | bytes 2097184 | tf_op jit(solution)/shard_map/all_to_all | solution.py:258
  166.0 4.6 %copy.69 = bf16[64,16,4,2,128]{4,3,2,1,0:T(2,128)(2,1)} copy(bf16[64,16,4,2,128]{4,2,0,3,1:T(4,128)(2,1)S(1)} %bitcast.92) | data formatting | bytes 4194304 | tf_op jit(solution)/shard_map/transpose | solution.py:259
  170.5 3.4 %collective-permute-done.1.high_ref = bf16[1,1920,128]{2,1,0:T(8,128)(2,1)} collective-permute-done((bf16[1,1920,128]{2,1,0:T(8,128)(2,1)}, bf16[1,1920,128]{2,1,0:T(8,128)(2,1)}, u32[]{:S(2)}, u32[]{:S(2)}) %collective-permute-start.1) | collective-permute-done | bytes 491552 | tf_op jit(solution)/shard_map/ppermute | solution.py:248
  174.0 3.5 %collective-permute-done.low_ref = bf16[1,1920,128]{2,1,0:T(8,128)(2,1)} collective-permute-done((bf16[1,1920,128]{2,1,0:T(8,128)(2,1)}, bf16[1,1920,128]{2,1,0:T(8,128)(2,1)}, u32[]{:S(2)}, u32[]{:S(2)}) %collective-permute-start) | collective-permute-done | bytes 491552 | tf_op jit(solution)/shard_map/ppermute | solution.py:247
  177.4 62.8 %shard_map.75 = bf16[64,1920,128]{2,1,0:T(8,128)(2,1)} custom-call(f32[9,128]{1,0:T(8,128)} %reshape.471.taps_ref, bf16[1,1920,128]{2,1,0:T(8,128)(2,1)} %collective-permute-done.low_ref, bf16[1,1920,128]{2,1,0:T(8,128)(2,1)} %collective-permute-done.1.high_ref, bf16[64,1920,128]{2,1,0:T(8,128)(2,1)} %below_ref.1, bf16[64,1920,128]{2,1,0:T(8,128)(2,1)} %below_ref.1, ...), custom_call_target="tpu_custom_call" | custom-call | tf_op jit(solution)/shard_map/pallas_call | solution.py:145
  (53 shorter events, 1.1 us)
Async XLA Ops:
  31.7 34.9 %all-to-all-start.1 = ((bf16[16,4,2,32,128]{4,3,2,1,0:T(8,128)(2,1)}), bf16[16,4,2,32,128]{4,3,2,1,0:T(8,128)(2,1)S(1)}, u32[]{:S(2)}, u32[]{:S(2)}) async-start(bf16[16,4,2,32,128]{4,3,2,1,0:T(8,128)(2,1)} %bitcast.89), calls=%async_computation.1 | async-start | bytes 2097152 | tf_op jit(solution)/shard_map/all_to_all | solution.py:188
  60.6 5.5 %copy-start.5 = (bf16[2,128,128]{2,1,0:T(8,128)(2,1)S(1)}, bf16[2,128,128]{2,1,0:T(8,128)(2,1)}, u32[]{:S(2)}) copy-start(bf16[2,128,128]{2,1,0:T(8,128)(2,1)} %param.10) | copy-start | bytes 196612
  60.6 5.5 %copy-start.6 = (bf16[2,128,128]{2,1,0:T(8,128)(2,1)S(1)}, bf16[2,128,128]{2,1,0:T(8,128)(2,1)}, u32[]{:S(2)}) copy-start(bf16[2,128,128]{2,1,0:T(8,128)(2,1)} %param.8) | copy-start | bytes 196612
  65.0 1.1 copy-start.12
  65.2 0.8 copy-start.9
  66.0 16.9 %copy-start.7 = (s32[4,128]{1,0:T(4,128)}, s32[4,128]{1,0:T(4,128)S(1)}, u32[]{:S(2)}) copy-start(s32[4,128]{1,0:T(4,128)S(1)} %add_add_fusion) | copy-start | bytes 6148
  66.7 30.9 %all-to-all-start = ((bf16[16,4,2,32,128]{4,3,2,1,0:T(8,128)(2,1)}), bf16[16,4,2,32,128]{4,3,2,1,0:T(8,128)(2,1)}, u32[]{:S(2)}, u32[]{:S(2)}) async-start(bf16[16,4,2,32,128]{4,3,2,1,0:T(8,128)(2,1)} %bitcast.90), calls=%async_computation | async-start | bytes 2097152 | tf_op jit(solution)/shard_map/all_to_all | solution.py:188
  83.3 0.9 copy-start.8
  97.6 1.8 copy-start.4
  99.5 4.9 %copy-start = (bf16[4,1,1,128,16,64]{3,5,2,4,1,0:T(8,128)(2,1)S(1)}, bf16[4,1,1,128,16,64]{3,5,2,4,1,0:T(8,128)(2,1)}, u32[]{:S(2)}) copy-start(bf16[4,1,1,128,16,64]{3,5,2,4,1,0:T(8,128)(2,1)} %get-tuple-element.18) | copy-start | bytes 3145732
  99.5 4.9 %copy-start.1 = (bf16[4,1,1,128,16,64]{3,5,2,4,1,0:T(8,128)(2,1)S(1)}, bf16[4,1,1,128,16,64]{3,5,2,4,1,0:T(8,128)(2,1)}, u32[]{:S(2)}) copy-start(bf16[4,1,1,128,16,64]{3,5,2,4,1,0:T(8,128)(2,1)} %get-tuple-element.19) | copy-start | bytes 3145732
  99.5 4.9 %copy-start.2 = (bf16[4,1,1,128,16,64]{3,5,2,4,1,0:T(8,128)(2,1)S(1)}, bf16[4,1,1,128,16,64]{3,5,2,4,1,0:T(8,128)(2,1)}, u32[]{:S(2)}) copy-start(bf16[4,1,1,128,16,64]{3,5,2,4,1,0:T(8,128)(2,1)} %get-tuple-element.20) | copy-start | bytes 3145732
  104.4 2.4 %copy-start.10 = (s32[4]{0:T(128)S(1)}, s32[4]{0:T(128)}, u32[]{:S(2)}) copy-start(s32[4]{0:T(128)} %copy-done.9) | copy-start | bytes 52
  104.4 2.4 %copy-start.13 = (pred[4]{0:T(512)(128)(4,1)S(1)}, pred[4]{0:T(512)(128)(4,1)}, u32[]{:S(2)}) copy-start(pred[4]{0:T(512)(128)(4,1)} %copy-done.12) | copy-start | bytes 16
  104.4 2.4 %copy-start.14 = (pred[4]{0:T(512)(128)(4,1)S(1)}, pred[4]{0:T(512)(128)(4,1)}, u32[]{:S(2)}) copy-start(pred[4]{0:T(512)(128)(4,1)} %not_and_fusion) | copy-start | bytes 16
  113.2 14.6 %copy-start.11 = (f32[3,3,128]{2,1,0:T(4,128)S(1)}, f32[3,3,128]{2,1,0:T(4,128)}, u32[]{:S(2)}) copy-start(f32[3,3,128]{2,1,0:T(4,128)} %param.12) | copy-start | bytes 13828
  113.3 15.2 %copy-start.3 = (bf16[1920,64,1]{0,1,2:T(8,128)(2,1)S(1)}, bf16[1920,64,1]{0,1,2:T(8,128)(2,1)}, u32[]{:S(2)}) copy-start(bf16[1920,64,1]{0,1,2:T(8,128)(2,1)} %get-tuple-element.28) | copy-start | bytes 737284
  113.3 52.7 %all-to-all-start.2 = ((bf16[16,4,2,64,128]{4,1,3,2,0:T(4,128)(2,1)}), bf16[16,4,2,64,128]{4,1,3,2,0:T(4,128)(2,1)S(1)}, u32[]{:S(2)}, u32[]{:S(2)}) async-start(bf16[16,4,2,64,128]{4,1,3,2,0:T(4,128)(2,1)} %convert_bitcast_fusion), calls=%async_computation.2 | async-start | bytes 4194304 | tf_op jit(solution)/shard_map/all_to_all | solution.py:258
  121.4 52.5 %collective-permute-start.1 = (bf16[1,1920,128]{2,1,0:T(8,128)(2,1)}, bf16[1,1920,128]{2,1,0:T(8,128)(2,1)}, u32[]{:S(2)}, u32[]{:S(2)}) collective-permute-start(bf16[1,1920,128]{2,1,0:T(8,128)(2,1)} %get-tuple-element.7), channel_id=1, source_target_pairs={{2,0},{4,2},{6,4},{8,6},{10,8},{12,10},{14,12},{16,14},{18,16},{20... | collective-permute-start | bytes 1474568 | tf_op jit(solution)/shard_map/ppermute | solution.py:248
  125.7 51.7 %collective-permute-start = (bf16[1,1920,128]{2,1,0:T(8,128)(2,1)}, bf16[1,1920,128]{2,1,0:T(8,128)(2,1)}, u32[]{:S(2)}, u32[]{:S(2)}) collective-permute-start(bf16[1,1920,128]{2,1,0:T(8,128)(2,1)} %get-tuple-element.8), channel_id=1, source_target_pairs={{0,2},{2,4},{4,6},{6,8},{8,10},{10,12},{12,14},{14,16},{16,18},{18... | collective-permute-start | bytes 1474568 | tf_op jit(solution)/shard_map/ppermute | solution.py:247

commit v7 on v6

--- a/solution.py
+++ b/solution.py
@@ -39,9 +39,10 @@
     return phases.astype(jnp.float32) * (2.0 * math.pi / width)
 
 
-def lat_trig(lat_modes, height):
+def lat_trig(lat_modes, height, rowids=None):
     freqs = lat_modes - KH // 2
-    rowids = jnp.arange(height, dtype=jnp.int32)
+    if rowids is None:
+        rowids = jnp.arange(height, dtype=jnp.int32)
     phases = jnp.mod(freqs[..., None] * rowids, height)
     angles = phases.astype(jnp.float32) * (2.0 * math.pi / height)
     factor = 1.0 / math.sqrt(height)
@@ -226,15 +227,6 @@
     filtered = jnp.where(my_valid[:, None, None], shrunk, 0.0).astype(jnp.bfloat16)
     filtered = filtered.reshape(slots, MB, 2, channels)
 
-    lat_inv = jnp.stack(
-        [jnp.stack([cosine, -sine], axis=1), jnp.stack([sine, cosine], axis=1)], axis=1
-    ).astype(jnp.bfloat16)
-    lat_inv = lat_inv.reshape(slots, 2, 2, MB, devs, rows)
-    same = (my_mode[:, None] == my_mode[None, :]) & my_valid[None, :]
-    earlier = jnp.tril(jnp.ones((slots, slots), jnp.bool_), -1)
-    first = my_valid & ~jnp.any(same & earlier, axis=1)
-    merge = (same & first[:, None]).astype(jnp.float32)
-
     inv_angles = lon_angles(modes.reshape(-1), width)
     weights = jnp.where(modes.reshape(-1) == 0, 1.0, 2.0).astype(jnp.float32) / math.sqrt(width)
     lon_inv = jnp.stack(
@@ -247,19 +239,53 @@
     low = lax.ppermute(field[rows - 1 :], ("lat", "lon"), forward_pairs)
     high = lax.ppermute(field[:1], ("lat", "lon"), backward_pairs)
 
-    partial = jnp.einsum(
-        "jabqsr,jqbc->sjarc", lat_inv, filtered, preferred_element_type=jnp.float32
-    )
-    combined = jnp.einsum(
-        "jk,skarc->sjarc", merge, partial, precision=lax.Precision.HIGHEST,
-        preferred_element_type=jnp.float32,
-    )
-    inverse = combined.astype(jnp.bfloat16)
-    rowwise = lax.all_to_all(inverse, ("lat", "lon"), split_axis=0, concat_axis=0, tiled=True)
-    grid_rows = jnp.transpose(rowwise, (3, 0, 1, 2, 4)).reshape(rows, n, channels)
     if n <= 512:
+        gathered = lax.all_gather(filtered, ("lat", "lon"), axis=0, tiled=True)
+        block_modes = (
+            jnp.arange(blocks, dtype=jnp.int32)[:, None] * MB
+            + jnp.arange(MB, dtype=jnp.int32)[None, :]
+        )
+        my_rows = me * rows + jnp.arange(rows, dtype=jnp.int32)
+        row_cos, row_sin = lat_trig(block_modes, height, my_rows)
+        inv_table = jnp.stack(
+            [jnp.stack([row_cos, -row_sin], axis=1), jnp.stack([row_sin, row_cos], axis=1)],
+            axis=1,
+        ).astype(jnp.bfloat16)
+        chosen = jnp.take(inv_table, lat_block.reshape(-1), axis=0)
+        partial = jnp.einsum(
+            "nabqr,nqbc->rnac", chosen, gathered, preferred_element_type=jnp.float32
+        )
+        partial = partial.reshape(rows, devs, slots, 2, channels)
+        same_all = (local_mode[:, :, None] == local_mode[:, None, :]) & valid[:, None, :]
+        earlier = jnp.tril(jnp.ones((slots, slots), jnp.bool_), -1)
+        first_all = valid & ~jnp.any(same_all & earlier[None], axis=2)
+        merge_all = (same_all & first_all[:, :, None]).astype(jnp.float32)
+        combined = jnp.einsum(
+            "djk,rdkac->rdjac", merge_all, partial, precision=lax.Precision.HIGHEST,
+            preferred_element_type=jnp.float32,
+        )
+        grid_rows = combined.astype(jnp.bfloat16).reshape(rows, n, channels)
         wave_args = (grid_rows, lon_inv)
     else:
+        lat_inv = jnp.stack(
+            [jnp.stack([cosine, -sine], axis=1), jnp.stack([sine, cosine], axis=1)], axis=1
+        ).astype(jnp.bfloat16)
+        lat_inv = lat_inv.reshape(slots, 2, 2, MB, devs, rows)
+        same = (my_mode[:, None] == my_mode[None, :]) & my_valid[None, :]
+        earlier = jnp.tril(jnp.ones((slots, slots), jnp.bool_), -1)
+        first = my_valid & ~jnp.any(same & earlier, axis=1)
+        merge = (same & first[:, None]).astype(jnp.float32)
+
+        partial = jnp.einsum(
+            "jabqsr,jqbc->sjarc", lat_inv, filtered, preferred_element_type=jnp.float32
+        )
+        combined = jnp.einsum(
+            "jk,skarc->sjarc", merge, partial, precision=lax.Precision.HIGHEST,
+            preferred_element_type=jnp.float32,
+        )
+        inverse = combined.astype(jnp.bfloat16)
+        rowwise = lax.all_to_all(inverse, ("lat", "lon"), split_axis=0, concat_axis=0, tiled=True)
+        grid_rows = jnp.transpose(rowwise, (3, 0, 1, 2, 4)).reshape(rows, n, channels)
         wave = jnp.einsum("rnc,wn->rwc", grid_rows, lon_inv, preferred_element_type=jnp.float32)
         wave_args = (wave.astype(jnp.bfloat16),)
     return epilogue(field, low, high, conv_kernel, wave_args, 0, rows, None)

time: 241 us -> 274 us (1.14)
  waiting for transfers between devices: 43.7 us -> 77.2 us
  between operations: 0.31 us -> 13.7 us
  other arithmetic: 27 us -> 15.8 us
  starting transfers between devices: 26.4 us -> 20.4 us
    all_gather x0 -> x1, waiting for transfers between devices: none -> 66.4 us  [on_device(): gathered = lax.all_gather(filtered, ('lat', 'lon'), axis=0, tiled=True)]
    all_to_all x1 -> x0, waiting for transfers between devices: 35.8 us -> none  [on_device(): lax.all_to_all(inverse, ('lat', 'lon'), split_axis=0, concat_axis=0, tile...]
    another operation x3 -> x5, other arithmetic: 23.4 us -> 13 us
    all_to_all x2, waiting for transfers between devices: 1.07 us -> 10.8 us  [on_device(): lax.all_to_all(forward, ('lat', 'lon'), split_axis=0, concat_axis=0, tile...]
    all_to_all x1 -> x0, starting transfers between devices: 5.98 us -> none  [on_device(): lax.all_to_all(inverse, ('lat', 'lon'), split_axis=0, concat_axis=0, tile...]
    transpose x1 -> x0, local copies, waits for them, and re-layouts: 4.56 us -> none  [on_device(): jnp.transpose(rowwise, (3, 0, 1, 2, 4)).reshape(rows, n, channels)]
    convert_element_type x0 -> x1, local copies, waits for them, and re-layouts: none -> 3.49 us  [on_device(): grid_rows = combined.astype(jnp.bfloat16).reshape(rows, n, channels)]
    ppermute x1, waiting for transfers between devices: 3.46 us -> 0.01 us  [on_device(): low = lax.ppermute(field[rows - 1:], ('lat', 'lon'), forward_pairs)]
  transfers between devices with their start and end apart: 5 -> 5, of which waited for: 4 -> 2; matrix products, arithmetic and copies ran while one was open for 16% -> 15% of each run, Pallas kernels for 9% -> 8%
where the time goes in v7:
time: 274 us; the launch traced here: 271 us
  Pallas kernels  106 us (39%)
  waiting for transfers between devices  77.2 us (28%)
  local copies, waits for them, and re-layouts  24 us (9%)
  starting transfers between devices  20.4 us (7%)
  other arithmetic  15.8 us (6%)
  matrix products  14 us (5%)
  between operations  13.7 us (5%)
    all_gather x1, waiting for transfers between devices, on_device(): gathered = lax.all_gather(filtered, ('lat', 'lon'), axis=0, tiled=True)  66.4 us
    pallas_call x1, Pallas kernels, epilogue(): pl.pallas_call(kernel, grid=(count // block_rows,), in_specs=specs, out_s...  62.9 us
    pallas_call x2, Pallas kernels, forward_rows(): pl.pallas_call(forward_kernel, grid=(count // block_rows,), in_specs=[pl....  43.2 us
    all_to_all x2, starting transfers between devices, on_device(): lax.all_to_all(forward, ('lat', 'lon'), split_axis=0, concat_axis=0, tile...  14 us
    another operation x3, other arithmetic  12.9 us
    all_to_all x2, waiting for transfers between devices, on_device(): lax.all_to_all(forward, ('lat', 'lon'), split_axis=0, concat_axis=0, tile...  10.8 us
    reshape x2, local copies, waits for them, and re-layouts, on_device(): forward = forward.reshape(part, devs, slots, 2, channels)  6.88 us
    dot_general x1, matrix products, on_device(): jnp.einsum('djk,rdkac->rdjac', merge_all, partial, precision=lax.Precisio...  5.55 us
  transfers between devices with their start and end apart: 5, of which 2 were waited for; matrix products, arithmetic and copies ran while one was open for 15% of the time, Pallas kernels for 8%

profile of v7, /device:TPU:16, one launch (start us, length us, event | category | flops | bytes accessed | tf_op | source)
XLA Modules:
  0.0 271.2 jit_solution(13403353005066012469)
XLA Ops:
  6.5 0.7 broadcast_compare_fusion.1
  7.2 0.7 maximum_shift-right-logical_fusion
  8.6 0.1 rem.113
  8.7 3.1 %multiply_convert_fusion.2 = (bf16[1920,64,1]{0,1,2:T(8,128)(2,1)S(1)}, bf16[1920,64,1]{0,1,2:T(8,128)(2,1)}, f32[1920,64,1]{0,1,2:T(8,128)S(1)}, f32[1920,64,1]{0,1,2:T(8,128)S(1)}) fusion(f32[64]{0:T(128)S(1)} %get-tuple-element.5, s32[64]{0:T(128)S(1)} %get-tuple-element.6, f32[64]{0:T(128)S(1)} %fusion.72), kind=kLoop, calls=%fused_computation.48 | loop fusion | flops 1720320 | bytes 1475328 | tf_op jit(solution)/shard_map/convert
  11.8 0.5 copy.93
  12.3 1.0 reshape.584.lon_ref
  13.3 21.6 %shard_map.74 = bf16[32,128,128]{2,1,0:T(8,128)(2,1)} custom-call(bf16[64,1920,128]{2,1,0:T(8,128)(2,1)} %below_ref.1, bf16[128,1920]{1,0:T(8,128)(2,1)} %reshape.584.lon_ref), custom_call_target="tpu_custom_call" | custom-call | tf_op jit(solution)/shard_map/pallas_call | solution.py:69
  34.9 3.4 %copy.136 = bf16[32,16,4,2,128]{4,0,3,2,1:T(8,128)(2,1)} copy(bf16[32,16,4,2,128]{4,3,2,1,0:T(2,128)(2,1)} %bitcast.108) | data formatting | bytes 2097152 | tf_op jit(solution)/shard_map/reshape | solution.py:186
  38.4 7.1 %all-to-all-start.1 = ((bf16[16,4,2,32,128]{4,3,2,1,0:T(8,128)(2,1)}), bf16[16,4,2,32,128]{4,3,2,1,0:T(8,128)(2,1)S(1)}, u32[]{:S(2)}, u32[]{:S(2)}) async-start(bf16[16,4,2,32,128]{4,3,2,1,0:T(8,128)(2,1)} %bitcast.102), calls=%async_computation.1 | async-start | bytes 2097152 | tf_op jit(solution)/shard_map/all_to_all | solution.py:189
  45.5 0.1 copy.101
  45.6 0.1 copy.102
  45.7 0.1 copy.95
  45.8 21.6 %shard_map.73 = bf16[32,128,128]{2,1,0:T(8,128)(2,1)} custom-call(bf16[64,1920,128]{2,1,0:T(8,128)(2,1)} %below_ref.1, bf16[128,1920]{1,0:T(8,128)(2,1)} %reshape.584.lon_ref), custom_call_target="tpu_custom_call" | custom-call | tf_op jit(solution)/shard_map/pallas_call | solution.py:69
  67.7 3.5 %copy.137 = bf16[32,16,4,2,128]{4,0,3,2,1:T(8,128)(2,1)} copy(bf16[32,16,4,2,128]{4,3,2,1,0:T(2,128)(2,1)} %bitcast.107) | data formatting | bytes 2097152 | tf_op jit(solution)/shard_map/reshape | solution.py:186
  71.1 0.2 multiply_reduce_fusion
  71.4 6.9 %all-to-all-start = ((bf16[16,4,2,32,128]{4,3,2,1,0:T(8,128)(2,1)}), bf16[16,4,2,32,128]{4,3,2,1,0:T(8,128)(2,1)}, u32[]{:S(2)}, u32[]{:S(2)}) async-start(bf16[16,4,2,32,128]{4,3,2,1,0:T(8,128)(2,1)} %bitcast.103), calls=%async_computation | async-start | bytes 2097152 | tf_op jit(solution)/shard_map/all_to_all | solution.py:189
  78.3 0.2 all-gather.2.cloned.1.call-start
  78.7 0.1 copy.89
  78.9 0.2 dynamic-slice_reduce_fusion
  79.1 0.6 slice_bitcast_fusion
  79.7 9.2 %fusion.16 = (bf16[4,1,128,1,16,64]{2,5,3,1,0,4:T(8,128)(2,1)S(1)}, bf16[4,1,128,1,16,64]{2,5,3,1,0,4:T(8,128)(2,1)S(1)}, bf16[4,1,128,1,16,64]{2,5,3,1,0,4:T(8,128)(2,1)S(1)}) fusion(s32[16,64]{1,0:T(8,128)S(1)} %multiply_add_fusion, s32[4,128]{1,0:T(4,128)S(1)} %add_add_fusion.1), kind=kLoop, calls=%fused_computation.25 | loop fusion | flops 10485760 | bytes 3151872 | tf_op jit(solution)/shard_map/convert.15
  89.0 0.4 maximum_maximum_fusion
  89.3 0.9 fusion.77
  90.2 1.4 fusion.9
  91.6 10.8 %all-to-all-done = bf16[16,4,2,32,128]{4,3,2,1,0:T(8,128)(2,1)} async-done(((bf16[16,4,2,32,128]{4,3,2,1,0:T(8,128)(2,1)}), bf16[16,4,2,32,128]{4,3,2,1,0:T(8,128)(2,1)}, u32[]{:S(2)}, u32[]{:S(2)}) %all-to-all-start) | async-done | bytes 1048608 | tf_op jit(solution)/shard_map/all_to_all | solution.py:189
  102.4 1.8 fusion.11
  104.4 0.4 fusion.24
  104.8 0.8 copy.138
  105.6 1.2 fusion.76
  106.8 4.2 %collective-permute-start.1 = (bf16[1,1920,128]{2,1,0:T(8,128)(2,1)S(1)}, bf16[1,1920,128]{2,1,0:T(8,128)(2,1)S(1)}, u32[]{:S(2)}, u32[]{:S(2)}) collective-permute-start(bf16[1,1920,128]{2,1,0:T(8,128)(2,1)S(1)} %get-tuple-element.7), channel_id=1, source_target_pairs={{2,0},{4,2},{6,4},{8,6},{10,8},{12,10},{14,12},{16,14},{18,16},{20... | collective-permute-start | bytes 1474568 | tf_op jit(solution)/shard_map/ppermute | solution.py:240
  111.0 1.9 collective-permute-start
  113.0 0.1 copy.105
  113.3 0.4 and_reduce_fusion
  113.7 0.1 copy.106
  113.9 0.1 copy.107
  114.0 0.6 reshape.583.taps_ref
  114.6 0.5 copy.110
  115.1 0.2 convert_element_type.103
  115.3 1.0 copy.111.refs_1_
  116.4 0.6 negate_convert_fusion.1
  117.1 3.1 %gather_fusion = bf16[64,2,2,128,64]{3,4,2,1,0:T(8,128)(2,1)} fusion(bf16[4,2,2,128,64]{3,4,2,1,0:T(8,128)(2,1)S(1)} %pad_maximum_fusion.1, s32[1024]{0:T(1024)S(1)} %pad_clamp_fusion), kind=kCustom, calls=%fused_computation | custom fusion | bytes 8388864 | tf_op jit(solution)/shard_map/jit(_take)/gather | solution.py:254
  120.2 66.4 %all-gather.2.cloned.1.call-done = bf16[64,128,2,128]{3,1,2,0:T(8,128)(2,1)} async-done(((bf16[4,128,2,128]{3,1,2,0:T(8,128)(2,1)}), bf16[64,128,2,128]{3,1,2,0:T(8,128)(2,1)}) %all-gather.2.cloned.1.call-update) | async-done | bytes 4194320 | tf_op jit(solution)/shard_map/all_gather | solution.py:243
  186.6 4.8 %fusion = f32[64,128,2,64,1]{1,3,4,2,0:T(8,128)S(1)} fusion(bf16[64,128,2,128]{3,1,2,0:T(8,128)(2,1)} %all-gather.2.cloned.1.call-done, bf16[64,2,2,128,64]{3,4,2,1,0:T(8,128)(2,1)} %gather_fusion, pred[64]{0:T(512)(128)(4,1)S(1)} %compare_and_fusion.2), kind=kOutput, calls=%fused_computation.2 | convolution fusion | flops 538968064 | bytes 12582976 | tf_op jit(solution)/shard_map/nabqr,nqbc->rnac/dot_general | solution.py:255
  191.4 5.6 %convert_bitcast_fusion = bf16[64,16,4,2,128]{4,2,3,0,1:T(4,128)(2,1)S(1)} fusion(f32[64,16,4,2,128]{4,0,3,2,1:T(8,128)S(1)} %bitcast.105, s32[16,4]{1,0:T(8,128)S(1)} %copy.103, pred[16,4]{1,0:T(8,128)(4,1)S(1)} %copy.107, pred[16,4]{1,0:T(8,128)(4,1)S(1)} %copy.105), kind=kOutput, calls=%fused_computation.20 | convolution fusion | flops 51380992 | bytes 6291840 | tf_op jit(solution)/shard_map/djk,rdkac->rdjac/dot_general | solution.py:263
  196.9 3.5 %copy.109 = bf16[64,16,4,2,128]{4,3,2,1,0:T(2,128)(2,1)} copy(bf16[64,16,4,2,128]{4,2,3,0,1:T(4,128)(2,1)S(1)} %convert_bitcast_fusion) | data formatting | bytes 4194304 | tf_op jit(solution)/shard_map/convert_element_type | solution.py:267
  200.5 0.8 copy-done.2
  201.2 0.2 copy-done.3
  201.4 62.9 %shard_map.75 = bf16[64,1920,128]{2,1,0:T(8,128)(2,1)} custom-call(f32[9,128]{1,0:T(8,128)} %reshape.583.taps_ref, bf16[1,1920,128]{2,1,0:T(8,128)(2,1)} %copy-done.3, bf16[1,1920,128]{2,1,0:T(8,128)(2,1)} %copy-done.2, bf16[64,1920,128]{2,1,0:T(8,128)(2,1)} %below_ref.1, bf16[64,1920,128]{2,1,0:T(8,128)(2,1)} %below_ref.1, ...), custom_call_target="tpu_custom_call" | custom-call | tf_op jit(solution)/shard_map/pallas_call | solution.py:146
  (62 shorter events, 1.8 us)
Async XLA Ops:
  38.4 33.1 %all-to-all-start.1 = ((bf16[16,4,2,32,128]{4,3,2,1,0:T(8,128)(2,1)}), bf16[16,4,2,32,128]{4,3,2,1,0:T(8,128)(2,1)S(1)}, u32[]{:S(2)}, u32[]{:S(2)}) async-start(bf16[16,4,2,32,128]{4,3,2,1,0:T(8,128)(2,1)} %bitcast.102), calls=%async_computation.1 | async-start | bytes 2097152 | tf_op jit(solution)/shard_map/all_to_all | solution.py:189
  67.7 11.4 %copy-start.4 = (bf16[2,128,128]{2,1,0:T(8,128)(2,1)S(1)}, bf16[2,128,128]{2,1,0:T(8,128)(2,1)}, u32[]{:S(2)}) copy-start(bf16[2,128,128]{2,1,0:T(8,128)(2,1)} %param.10) | copy-start | bytes 196612
  67.7 11.4 %copy-start.5 = (bf16[2,128,128]{2,1,0:T(8,128)(2,1)S(1)}, bf16[2,128,128]{2,1,0:T(8,128)(2,1)}, u32[]{:S(2)}) copy-start(bf16[2,128,128]{2,1,0:T(8,128)(2,1)} %param.8) | copy-start | bytes 196612
  71.4 30.9 %all-to-all-start = ((bf16[16,4,2,32,128]{4,3,2,1,0:T(8,128)(2,1)}), bf16[16,4,2,32,128]{4,3,2,1,0:T(8,128)(2,1)}, u32[]{:S(2)}, u32[]{:S(2)}) async-start(bf16[16,4,2,32,128]{4,3,2,1,0:T(8,128)(2,1)} %bitcast.103), calls=%async_computation | async-start | bytes 2097152 | tf_op jit(solution)/shard_map/all_to_all | solution.py:189
  78.3 108.3 %all-gather.2.cloned.1.call-start = ((), (), s32[]{:S(2)}) async-start(), calls=%async_computation.2 | async-start | bytes 4456448 | tf_op jit(solution)/shard_map/all_gather | solution.py:243
  102.4 1.9 copy-start.1
  102.4 2.0 copy-start.6
  102.4 2.0 copy-start.7
  102.4 2.0 copy-start.9
  102.4 2.0 copy-start.10
  104.4 9.6 %copy-start.8 = (f32[3,3,128]{2,1,0:T(4,128)S(1)}, f32[3,3,128]{2,1,0:T(4,128)}, u32[]{:S(2)}) copy-start(f32[3,3,128]{2,1,0:T(4,128)} %param.12) | copy-start | bytes 13828
  104.4 10.2 %copy-start = (bf16[1920,64,1]{0,1,2:T(8,128)(2,1)S(1)}, bf16[1920,64,1]{0,1,2:T(8,128)(2,1)}, u32[]{:S(2)}) copy-start(bf16[1920,64,1]{0,1,2:T(8,128)(2,1)} %get-tuple-element.30) | copy-start | bytes 737284
  106.8 93.6 %collective-permute-start.1 = (bf16[1,1920,128]{2,1,0:T(8,128)(2,1)S(1)}, bf16[1,1920,128]{2,1,0:T(8,128)(2,1)S(1)}, u32[]{:S(2)}, u32[]{:S(2)}) collective-permute-start(bf16[1,1920,128]{2,1,0:T(8,128)(2,1)S(1)} %get-tuple-element.7), channel_id=1, source_target_pairs={{2,0},{4,2},{6,4},{8,6},{10,8},{12,10},{14,12},{16,14},{18,16},{20... | collective-permute-start | bytes 1474568 | tf_op jit(solution)/shard_map/ppermute | solution.py:240
  111.0 89.4 %collective-permute-start = (bf16[1,1920,128]{2,1,0:T(8,128)(2,1)S(1)}, bf16[1,1920,128]{2,1,0:T(8,128)(2,1)S(1)}, u32[]{:S(2)}, u32[]{:S(2)}) collective-permute-start(bf16[1,1920,128]{2,1,0:T(8,128)(2,1)S(1)} %get-tuple-element.8), channel_id=1, source_target_pairs={{0,2},{2,4},{4,6},{6,8},{8,10},{10,12},{12,14},{14,16},{16,18},{18... | collective-permute-start | bytes 1474568 | tf_op jit(solution)/shard_map/ppermute | solution.py:239
  200.4 0.8 copy-start.2
  200.4 0.9 copy-start.3
Sparse Core Ops, SparseCore 0:
  105.7 80.8 all-gather.1

commit v8 on v6

--- a/solution.py
+++ b/solution.py
@@ -57,13 +57,15 @@
         centred = x - average
         spread = jnp.sum(centred * centred, axis=1, keepdims=True) * (1.0 / channels)
         normed = (centred * lax.rsqrt(spread + 1e-05)).astype(jnp.bfloat16)
-        out_ref[h] = jnp.dot(lon, normed, preferred_element_type=jnp.float32).astype(jnp.bfloat16)
+        out_ref[:, h, :] = jnp.dot(lon, normed, preferred_element_type=jnp.float32).astype(
+            jnp.bfloat16
+        )
 
 
 def forward_rows(field, lon_t, start, count):
     _, width, channels = field.shape
     n = lon_t.shape[0]
-    block_rows = math.gcd(count, 4)
+    block_rows = math.gcd(count, 8)
     offset = start // block_rows
     return pl.pallas_call(
         forward_kernel,
@@ -72,8 +74,8 @@
             pl.BlockSpec((block_rows, width, channels), lambda i: (i + offset, 0, 0)),
             pl.BlockSpec((n, width), lambda i: (0, 0)),
         ],
-        out_specs=pl.BlockSpec((block_rows, n, channels), lambda i: (i, 0, 0)),
-        out_shape=jax.ShapeDtypeStruct((count, n, channels), jnp.bfloat16),
+        out_specs=pl.BlockSpec((n, block_rows, channels), lambda i: (0, i, 0)),
+        out_shape=jax.ShapeDtypeStruct((n, count, channels), jnp.bfloat16),
         compiler_params=pltpu.CompilerParams(dimension_semantics=("arbitrary",)),
     )(field, lon_t)
 
@@ -182,8 +184,7 @@
         lon_t = jnp.transpose(lon_sub, (1, 2, 0)).reshape(n, width)
         for c in range(chunks):
             forward = forward_rows(field, lon_t, c * part, part)
-            forward = forward.reshape(part, devs, slots, 2, channels)
-            forward = jnp.transpose(forward, (1, 2, 3, 0, 4))
+            forward = forward.reshape(devs, slots, 2, part, channels)
             pencils.append(
                 lax.all_to_all(forward, ("lat", "lon"), split_axis=0, concat_axis=0, tiled=True)
             )

time: 241 us -> 237 us (0.983)
  local copies, waits for them, and re-layouts: 22.3 us -> 15.5 us
  Pallas kernels: 106 us -> 109 us
    reshape x2 -> x0, local copies, waits for them, and re-layouts: 6.87 us -> none  [on_device(): forward = forward.reshape(part, devs, slots, 2, channels)]
    pallas_call x2, Pallas kernels: 43.2 us -> 46.4 us  [forward_rows(): pl.pallas_call(forward_kernel, grid=(count // block_rows,), in_specs=[pl....]
  transfers between devices with their start and end apart: 5 -> 5, of which waited for: 4 -> 4; matrix products, arithmetic and copies ran while one was open for 16% -> 15% of each run, Pallas kernels for 9% -> 10%
where the time goes in v8:
time: 237 us
  Pallas kernels  109 us (46%)
  waiting for transfers between devices  43.7 us (18%)
  other arithmetic  27 us (11%)
  starting transfers between devices  26.5 us (11%)
  local copies, waits for them, and re-layouts  15.5 us (7%)
  matrix products  14.4 us (6%)
    pallas_call x1, Pallas kernels, epilogue(): pl.pallas_call(kernel, grid=(count // block_rows,), in_specs=specs, out_s...  62.8 us
    pallas_call x2, Pallas kernels, forward_rows(): pl.pallas_call(forward_kernel, grid=(count // block_rows,), in_specs=[pl....  46.4 us
    all_to_all x1, waiting for transfers between devices, on_device(): lax.all_to_all(inverse, ('lat', 'lon'), split_axis=0, concat_axis=0, tile...  35.7 us
    another operation x3, other arithmetic  23.4 us
    all_to_all x2, starting transfers between devices, on_device(): lax.all_to_all(forward, ('lat', 'lon'), split_axis=0, concat_axis=0, tile...  14 us
    dot_general x1, matrix products, on_device(): jnp.einsum('jk,skarc->sjarc', merge, partial, precision=lax.Precision.HIG...  6.41 us
    all_to_all x1, starting transfers between devices, on_device(): lax.all_to_all(inverse, ('lat', 'lon'), split_axis=0, concat_axis=0, tile...  5.99 us
  transfers between devices with their start and end apart: 5, of which 4 were waited for; matrix products, arithmetic and copies ran while one was open for 15% of the time, Pallas kernels for 10%

profile of v8, /device:TPU:16, one launch (start us, length us, event | category | flops | bytes accessed | tf_op | source)
XLA Modules:
  0.0 236.6 jit_solution(4251429081406430618)
XLA Ops:
  0.0 0.7 broadcast_compare_fusion.1
  0.7 0.7 maximum_shift-right-logical_fusion
  1.6 0.1 add.184
  1.8 0.1 and.174
  1.9 0.1 div.26
  2.0 3.1 %multiply_convert_fusion.3 = (bf16[1920,64,1]{0,1,2:T(8,128)(2,1)S(1)}, bf16[1920,64,1]{0,1,2:T(8,128)(2,1)}, f32[1920,64,1]{0,1,2:T(8,128)S(1)}, f32[1920,64,1]{0,1,2:T(8,128)S(1)}) fusion(f32[64]{0:T(128)S(1)} %get-tuple-element.5, s32[64]{0:T(128)S(1)} %get-tuple-element.6, f32[64]{0:T(128)S(1)} %fusion.79), kind=kLoop, calls=%fused_computation.60 | loop fusion | flops 1720320 | bytes 1475328 | tf_op jit(solution)/shard_map/convert
  5.2 0.5 copy.56
  5.7 1.0 reshape.472.lon_ref
  6.7 23.2 %shard_map.74 = bf16[128,32,128]{2,1,0:T(8,128)(2,1)} custom-call(bf16[64,1920,128]{2,1,0:T(8,128)(2,1)} %below_ref.1, bf16[128,1920]{1,0:T(8,128)(2,1)} %reshape.472.lon_ref), custom_call_target="tpu_custom_call" | custom-call | tf_op jit(solution)/shard_map/pallas_call | solution.py:70
  29.9 7.1 %all-to-all-start.1 = ((bf16[16,4,2,32,128]{4,3,2,1,0:T(8,128)(2,1)}), bf16[16,4,2,32,128]{4,3,2,1,0:T(8,128)(2,1)S(1)}, u32[]{:S(2)}, u32[]{:S(2)}) async-start(bf16[16,4,2,32,128]{4,3,2,1,0:T(8,128)(2,1)} %bitcast.88), calls=%async_computation.1 | async-start | bytes 2097152 | tf_op jit(solution)/shard_map/all_to_all | solution.py:189
  37.0 0.1 copy.61
  37.1 23.3 %shard_map.73 = bf16[128,32,128]{2,1,0:T(8,128)(2,1)} custom-call(bf16[64,1920,128]{2,1,0:T(8,128)(2,1)} %below_ref.1, bf16[128,1920]{1,0:T(8,128)(2,1)} %reshape.472.lon_ref), custom_call_target="tpu_custom_call" | custom-call | tf_op jit(solution)/shard_map/pallas_call | solution.py:70
  60.4 0.1 copy.53
  60.6 0.1 ge.19
  60.7 0.1 copy.60
  60.8 0.1 ne.200
  60.9 0.1 copy.57
  61.2 0.2 dynamic-slice_reduce_fusion.1
  61.4 0.2 dynamic-slice_reduce_fusion
  61.6 0.2 fusion.66
  61.8 0.5 not_and_fusion
  62.4 0.6 slice_bitcast_fusion
  63.0 6.9 %all-to-all-start = ((bf16[16,4,2,32,128]{4,3,2,1,0:T(8,128)(2,1)}), bf16[16,4,2,32,128]{4,3,2,1,0:T(8,128)(2,1)}, u32[]{:S(2)}, u32[]{:S(2)}) async-start(bf16[16,4,2,32,128]{4,3,2,1,0:T(8,128)(2,1)} %bitcast.87), calls=%async_computation | async-start | bytes 2097152 | tf_op jit(solution)/shard_map/all_to_all | solution.py:189
  70.0 9.3 %fusion.25 = (bf16[4,1,128,1,16,64]{2,5,3,1,0,4:T(8,128)(2,1)S(1)}, bf16[4,1,128,1,16,64]{2,5,3,1,0,4:T(8,128)(2,1)S(1)}, bf16[4,1,128,1,16,64]{2,5,3,1,0,4:T(8,128)(2,1)S(1)}) fusion(s32[16,64]{1,0:T(8,128)S(1)} %multiply_add_fusion, s32[4,128]{1,0:T(4,128)S(1)} %add_add_fusion), kind=kLoop, calls=%fused_computation.39 | loop fusion | flops 10485760 | bytes 3151872 | tf_op jit(solution)/shard_map/convert.13
  79.3 0.4 maximum_maximum_fusion
  79.6 0.9 fusion.84
  80.5 11.0 %negate_convert_fusion = (bf16[4,1,1,128,16,64]{3,5,2,4,1,0:T(8,128)(2,1)}, bf16[4,1,1,128,16,64]{3,5,2,4,1,0:T(8,128)(2,1)}, bf16[4,1,1,128,16,64]{3,5,2,4,1,0:T(8,128)(2,1)}) fusion(s32[16,64]{1,0:T(8,128)S(1)} %multiply_add_fusion, s32[4,128]{1,0:T(4,128)S(1)} %copy-done.8), kind=kLoop, calls=%fused_computation.33 | loop fusion | flops 10485760 | bytes 3151872 | tf_op jit(solution)/shard_map/convert.7
  91.5 1.4 fusion.19
  92.9 1.1 all-to-all-done
  94.0 1.8 fusion.21
  95.9 0.8 fusion.34
  96.6 2.4 %fusion.33 = bf16[4,128,256]{2,1,0:T(8,128)(2,1)} fusion(bf16[4,128,256]{1,2,0:T(8,128)(2,1)} %bitcast.89, f32[256]{0:T(256)} %bitcast.96, f32[256]{0:T(256)} %bitcast.97, pred[4]{0:T(512)(128)(4,1)} %copy-done.12, bf16[128,128]{1,0:T(8,128)(2,1)S(1)} %get-tuple-element.33, bf16[128,128]{1,0:T(8,128)(2,1)S(1)} %get-tuple-element.35, ...), kind=kOutput, calls=%fused_computation.51 | convolution fusion | flops 136314880 | bytes 722948 | tf_op jit(solution)/shard_map/tmc,cd->tmd/dot_general | solution.py:31
  99.0 1.7 reshape.476
  100.8 2.4 %fusion.10 = f32[16,4,2,64,128]{4,3,0,2,1:T(8,128)S(1)} fusion(bf16[4,1,1,128,16,64]{3,5,2,4,1,0:T(8,128)(2,1)S(1)} %copy-done.2, bf16[4,1,1,128,16,64]{3,5,2,4,1,0:T(8,128)(2,1)S(1)} %copy-done.1, bf16[4,1,1,128,16,64]{3,5,2,4,1,0:T(8,128)(2,1)S(1)} %copy-done, bf16[4,128,2,128,1,1]{3,2,1,0,5,4:T(2,128)(2,1)} %bitcast.90), kind=kOutput, calls=%fused_computation.21 | convolution fusion | flops 553648128 | bytes 7602176 | tf_op jit(solution)/shard_map/jabqsr,jqbc->sjarc/dot_general | solution.py:251
  103.2 6.4 %convert_bitcast_fusion = bf16[16,4,2,64,128]{4,1,3,2,0:T(4,128)(2,1)} fusion(f32[16,4,2,64,128]{4,3,0,2,1:T(8,128)S(1)} %fusion.10, s32[4]{0:T(128)S(1)} %copy-done.10, pred[4]{0:T(512)(128)(4,1)S(1)} %copy-done.14, pred[4]{0:T(512)(128)(4,1)S(1)} %copy-done.13), kind=kOutput, calls=%fused_computation.32 | convolution fusion | flops 51380272 | bytes 6291480 | tf_op jit(solution)/shard_map/jk,skarc->sjarc/dot_general | solution.py:254
  109.6 6.0 %all-to-all-start.2 = ((bf16[16,4,2,64,128]{4,1,3,2,0:T(4,128)(2,1)}), bf16[16,4,2,64,128]{4,1,3,2,0:T(4,128)(2,1)S(1)}, u32[]{:S(2)}, u32[]{:S(2)}) async-start(bf16[16,4,2,64,128]{4,1,3,2,0:T(4,128)(2,1)} %convert_bitcast_fusion), calls=%async_computation.2 | async-start | bytes 4194304 | tf_op jit(solution)/shard_map/all_to_all | solution.py:259
  115.6 2.2 fusion.83
  117.8 4.3 %collective-permute-start.1 = (bf16[1,1920,128]{2,1,0:T(8,128)(2,1)}, bf16[1,1920,128]{2,1,0:T(8,128)(2,1)}, u32[]{:S(2)}, u32[]{:S(2)}) collective-permute-start(bf16[1,1920,128]{2,1,0:T(8,128)(2,1)} %get-tuple-element.7), channel_id=1, source_target_pairs={{2,0},{4,2},{6,4},{8,6},{10,8},{12,10},{14,12},{16,14},{18,16},{20... | collective-permute-start | bytes 1474568 | tf_op jit(solution)/shard_map/ppermute | solution.py:249
  122.1 2.2 collective-permute-start
  124.3 0.6 reshape.471.taps_ref
  124.9 0.5 copy.64
  125.4 0.2 convert_element_type.107
  125.6 1.0 copy.65.refs_1_
  126.6 35.7 %all-to-all-done.2 = bf16[16,4,2,64,128]{4,1,3,2,0:T(4,128)(2,1)S(1)} async-done(((bf16[16,4,2,64,128]{4,1,3,2,0:T(4,128)(2,1)}), bf16[16,4,2,64,128]{4,1,3,2,0:T(4,128)(2,1)S(1)}, u32[]{:S(2)}, u32[]{:S(2)}) %all-to-all-start.2) | async-done | bytes 2097184 | tf_op jit(solution)/shard_map/all_to_all | solution.py:259
  162.4 4.6 %copy.63 = bf16[64,16,4,2,128]{4,3,2,1,0:T(2,128)(2,1)} copy(bf16[64,16,4,2,128]{4,2,0,3,1:T(4,128)(2,1)S(1)} %bitcast.86) | data formatting | bytes 4194304 | tf_op jit(solution)/shard_map/transpose | solution.py:260
  166.9 3.4 %collective-permute-done.1.high_ref = bf16[1,1920,128]{2,1,0:T(8,128)(2,1)} collective-permute-done((bf16[1,1920,128]{2,1,0:T(8,128)(2,1)}, bf16[1,1920,128]{2,1,0:T(8,128)(2,1)}, u32[]{:S(2)}, u32[]{:S(2)}) %collective-permute-start.1) | collective-permute-done | bytes 491552 | tf_op jit(solution)/shard_map/ppermute | solution.py:249
  170.3 3.5 %collective-permute-done.low_ref = bf16[1,1920,128]{2,1,0:T(8,128)(2,1)} collective-permute-done((bf16[1,1920,128]{2,1,0:T(8,128)(2,1)}, bf16[1,1920,128]{2,1,0:T(8,128)(2,1)}, u32[]{:S(2)}, u32[]{:S(2)}) %collective-permute-start) | collective-permute-done | bytes 491552 | tf_op jit(solution)/shard_map/ppermute | solution.py:248
  173.8 62.8 %shard_map.75 = bf16[64,1920,128]{2,1,0:T(8,128)(2,1)} custom-call(f32[9,128]{1,0:T(8,128)} %reshape.471.taps_ref, bf16[1,1920,128]{2,1,0:T(8,128)(2,1)} %collective-permute-done.low_ref, bf16[1,1920,128]{2,1,0:T(8,128)(2,1)} %collective-permute-done.1.high_ref, bf16[64,1920,128]{2,1,0:T(8,128)(2,1)} %below_ref.1, bf16[64,1920,128]{2,1,0:T(8,128)(2,1)} %below_ref.1, ...), custom_call_target="tpu_custom_call" | custom-call | tf_op jit(solution)/shard_map/pallas_call | solution.py:147
  (51 shorter events, 0.9 us)
Async XLA Ops:
  29.9 33.2 %all-to-all-start.1 = ((bf16[16,4,2,32,128]{4,3,2,1,0:T(8,128)(2,1)}), bf16[16,4,2,32,128]{4,3,2,1,0:T(8,128)(2,1)S(1)}, u32[]{:S(2)}, u32[]{:S(2)}) async-start(bf16[16,4,2,32,128]{4,3,2,1,0:T(8,128)(2,1)} %bitcast.88), calls=%async_computation.1 | async-start | bytes 2097152 | tf_op jit(solution)/shard_map/all_to_all | solution.py:189
  37.1 25.3 %copy-start.5 = (bf16[2,128,128]{2,1,0:T(8,128)(2,1)S(1)}, bf16[2,128,128]{2,1,0:T(8,128)(2,1)}, u32[]{:S(2)}) copy-start(bf16[2,128,128]{2,1,0:T(8,128)(2,1)} %param.10) | copy-start | bytes 196612
  37.1 25.3 %copy-start.6 = (bf16[2,128,128]{2,1,0:T(8,128)(2,1)S(1)}, bf16[2,128,128]{2,1,0:T(8,128)(2,1)}, u32[]{:S(2)}) copy-start(bf16[2,128,128]{2,1,0:T(8,128)(2,1)} %param.8) | copy-start | bytes 196612
  61.3 17.9 %copy-start.12 = (pred[4]{0:T(512)(128)(4,1)}, pred[4]{0:T(512)(128)(4,1)S(1)}, u32[]{:S(2)}) copy-start(pred[4]{0:T(512)(128)(4,1)S(1)} %dynamic-slice_reduce_fusion.1) | copy-start | bytes 16
  61.6 0.7 copy-start.9
  62.4 16.9 %copy-start.7 = (s32[4,128]{1,0:T(4,128)}, s32[4,128]{1,0:T(4,128)S(1)}, u32[]{:S(2)}) copy-start(s32[4,128]{1,0:T(4,128)S(1)} %add_add_fusion) | copy-start | bytes 6148
  63.0 30.9 %all-to-all-start = ((bf16[16,4,2,32,128]{4,3,2,1,0:T(8,128)(2,1)}), bf16[16,4,2,32,128]{4,3,2,1,0:T(8,128)(2,1)}, u32[]{:S(2)}, u32[]{:S(2)}) async-start(bf16[16,4,2,32,128]{4,3,2,1,0:T(8,128)(2,1)} %bitcast.87), calls=%async_computation | async-start | bytes 2097152 | tf_op jit(solution)/shard_map/all_to_all | solution.py:189
  79.6 0.9 copy-start.8
  94.0 1.8 copy-start.4
  95.8 4.9 %copy-start = (bf16[4,1,1,128,16,64]{3,5,2,4,1,0:T(8,128)(2,1)S(1)}, bf16[4,1,1,128,16,64]{3,5,2,4,1,0:T(8,128)(2,1)}, u32[]{:S(2)}) copy-start(bf16[4,1,1,128,16,64]{3,5,2,4,1,0:T(8,128)(2,1)} %get-tuple-element.18) | copy-start | bytes 3145732
  95.9 4.9 %copy-start.1 = (bf16[4,1,1,128,16,64]{3,5,2,4,1,0:T(8,128)(2,1)S(1)}, bf16[4,1,1,128,16,64]{3,5,2,4,1,0:T(8,128)(2,1)}, u32[]{:S(2)}) copy-start(bf16[4,1,1,128,16,64]{3,5,2,4,1,0:T(8,128)(2,1)} %get-tuple-element.19) | copy-start | bytes 3145732
  95.9 4.9 %copy-start.2 = (bf16[4,1,1,128,16,64]{3,5,2,4,1,0:T(8,128)(2,1)S(1)}, bf16[4,1,1,128,16,64]{3,5,2,4,1,0:T(8,128)(2,1)}, u32[]{:S(2)}) copy-start(bf16[4,1,1,128,16,64]{3,5,2,4,1,0:T(8,128)(2,1)} %get-tuple-element.20) | copy-start | bytes 3145732
  100.7 2.4 %copy-start.10 = (s32[4]{0:T(128)S(1)}, s32[4]{0:T(128)}, u32[]{:S(2)}) copy-start(s32[4]{0:T(128)} %copy-done.9) | copy-start | bytes 52
  100.8 2.4 %copy-start.13 = (pred[4]{0:T(512)(128)(4,1)S(1)}, pred[4]{0:T(512)(128)(4,1)}, u32[]{:S(2)}) copy-start(pred[4]{0:T(512)(128)(4,1)} %copy-done.12) | copy-start | bytes 16
  100.8 2.4 %copy-start.14 = (pred[4]{0:T(512)(128)(4,1)S(1)}, pred[4]{0:T(512)(128)(4,1)}, u32[]{:S(2)}) copy-start(pred[4]{0:T(512)(128)(4,1)} %not_and_fusion) | copy-start | bytes 16
  109.6 14.6 %copy-start.11 = (f32[3,3,128]{2,1,0:T(4,128)S(1)}, f32[3,3,128]{2,1,0:T(4,128)}, u32[]{:S(2)}) copy-start(f32[3,3,128]{2,1,0:T(4,128)} %param.12) | copy-start | bytes 13828
  109.6 15.3 %copy-start.3 = (bf16[1920,64,1]{0,1,2:T(8,128)(2,1)S(1)}, bf16[1920,64,1]{0,1,2:T(8,128)(2,1)}, u32[]{:S(2)}) copy-start(bf16[1920,64,1]{0,1,2:T(8,128)(2,1)} %get-tuple-element.28) | copy-start | bytes 737284
  109.6 52.7 %all-to-all-start.2 = ((bf16[16,4,2,64,128]{4,1,3,2,0:T(4,128)(2,1)}), bf16[16,4,2,64,128]{4,1,3,2,0:T(4,128)(2,1)S(1)}, u32[]{:S(2)}, u32[]{:S(2)}) async-start(bf16[16,4,2,64,128]{4,1,3,2,0:T(4,128)(2,1)} %convert_bitcast_fusion), calls=%async_computation.2 | async-start | bytes 4194304 | tf_op jit(solution)/shard_map/all_to_all | solution.py:259
  117.8 52.5 %collective-permute-start.1 = (bf16[1,1920,128]{2,1,0:T(8,128)(2,1)}, bf16[1,1920,128]{2,1,0:T(8,128)(2,1)}, u32[]{:S(2)}, u32[]{:S(2)}) collective-permute-start(bf16[1,1920,128]{2,1,0:T(8,128)(2,1)} %get-tuple-element.7), channel_id=1, source_target_pairs={{2,0},{4,2},{6,4},{8,6},{10,8},{12,10},{14,12},{16,14},{18,16},{20... | collective-permute-start | bytes 1474568 | tf_op jit(solution)/shard_map/ppermute | solution.py:249
  122.1 51.7 %collective-permute-start = (bf16[1,1920,128]{2,1,0:T(8,128)(2,1)}, bf16[1,1920,128]{2,1,0:T(8,128)(2,1)}, u32[]{:S(2)}, u32[]{:S(2)}) collective-permute-start(bf16[1,1920,128]{2,1,0:T(8,128)(2,1)} %get-tuple-element.8), channel_id=1, source_target_pairs={{0,2},{2,4},{4,6},{6,8},{8,10},{10,12},{12,14},{14,16},{16,18},{18... | collective-permute-start | bytes 1474568 | tf_op jit(solution)/shard_map/ppermute | solution.py:248

commit v9 on v8

--- a/solution.py
+++ b/solution.py
@@ -103,7 +103,7 @@
             stencil = pltpu.roll(cols[0], 1, 0) + cols[1] + pltpu.roll(cols[2], width - 1, 0)
             if in_wave:
                 grid_ref, lon_ref = refs[0], refs[1]
-                wave = jnp.dot(lon_ref[...], grid_ref[h], preferred_element_type=jnp.float32)
+                wave = jnp.dot(lon_ref[...], grid_ref[:, h, :], preferred_element_type=jnp.float32)
             else:
                 wave = refs[0][h].astype(jnp.float32)
             out_ref[h] = ((xs[1] + wave) + stencil).astype(jnp.bfloat16)
@@ -128,9 +128,9 @@
     in_wave = len(wave_args) == 2
     if in_wave:
         grid_rows, lon_inv = wave_args
-        n = grid_rows.shape[1]
+        n = grid_rows.shape[0]
         wave_specs = [
-            pl.BlockSpec((block_rows, n, channels), lambda i: (i, 0, 0)),
+            pl.BlockSpec((n, block_rows, channels), lambda i: (0, i, 0)),
             pl.BlockSpec((width, n), lambda i: (0, 0)),
         ]
     else:
@@ -257,10 +257,10 @@
     )
     inverse = combined.astype(jnp.bfloat16)
     rowwise = lax.all_to_all(inverse, ("lat", "lon"), split_axis=0, concat_axis=0, tiled=True)
-    grid_rows = jnp.transpose(rowwise, (3, 0, 1, 2, 4)).reshape(rows, n, channels)
     if n <= 512:
-        wave_args = (grid_rows, lon_inv)
+        wave_args = (rowwise.reshape(n, rows, channels), lon_inv)
     else:
+        grid_rows = jnp.transpose(rowwise, (3, 0, 1, 2, 4)).reshape(rows, n, channels)
         wave = jnp.einsum("rnc,wn->rwc", grid_rows, lon_inv, preferred_element_type=jnp.float32)
         wave_args = (wave.astype(jnp.bfloat16),)
     return epilogue(field, low, high, conv_kernel, wave_args, 0, rows, None)

time: 237 us -> 239 us (level)
  Pallas kernels: 109 us -> 112 us
  local copies, waits for them, and re-layouts: 15.5 us -> 12.8 us
  waiting for transfers between devices: 43.7 us -> 46.3 us
    transpose x1 -> x0, local copies, waits for them, and re-layouts: 4.56 us -> none  [on_device(): jnp.transpose(rowwise, (3, 0, 1, 2, 4)).reshape(rows, n, channels)]
    ppermute x1, waiting for transfers between devices: 3.43 us -> 6.08 us  [on_device(): high = lax.ppermute(field[:1], ('lat', 'lon'), backward_pairs)]
  transfers between devices with their start and end apart: 5 -> 5, of which waited for: 4 -> 4; matrix products, arithmetic and copies ran while one was open for 15% -> 13% of each run, Pallas kernels for 10% -> 10%
where the time goes in v9:
time: 239 us
  Pallas kernels  112 us (47%)
  waiting for transfers between devices  46.3 us (19%)
  other arithmetic  27 us (11%)
  starting transfers between devices  26.5 us (11%)
  matrix products  14.4 us (6%)
  local copies, waits for them, and re-layouts  12.8 us (5%)
    pallas_call x1, Pallas kernels, epilogue(): pl.pallas_call(kernel, grid=(count // block_rows,), in_specs=specs, out_s...  65.1 us
    pallas_call x2, Pallas kernels, forward_rows(): pl.pallas_call(forward_kernel, grid=(count // block_rows,), in_specs=[pl....  46.4 us
    all_to_all x1, waiting for transfers between devices, on_device(): lax.all_to_all(inverse, ('lat', 'lon'), split_axis=0, concat_axis=0, tile...  35.7 us
    another operation x3, other arithmetic  23.4 us
    all_to_all x2, starting transfers between devices, on_device(): lax.all_to_all(forward, ('lat', 'lon'), split_axis=0, concat_axis=0, tile...  14 us
    dot_general x1, matrix products, on_device(): jnp.einsum('jk,skarc->sjarc', merge, partial, precision=lax.Precision.HIG...  6.41 us
    ppermute x1, waiting for transfers between devices, on_device(): high = lax.ppermute(field[:1], ('lat', 'lon'), backward_pairs)  6.08 us
    all_to_all x1, starting transfers between devices, on_device(): lax.all_to_all(inverse, ('lat', 'lon'), split_axis=0, concat_axis=0, tile...  5.99 us
  transfers between devices with their start and end apart: 5, of which 4 were waited for; matrix products, arithmetic and copies ran while one was open for 13% of the time, Pallas kernels for 10%

profile of v9, /device:TPU:16, one launch (start us, length us, event | category | flops | bytes accessed | tf_op | source)
XLA Modules:
  0.0 238.9 jit_solution(16668306133532128269)
XLA Ops:
  0.0 0.7 broadcast_compare_fusion.1
  0.7 0.7 maximum_shift-right-logical_fusion
  1.6 0.1 add.184
  1.8 0.1 and.174
  1.9 0.1 div.26
  2.0 3.1 %multiply_convert_fusion.3 = (bf16[1920,64,1]{0,1,2:T(8,128)(2,1)S(1)}, bf16[1920,64,1]{0,1,2:T(8,128)(2,1)}, f32[1920,64,1]{0,1,2:T(8,128)S(1)}, f32[1920,64,1]{0,1,2:T(8,128)S(1)}) fusion(f32[64]{0:T(128)S(1)} %get-tuple-element.5, s32[64]{0:T(128)S(1)} %get-tuple-element.6, f32[64]{0:T(128)S(1)} %fusion.79), kind=kLoop, calls=%fused_computation.60 | loop fusion | flops 1720320 | bytes 1475328 | tf_op jit(solution)/shard_map/convert
  5.2 0.5 copy.56
  5.7 1.0 reshape.472.lon_ref
  6.7 23.2 %shard_map.74 = bf16[128,32,128]{2,1,0:T(8,128)(2,1)} custom-call(bf16[64,1920,128]{2,1,0:T(8,128)(2,1)} %below_ref.1, bf16[128,1920]{1,0:T(8,128)(2,1)} %reshape.472.lon_ref), custom_call_target="tpu_custom_call" | custom-call | tf_op jit(solution)/shard_map/pallas_call | solution.py:70
  29.9 7.1 %all-to-all-start.1 = ((bf16[16,4,2,32,128]{4,3,2,1,0:T(8,128)(2,1)}), bf16[16,4,2,32,128]{4,3,2,1,0:T(8,128)(2,1)S(1)}, u32[]{:S(2)}, u32[]{:S(2)}) async-start(bf16[16,4,2,32,128]{4,3,2,1,0:T(8,128)(2,1)} %bitcast.86), calls=%async_computation.1 | async-start | bytes 2097152 | tf_op jit(solution)/shard_map/all_to_all | solution.py:189
  37.0 0.1 copy.61
  37.1 23.3 %shard_map.73 = bf16[128,32,128]{2,1,0:T(8,128)(2,1)} custom-call(bf16[64,1920,128]{2,1,0:T(8,128)(2,1)} %below_ref.1, bf16[128,1920]{1,0:T(8,128)(2,1)} %reshape.472.lon_ref), custom_call_target="tpu_custom_call" | custom-call | tf_op jit(solution)/shard_map/pallas_call | solution.py:70
  60.4 0.1 copy.53
  60.6 0.1 ge.19
  60.7 0.1 copy.60
  60.8 0.1 ne.200
  60.9 0.1 copy.57
  61.2 0.2 dynamic-slice_reduce_fusion.1
  61.4 0.2 dynamic-slice_reduce_fusion
  61.6 0.2 fusion.66
  61.8 0.5 not_and_fusion
  62.4 0.6 slice_bitcast_fusion
  63.0 6.9 %all-to-all-start = ((bf16[16,4,2,32,128]{4,3,2,1,0:T(8,128)(2,1)}), bf16[16,4,2,32,128]{4,3,2,1,0:T(8,128)(2,1)}, u32[]{:S(2)}, u32[]{:S(2)}) async-start(bf16[16,4,2,32,128]{4,3,2,1,0:T(8,128)(2,1)} %bitcast.85), calls=%async_computation | async-start | bytes 2097152 | tf_op jit(solution)/shard_map/all_to_all | solution.py:189
  70.0 9.3 %fusion.25 = (bf16[4,1,128,1,16,64]{2,5,3,1,0,4:T(8,128)(2,1)S(1)}, bf16[4,1,128,1,16,64]{2,5,3,1,0,4:T(8,128)(2,1)S(1)}, bf16[4,1,128,1,16,64]{2,5,3,1,0,4:T(8,128)(2,1)S(1)}) fusion(s32[16,64]{1,0:T(8,128)S(1)} %multiply_add_fusion, s32[4,128]{1,0:T(4,128)S(1)} %add_add_fusion), kind=kLoop, calls=%fused_computation.39 | loop fusion | flops 10485760 | bytes 3151872 | tf_op jit(solution)/shard_map/convert.13
  79.3 0.4 maximum_maximum_fusion
  79.6 0.9 fusion.84
  80.5 11.0 %negate_convert_fusion = (bf16[4,1,1,128,16,64]{3,5,2,4,1,0:T(8,128)(2,1)}, bf16[4,1,1,128,16,64]{3,5,2,4,1,0:T(8,128)(2,1)}, bf16[4,1,1,128,16,64]{3,5,2,4,1,0:T(8,128)(2,1)}) fusion(s32[16,64]{1,0:T(8,128)S(1)} %multiply_add_fusion, s32[4,128]{1,0:T(4,128)S(1)} %copy-done.8), kind=kLoop, calls=%fused_computation.33 | loop fusion | flops 10485760 | bytes 3151872 | tf_op jit(solution)/shard_map/convert.7
  91.5 1.4 fusion.19
  92.9 1.1 all-to-all-done
  94.0 1.8 fusion.21
  95.9 0.8 fusion.34
  96.6 2.4 fusion.33
  99.0 1.7 reshape.476
  100.8 2.4 %fusion.10 = f32[16,4,2,64,128]{4,3,0,2,1:T(8,128)S(1)} fusion(bf16[4,1,1,128,16,64]{3,5,2,4,1,0:T(8,128)(2,1)S(1)} %copy-done.2, bf16[4,1,1,128,16,64]{3,5,2,4,1,0:T(8,128)(2,1)S(1)} %copy-done.1, bf16[4,1,1,128,16,64]{3,5,2,4,1,0:T(8,128)(2,1)S(1)} %copy-done, bf16[4,128,2,128,1,1]{3,2,1,0,5,4:T(2,128)(2,1)} %bitcast.88), kind=kOutput, calls=%fused_computation.21 | convolution fusion | flops 553648128 | bytes 7602176 | tf_op jit(solution)/shard_map/jabqsr,jqbc->sjarc/dot_general | solution.py:251
  103.2 6.4 %convert_bitcast_fusion = bf16[16,4,2,64,128]{4,1,3,2,0:T(4,128)(2,1)} fusion(f32[16,4,2,64,128]{4,3,0,2,1:T(8,128)S(1)} %fusion.10, s32[4]{0:T(128)S(1)} %copy-done.10, pred[4]{0:T(512)(128)(4,1)S(1)} %copy-done.14, pred[4]{0:T(512)(128)(4,1)S(1)} %copy-done.13), kind=kOutput, calls=%fused_computation.32 | convolution fusion | flops 51380272 | bytes 6291480 | tf_op jit(solution)/shard_map/jk,skarc->sjarc/dot_general | solution.py:254
  109.6 6.0 %all-to-all-start.2 = ((bf16[16,4,2,64,128]{4,1,3,2,0:T(4,128)(2,1)}), bf16[16,4,2,64,128]{4,1,3,2,0:T(4,128)(2,1)S(1)}, u32[]{:S(2)}, u32[]{:S(2)}) async-start(bf16[16,4,2,64,128]{4,1,3,2,0:T(4,128)(2,1)} %convert_bitcast_fusion), calls=%async_computation.2 | async-start | bytes 4194304 | tf_op jit(solution)/shard_map/all_to_all | solution.py:259
  115.6 2.2 fusion.83
  117.8 4.3 %collective-permute-start.1 = (bf16[1,1920,128]{2,1,0:T(8,128)(2,1)}, bf16[1,1920,128]{2,1,0:T(8,128)(2,1)}, u32[]{:S(2)}, u32[]{:S(2)}) collective-permute-start(bf16[1,1920,128]{2,1,0:T(8,128)(2,1)} %get-tuple-element.7), channel_id=1, source_target_pairs={{2,0},{4,2},{6,4},{8,6},{10,8},{12,10},{14,12},{16,14},{18,16},{20... | collective-permute-start | bytes 1474568 | tf_op jit(solution)/shard_map/ppermute | solution.py:249
  122.1 2.2 collective-permute-start
  124.3 0.6 reshape.471.taps_ref
  124.9 0.5 copy.64
  125.4 0.2 convert_element_type.107
  125.6 1.0 copy.65.refs_1_
  126.6 35.7 %all-to-all-done.2 = bf16[16,4,2,64,128]{4,1,3,2,0:T(4,128)(2,1)S(1)} async-done(((bf16[16,4,2,64,128]{4,1,3,2,0:T(4,128)(2,1)}), bf16[16,4,2,64,128]{4,1,3,2,0:T(4,128)(2,1)S(1)}, u32[]{:S(2)}, u32[]{:S(2)}) %all-to-all-start.2) | async-done | bytes 2097184 | tf_op jit(solution)/shard_map/all_to_all | solution.py:259
  162.4 1.9 copy.63
  164.3 6.1 %collective-permute-done.1.high_ref = bf16[1,1920,128]{2,1,0:T(8,128)(2,1)} collective-permute-done((bf16[1,1920,128]{2,1,0:T(8,128)(2,1)}, bf16[1,1920,128]{2,1,0:T(8,128)(2,1)}, u32[]{:S(2)}, u32[]{:S(2)}) %collective-permute-start.1) | collective-permute-done | bytes 491552 | tf_op jit(solution)/shard_map/ppermute | solution.py:249
  170.3 3.5 %collective-permute-done.low_ref = bf16[1,1920,128]{2,1,0:T(8,128)(2,1)} collective-permute-done((bf16[1,1920,128]{2,1,0:T(8,128)(2,1)}, bf16[1,1920,128]{2,1,0:T(8,128)(2,1)}, u32[]{:S(2)}, u32[]{:S(2)}) %collective-permute-start) | collective-permute-done | bytes 491552 | tf_op jit(solution)/shard_map/ppermute | solution.py:248
  173.8 65.1 %shard_map.75 = bf16[64,1920,128]{2,1,0:T(8,128)(2,1)} custom-call(f32[9,128]{1,0:T(8,128)} %reshape.471.taps_ref, bf16[1,1920,128]{2,1,0:T(8,128)(2,1)} %collective-permute-done.low_ref, bf16[1,1920,128]{2,1,0:T(8,128)(2,1)} %collective-permute-done.1.high_ref, bf16[64,1920,128]{2,1,0:T(8,128)(2,1)} %below_ref.1, bf16[64,1920,128]{2,1,0:T(8,128)(2,1)} %below_ref.1, ...), custom_call_target="tpu_custom_call" | custom-call | tf_op jit(solution)/shard_map/pallas_call | solution.py:147
  (51 shorter events, 0.9 us)
Async XLA Ops:
  29.9 33.2 %all-to-all-start.1 = ((bf16[16,4,2,32,128]{4,3,2,1,0:T(8,128)(2,1)}), bf16[16,4,2,32,128]{4,3,2,1,0:T(8,128)(2,1)S(1)}, u32[]{:S(2)}, u32[]{:S(2)}) async-start(bf16[16,4,2,32,128]{4,3,2,1,0:T(8,128)(2,1)} %bitcast.86), calls=%async_computation.1 | async-start | bytes 2097152 | tf_op jit(solution)/shard_map/all_to_all | solution.py:189
  37.1 25.3 %copy-start.5 = (bf16[2,128,128]{2,1,0:T(8,128)(2,1)S(1)}, bf16[2,128,128]{2,1,0:T(8,128)(2,1)}, u32[]{:S(2)}) copy-start(bf16[2,128,128]{2,1,0:T(8,128)(2,1)} %param.10) | copy-start | bytes 196612
  37.1 25.3 %copy-start.6 = (bf16[2,128,128]{2,1,0:T(8,128)(2,1)S(1)}, bf16[2,128,128]{2,1,0:T(8,128)(2,1)}, u32[]{:S(2)}) copy-start(bf16[2,128,128]{2,1,0:T(8,128)(2,1)} %param.8) | copy-start | bytes 196612
  61.3 17.9 %copy-start.12 = (pred[4]{0:T(512)(128)(4,1)}, pred[4]{0:T(512)(128)(4,1)S(1)}, u32[]{:S(2)}) copy-start(pred[4]{0:T(512)(128)(4,1)S(1)} %dynamic-slice_reduce_fusion.1) | copy-start | bytes 16
  61.6 0.7 copy-start.9
  62.4 16.9 %copy-start.7 = (s32[4,128]{1,0:T(4,128)}, s32[4,128]{1,0:T(4,128)S(1)}, u32[]{:S(2)}) copy-start(s32[4,128]{1,0:T(4,128)S(1)} %add_add_fusion) | copy-start | bytes 6148
  63.0 30.9 %all-to-all-start = ((bf16[16,4,2,32,128]{4,3,2,1,0:T(8,128)(2,1)}), bf16[16,4,2,32,128]{4,3,2,1,0:T(8,128)(2,1)}, u32[]{:S(2)}, u32[]{:S(2)}) async-start(bf16[16,4,2,32,128]{4,3,2,1,0:T(8,128)(2,1)} %bitcast.85), calls=%async_computation | async-start | bytes 2097152 | tf_op jit(solution)/shard_map/all_to_all | solution.py:189
  79.6 0.9 copy-start.8
  94.0 1.8 copy-start.4
  95.8 4.9 %copy-start = (bf16[4,1,1,128,16,64]{3,5,2,4,1,0:T(8,128)(2,1)S(1)}, bf16[4,1,1,128,16,64]{3,5,2,4,1,0:T(8,128)(2,1)}, u32[]{:S(2)}) copy-start(bf16[4,1,1,128,16,64]{3,5,2,4,1,0:T(8,128)(2,1)} %get-tuple-element.18) | copy-start | bytes 3145732
  95.9 4.9 %copy-start.1 = (bf16[4,1,1,128,16,64]{3,5,2,4,1,0:T(8,128)(2,1)S(1)}, bf16[4,1,1,128,16,64]{3,5,2,4,1,0:T(8,128)(2,1)}, u32[]{:S(2)}) copy-start(bf16[4,1,1,128,16,64]{3,5,2,4,1,0:T(8,128)(2,1)} %get-tuple-element.19) | copy-start | bytes 3145732
  95.9 4.9 %copy-start.2 = (bf16[4,1,1,128,16,64]{3,5,2,4,1,0:T(8,128)(2,1)S(1)}, bf16[4,1,1,128,16,64]{3,5,2,4,1,0:T(8,128)(2,1)}, u32[]{:S(2)}) copy-start(bf16[4,1,1,128,16,64]{3,5,2,4,1,0:T(8,128)(2,1)} %get-tuple-element.20) | copy-start | bytes 3145732
  100.7 2.4 %copy-start.10 = (s32[4]{0:T(128)S(1)}, s32[4]{0:T(128)}, u32[]{:S(2)}) copy-start(s32[4]{0:T(128)} %copy-done.9) | copy-start | bytes 52
  100.8 2.4 %copy-start.13 = (pred[4]{0:T(512)(128)(4,1)S(1)}, pred[4]{0:T(512)(128)(4,1)}, u32[]{:S(2)}) copy-start(pred[4]{0:T(512)(128)(4,1)} %copy-done.12) | copy-start | bytes 16
  100.8 2.4 %copy-start.14 = (pred[4]{0:T(512)(128)(4,1)S(1)}, pred[4]{0:T(512)(128)(4,1)}, u32[]{:S(2)}) copy-start(pred[4]{0:T(512)(128)(4,1)} %not_and_fusion) | copy-start | bytes 16
  109.6 14.6 %copy-start.11 = (f32[3,3,128]{2,1,0:T(4,128)S(1)}, f32[3,3,128]{2,1,0:T(4,128)}, u32[]{:S(2)}) copy-start(f32[3,3,128]{2,1,0:T(4,128)} %param.12) | copy-start | bytes 13828
  109.6 15.3 %copy-start.3 = (bf16[1920,64,1]{0,1,2:T(8,128)(2,1)S(1)}, bf16[1920,64,1]{0,1,2:T(8,128)(2,1)}, u32[]{:S(2)}) copy-start(bf16[1920,64,1]{0,1,2:T(8,128)(2,1)} %get-tuple-element.28) | copy-start | bytes 737284
  109.6 52.7 %all-to-all-start.2 = ((bf16[16,4,2,64,128]{4,1,3,2,0:T(4,128)(2,1)}), bf16[16,4,2,64,128]{4,1,3,2,0:T(4,128)(2,1)S(1)}, u32[]{:S(2)}, u32[]{:S(2)}) async-start(bf16[16,4,2,64,128]{4,1,3,2,0:T(4,128)(2,1)} %convert_bitcast_fusion), calls=%async_computation.2 | async-start | bytes 4194304 | tf_op jit(solution)/shard_map/all_to_all | solution.py:259
  117.8 52.5 %collective-permute-start.1 = (bf16[1,1920,128]{2,1,0:T(8,128)(2,1)}, bf16[1,1920,128]{2,1,0:T(8,128)(2,1)}, u32[]{:S(2)}, u32[]{:S(2)}) collective-permute-start(bf16[1,1920,128]{2,1,0:T(8,128)(2,1)} %get-tuple-element.7), channel_id=1, source_target_pairs={{2,0},{4,2},{6,4},{8,6},{10,8},{12,10},{14,12},{16,14},{18,16},{20... | collective-permute-start | bytes 1474568 | tf_op jit(solution)/shard_map/ppermute | solution.py:249
  122.1 51.7 %collective-permute-start = (bf16[1,1920,128]{2,1,0:T(8,128)(2,1)}, bf16[1,1920,128]{2,1,0:T(8,128)(2,1)}, u32[]{:S(2)}, u32[]{:S(2)}) collective-permute-start(bf16[1,1920,128]{2,1,0:T(8,128)(2,1)} %get-tuple-element.8), channel_id=1, source_target_pairs={{0,2},{2,4},{4,6},{6,8},{8,10},{10,12},{12,14},{14,16},{16,18},{18... | collective-permute-start | bytes 1474568 | tf_op jit(solution)/shard_map/ppermute | solution.py:248

commit v10 on v8

--- a/solution.py
+++ b/solution.py
@@ -86,6 +86,7 @@
         block_rows, width, _ = main_ref.shape
         step = pl.program_id(0) + first_block
         taps = [taps_ref[pl.ds(i, 1), :] for i in range(9)]
+        taps[4] = taps[4] + 1.0
         first_row = jnp.where(step == 0, low_ref[0], above_ref[0]).astype(jnp.float32)
         last_row = jnp.where(step == last_block, high_ref[0], below_ref[0])
         last_row = last_row.astype(jnp.float32)
@@ -106,7 +107,7 @@
                 wave = jnp.dot(lon_ref[...], grid_ref[h], preferred_element_type=jnp.float32)
             else:
                 wave = refs[0][h].astype(jnp.float32)
-            out_ref[h] = ((xs[1] + wave) + stencil).astype(jnp.bfloat16)
+            out_ref[h] = (stencil + wave).astype(jnp.bfloat16)
 
     return kernel
 

time: 237 us -> 235 us (level)
  no operation moved by 1% of the time
where the time goes in v10:
time: 235 us
  Pallas kernels  107 us (46%)
  waiting for transfers between devices  43.7 us (19%)
  other arithmetic  27 us (11%)
  starting transfers between devices  26.5 us (11%)
  local copies, waits for them, and re-layouts  15.5 us (7%)
  matrix products  14.4 us (6%)
    pallas_call x1, Pallas kernels, epilogue(): pl.pallas_call(kernel, grid=(count // block_rows,), in_specs=specs, out_s...  60.8 us
    pallas_call x2, Pallas kernels, forward_rows(): pl.pallas_call(forward_kernel, grid=(count // block_rows,), in_specs=[pl....  46.4 us
    all_to_all x1, waiting for transfers between devices, on_device(): lax.all_to_all(inverse, ('lat', 'lon'), split_axis=0, concat_axis=0, tile...  35.7 us
    another operation x3, other arithmetic  23.4 us
    all_to_all x2, starting transfers between devices, on_device(): lax.all_to_all(forward, ('lat', 'lon'), split_axis=0, concat_axis=0, tile...  14 us
    dot_general x1, matrix products, on_device(): jnp.einsum('jk,skarc->sjarc', merge, partial, precision=lax.Precision.HIG...  6.41 us
    all_to_all x1, starting transfers between devices, on_device(): lax.all_to_all(inverse, ('lat', 'lon'), split_axis=0, concat_axis=0, tile...  5.99 us
  transfers between devices with their start and end apart: 5, of which 4 were waited for; matrix products, arithmetic and copies ran while one was open for 15% of the time, Pallas kernels for 10%

profile of v10, /device:TPU:16, one launch (start us, length us, event | category | flops | bytes accessed | tf_op | source)
XLA Modules:
  0.0 234.6 jit_solution(594722674717010658)
XLA Ops:
  0.0 0.7 broadcast_compare_fusion.1
  0.7 0.7 maximum_shift-right-logical_fusion
  1.6 0.1 add.184
  1.8 0.1 and.174
  1.9 0.1 div.26
  2.0 3.1 %multiply_convert_fusion.3 = (bf16[1920,64,1]{0,1,2:T(8,128)(2,1)S(1)}, bf16[1920,64,1]{0,1,2:T(8,128)(2,1)}, f32[1920,64,1]{0,1,2:T(8,128)S(1)}, f32[1920,64,1]{0,1,2:T(8,128)S(1)}) fusion(f32[64]{0:T(128)S(1)} %get-tuple-element.5, s32[64]{0:T(128)S(1)} %get-tuple-element.6, f32[64]{0:T(128)S(1)} %fusion.79), kind=kLoop, calls=%fused_computation.60 | loop fusion | flops 1720320 | bytes 1475328 | tf_op jit(solution)/shard_map/convert
  5.2 0.5 copy.56
  5.7 1.0 reshape.472.lon_ref
  6.7 23.2 %shard_map.74 = bf16[128,32,128]{2,1,0:T(8,128)(2,1)} custom-call(bf16[64,1920,128]{2,1,0:T(8,128)(2,1)} %below_ref.1, bf16[128,1920]{1,0:T(8,128)(2,1)} %reshape.472.lon_ref), custom_call_target="tpu_custom_call" | custom-call | tf_op jit(solution)/shard_map/pallas_call | solution.py:70
  29.9 7.1 %all-to-all-start.1 = ((bf16[16,4,2,32,128]{4,3,2,1,0:T(8,128)(2,1)}), bf16[16,4,2,32,128]{4,3,2,1,0:T(8,128)(2,1)S(1)}, u32[]{:S(2)}, u32[]{:S(2)}) async-start(bf16[16,4,2,32,128]{4,3,2,1,0:T(8,128)(2,1)} %bitcast.88), calls=%async_computation.1 | async-start | bytes 2097152 | tf_op jit(solution)/shard_map/all_to_all | solution.py:190
  37.0 0.1 copy.61
  37.1 23.3 %shard_map.73 = bf16[128,32,128]{2,1,0:T(8,128)(2,1)} custom-call(bf16[64,1920,128]{2,1,0:T(8,128)(2,1)} %below_ref.1, bf16[128,1920]{1,0:T(8,128)(2,1)} %reshape.472.lon_ref), custom_call_target="tpu_custom_call" | custom-call | tf_op jit(solution)/shard_map/pallas_call | solution.py:70
  60.4 0.1 copy.53
  60.6 0.1 ge.19
  60.7 0.1 copy.60
  60.8 0.1 ne.200
  60.9 0.1 copy.57
  61.2 0.2 dynamic-slice_reduce_fusion.1
  61.4 0.2 dynamic-slice_reduce_fusion
  61.6 0.2 fusion.66
  61.8 0.5 not_and_fusion
  62.4 0.6 slice_bitcast_fusion
  63.0 6.9 %all-to-all-start = ((bf16[16,4,2,32,128]{4,3,2,1,0:T(8,128)(2,1)}), bf16[16,4,2,32,128]{4,3,2,1,0:T(8,128)(2,1)}, u32[]{:S(2)}, u32[]{:S(2)}) async-start(bf16[16,4,2,32,128]{4,3,2,1,0:T(8,128)(2,1)} %bitcast.87), calls=%async_computation | async-start | bytes 2097152 | tf_op jit(solution)/shard_map/all_to_all | solution.py:190
  70.0 9.3 %fusion.25 = (bf16[4,1,128,1,16,64]{2,5,3,1,0,4:T(8,128)(2,1)S(1)}, bf16[4,1,128,1,16,64]{2,5,3,1,0,4:T(8,128)(2,1)S(1)}, bf16[4,1,128,1,16,64]{2,5,3,1,0,4:T(8,128)(2,1)S(1)}) fusion(s32[16,64]{1,0:T(8,128)S(1)} %multiply_add_fusion, s32[4,128]{1,0:T(4,128)S(1)} %add_add_fusion), kind=kLoop, calls=%fused_computation.39 | loop fusion | flops 10485760 | bytes 3151872 | tf_op jit(solution)/shard_map/convert.13
  79.3 0.4 maximum_maximum_fusion
  79.6 0.9 fusion.84
  80.5 11.0 %negate_convert_fusion = (bf16[4,1,1,128,16,64]{3,5,2,4,1,0:T(8,128)(2,1)}, bf16[4,1,1,128,16,64]{3,5,2,4,1,0:T(8,128)(2,1)}, bf16[4,1,1,128,16,64]{3,5,2,4,1,0:T(8,128)(2,1)}) fusion(s32[16,64]{1,0:T(8,128)S(1)} %multiply_add_fusion, s32[4,128]{1,0:T(4,128)S(1)} %copy-done.8), kind=kLoop, calls=%fused_computation.33 | loop fusion | flops 10485760 | bytes 3151872 | tf_op jit(solution)/shard_map/convert.7
  91.5 1.4 fusion.19
  92.9 1.1 all-to-all-done
  94.0 1.8 fusion.21
  95.9 0.8 fusion.34
  96.6 2.4 %fusion.33 = bf16[4,128,256]{2,1,0:T(8,128)(2,1)} fusion(bf16[4,128,256]{1,2,0:T(8,128)(2,1)} %bitcast.89, f32[256]{0:T(256)} %bitcast.96, f32[256]{0:T(256)} %bitcast.97, pred[4]{0:T(512)(128)(4,1)} %copy-done.12, bf16[128,128]{1,0:T(8,128)(2,1)S(1)} %get-tuple-element.33, bf16[128,128]{1,0:T(8,128)(2,1)S(1)} %get-tuple-element.35, ...), kind=kOutput, calls=%fused_computation.51 | convolution fusion | flops 136314880 | bytes 722948 | tf_op jit(solution)/shard_map/tmc,cd->tmd/dot_general | solution.py:31
  99.0 1.7 reshape.476
  100.8 2.4 %fusion.10 = f32[16,4,2,64,128]{4,3,0,2,1:T(8,128)S(1)} fusion(bf16[4,1,1,128,16,64]{3,5,2,4,1,0:T(8,128)(2,1)S(1)} %copy-done.2, bf16[4,1,1,128,16,64]{3,5,2,4,1,0:T(8,128)(2,1)S(1)} %copy-done.1, bf16[4,1,1,128,16,64]{3,5,2,4,1,0:T(8,128)(2,1)S(1)} %copy-done, bf16[4,128,2,128,1,1]{3,2,1,0,5,4:T(2,128)(2,1)} %bitcast.90), kind=kOutput, calls=%fused_computation.21 | convolution fusion | flops 553648128 | bytes 7602176 | tf_op jit(solution)/shard_map/jabqsr,jqbc->sjarc/dot_general | solution.py:252
  103.2 6.4 %convert_bitcast_fusion = bf16[16,4,2,64,128]{4,1,3,2,0:T(4,128)(2,1)} fusion(f32[16,4,2,64,128]{4,3,0,2,1:T(8,128)S(1)} %fusion.10, s32[4]{0:T(128)S(1)} %copy-done.10, pred[4]{0:T(512)(128)(4,1)S(1)} %copy-done.14, pred[4]{0:T(512)(128)(4,1)S(1)} %copy-done.13), kind=kOutput, calls=%fused_computation.32 | convolution fusion | flops 51380272 | bytes 6291480 | tf_op jit(solution)/shard_map/jk,skarc->sjarc/dot_general | solution.py:255
  109.6 6.0 %all-to-all-start.2 = ((bf16[16,4,2,64,128]{4,1,3,2,0:T(4,128)(2,1)}), bf16[16,4,2,64,128]{4,1,3,2,0:T(4,128)(2,1)S(1)}, u32[]{:S(2)}, u32[]{:S(2)}) async-start(bf16[16,4,2,64,128]{4,1,3,2,0:T(4,128)(2,1)} %convert_bitcast_fusion), calls=%async_computation.2 | async-start | bytes 4194304 | tf_op jit(solution)/shard_map/all_to_all | solution.py:260
  115.6 2.2 fusion.83
  117.8 4.3 %collective-permute-start.1 = (bf16[1,1920,128]{2,1,0:T(8,128)(2,1)}, bf16[1,1920,128]{2,1,0:T(8,128)(2,1)}, u32[]{:S(2)}, u32[]{:S(2)}) collective-permute-start(bf16[1,1920,128]{2,1,0:T(8,128)(2,1)} %get-tuple-element.7), channel_id=1, source_target_pairs={{2,0},{4,2},{6,4},{8,6},{10,8},{12,10},{14,12},{16,14},{18,16},{20... | collective-permute-start | bytes 1474568 | tf_op jit(solution)/shard_map/ppermute | solution.py:250
  122.1 2.2 collective-permute-start
  124.3 0.6 reshape.471.taps_ref
  124.9 0.5 copy.64
  125.4 0.2 convert_element_type.107
  125.6 1.0 copy.65.refs_1_
  126.6 35.7 %all-to-all-done.2 = bf16[16,4,2,64,128]{4,1,3,2,0:T(4,128)(2,1)S(1)} async-done(((bf16[16,4,2,64,128]{4,1,3,2,0:T(4,128)(2,1)}), bf16[16,4,2,64,128]{4,1,3,2,0:T(4,128)(2,1)S(1)}, u32[]{:S(2)}, u32[]{:S(2)}) %all-to-all-start.2) | async-done | bytes 2097184 | tf_op jit(solution)/shard_map/all_to_all | solution.py:260
  162.4 4.6 %copy.63 = bf16[64,16,4,2,128]{4,3,2,1,0:T(2,128)(2,1)} copy(bf16[64,16,4,2,128]{4,2,0,3,1:T(4,128)(2,1)S(1)} %bitcast.86) | data formatting | bytes 4194304 | tf_op jit(solution)/shard_map/transpose | solution.py:261
  166.9 3.4 %collective-permute-done.1.high_ref = bf16[1,1920,128]{2,1,0:T(8,128)(2,1)} collective-permute-done((bf16[1,1920,128]{2,1,0:T(8,128)(2,1)}, bf16[1,1920,128]{2,1,0:T(8,128)(2,1)}, u32[]{:S(2)}, u32[]{:S(2)}) %collective-permute-start.1) | collective-permute-done | bytes 491552 | tf_op jit(solution)/shard_map/ppermute | solution.py:250
  170.3 3.5 %collective-permute-done.low_ref = bf16[1,1920,128]{2,1,0:T(8,128)(2,1)} collective-permute-done((bf16[1,1920,128]{2,1,0:T(8,128)(2,1)}, bf16[1,1920,128]{2,1,0:T(8,128)(2,1)}, u32[]{:S(2)}, u32[]{:S(2)}) %collective-permute-start) | collective-permute-done | bytes 491552 | tf_op jit(solution)/shard_map/ppermute | solution.py:249
  173.8 60.8 %shard_map.75 = bf16[64,1920,128]{2,1,0:T(8,128)(2,1)} custom-call(f32[9,128]{1,0:T(8,128)} %reshape.471.taps_ref, bf16[1,1920,128]{2,1,0:T(8,128)(2,1)} %collective-permute-done.low_ref, bf16[1,1920,128]{2,1,0:T(8,128)(2,1)} %collective-permute-done.1.high_ref, bf16[64,1920,128]{2,1,0:T(8,128)(2,1)} %below_ref.1, bf16[64,1920,128]{2,1,0:T(8,128)(2,1)} %below_ref.1, ...), custom_call_target="tpu_custom_call" | custom-call | tf_op jit(solution)/shard_map/pallas_call | solution.py:148
  (51 shorter events, 0.9 us)
Async XLA Ops:
  29.9 33.2 %all-to-all-start.1 = ((bf16[16,4,2,32,128]{4,3,2,1,0:T(8,128)(2,1)}), bf16[16,4,2,32,128]{4,3,2,1,0:T(8,128)(2,1)S(1)}, u32[]{:S(2)}, u32[]{:S(2)}) async-start(bf16[16,4,2,32,128]{4,3,2,1,0:T(8,128)(2,1)} %bitcast.88), calls=%async_computation.1 | async-start | bytes 2097152 | tf_op jit(solution)/shard_map/all_to_all | solution.py:190
  37.1 25.3 %copy-start.5 = (bf16[2,128,128]{2,1,0:T(8,128)(2,1)S(1)}, bf16[2,128,128]{2,1,0:T(8,128)(2,1)}, u32[]{:S(2)}) copy-start(bf16[2,128,128]{2,1,0:T(8,128)(2,1)} %param.10) | copy-start | bytes 196612
  37.1 25.3 %copy-start.6 = (bf16[2,128,128]{2,1,0:T(8,128)(2,1)S(1)}, bf16[2,128,128]{2,1,0:T(8,128)(2,1)}, u32[]{:S(2)}) copy-start(bf16[2,128,128]{2,1,0:T(8,128)(2,1)} %param.8) | copy-start | bytes 196612
  61.3 17.9 %copy-start.12 = (pred[4]{0:T(512)(128)(4,1)}, pred[4]{0:T(512)(128)(4,1)S(1)}, u32[]{:S(2)}) copy-start(pred[4]{0:T(512)(128)(4,1)S(1)} %dynamic-slice_reduce_fusion.1) | copy-start | bytes 16
  61.6 0.7 copy-start.9
  62.4 16.9 %copy-start.7 = (s32[4,128]{1,0:T(4,128)}, s32[4,128]{1,0:T(4,128)S(1)}, u32[]{:S(2)}) copy-start(s32[4,128]{1,0:T(4,128)S(1)} %add_add_fusion) | copy-start | bytes 6148
  63.0 30.9 %all-to-all-start = ((bf16[16,4,2,32,128]{4,3,2,1,0:T(8,128)(2,1)}), bf16[16,4,2,32,128]{4,3,2,1,0:T(8,128)(2,1)}, u32[]{:S(2)}, u32[]{:S(2)}) async-start(bf16[16,4,2,32,128]{4,3,2,1,0:T(8,128)(2,1)} %bitcast.87), calls=%async_computation | async-start | bytes 2097152 | tf_op jit(solution)/shard_map/all_to_all | solution.py:190
  79.6 0.9 copy-start.8
  94.0 1.8 copy-start.4
  95.8 4.9 %copy-start = (bf16[4,1,1,128,16,64]{3,5,2,4,1,0:T(8,128)(2,1)S(1)}, bf16[4,1,1,128,16,64]{3,5,2,4,1,0:T(8,128)(2,1)}, u32[]{:S(2)}) copy-start(bf16[4,1,1,128,16,64]{3,5,2,4,1,0:T(8,128)(2,1)} %get-tuple-element.18) | copy-start | bytes 3145732
  95.9 4.9 %copy-start.1 = (bf16[4,1,1,128,16,64]{3,5,2,4,1,0:T(8,128)(2,1)S(1)}, bf16[4,1,1,128,16,64]{3,5,2,4,1,0:T(8,128)(2,1)}, u32[]{:S(2)}) copy-start(bf16[4,1,1,128,16,64]{3,5,2,4,1,0:T(8,128)(2,1)} %get-tuple-element.19) | copy-start | bytes 3145732
  95.9 4.9 %copy-start.2 = (bf16[4,1,1,128,16,64]{3,5,2,4,1,0:T(8,128)(2,1)S(1)}, bf16[4,1,1,128,16,64]{3,5,2,4,1,0:T(8,128)(2,1)}, u32[]{:S(2)}) copy-start(bf16[4,1,1,128,16,64]{3,5,2,4,1,0:T(8,128)(2,1)} %get-tuple-element.20) | copy-start | bytes 3145732
  100.7 2.4 %copy-start.10 = (s32[4]{0:T(128)S(1)}, s32[4]{0:T(128)}, u32[]{:S(2)}) copy-start(s32[4]{0:T(128)} %copy-done.9) | copy-start | bytes 52
  100.8 2.4 %copy-start.13 = (pred[4]{0:T(512)(128)(4,1)S(1)}, pred[4]{0:T(512)(128)(4,1)}, u32[]{:S(2)}) copy-start(pred[4]{0:T(512)(128)(4,1)} %copy-done.12) | copy-start | bytes 16
  100.8 2.4 %copy-start.14 = (pred[4]{0:T(512)(128)(4,1)S(1)}, pred[4]{0:T(512)(128)(4,1)}, u32[]{:S(2)}) copy-start(pred[4]{0:T(512)(128)(4,1)} %not_and_fusion) | copy-start | bytes 16
  109.6 14.6 %copy-start.11 = (f32[3,3,128]{2,1,0:T(4,128)S(1)}, f32[3,3,128]{2,1,0:T(4,128)}, u32[]{:S(2)}) copy-start(f32[3,3,128]{2,1,0:T(4,128)} %param.12) | copy-start | bytes 13828
  109.6 15.3 %copy-start.3 = (bf16[1920,64,1]{0,1,2:T(8,128)(2,1)S(1)}, bf16[1920,64,1]{0,1,2:T(8,128)(2,1)}, u32[]{:S(2)}) copy-start(bf16[1920,64,1]{0,1,2:T(8,128)(2,1)} %get-tuple-element.28) | copy-start | bytes 737284
  109.6 52.7 %all-to-all-start.2 = ((bf16[16,4,2,64,128]{4,1,3,2,0:T(4,128)(2,1)}), bf16[16,4,2,64,128]{4,1,3,2,0:T(4,128)(2,1)S(1)}, u32[]{:S(2)}, u32[]{:S(2)}) async-start(bf16[16,4,2,64,128]{4,1,3,2,0:T(4,128)(2,1)} %convert_bitcast_fusion), calls=%async_computation.2 | async-start | bytes 4194304 | tf_op jit(solution)/shard_map/all_to_all | solution.py:260
  117.8 52.5 %collective-permute-start.1 = (bf16[1,1920,128]{2,1,0:T(8,128)(2,1)}, bf16[1,1920,128]{2,1,0:T(8,128)(2,1)}, u32[]{:S(2)}, u32[]{:S(2)}) collective-permute-start(bf16[1,1920,128]{2,1,0:T(8,128)(2,1)} %get-tuple-element.7), channel_id=1, source_target_pairs={{2,0},{4,2},{6,4},{8,6},{10,8},{12,10},{14,12},{16,14},{18,16},{20... | collective-permute-start | bytes 1474568 | tf_op jit(solution)/shard_map/ppermute | solution.py:250
  122.1 51.7 %collective-permute-start = (bf16[1,1920,128]{2,1,0:T(8,128)(2,1)}, bf16[1,1920,128]{2,1,0:T(8,128)(2,1)}, u32[]{:S(2)}, u32[]{:S(2)}) collective-permute-start(bf16[1,1920,128]{2,1,0:T(8,128)(2,1)} %get-tuple-element.8), channel_id=1, source_target_pairs={{0,2},{2,4},{4,6},{6,8},{8,10},{10,12},{12,14},{14,16},{16,18},{18... | collective-permute-start | bytes 1474568 | tf_op jit(solution)/shard_map/ppermute | solution.py:249
